TPU v7x, 32 devices: a whole 2x2x4 slice. The times are simulated.
32 devices in a mesh: fiber: 2 (over x), chan: 16 (over z, y, core).
Axes of the slice: x: 2, y: 2, z: 4, core: 2. Of those that a mesh axis runs over, the one named last changes fastest.
Arguments:
- recording: bfloat16 [1024, 16384], P('fiber', 'chan'), parts along dimension 0, may hold values from -6 to 6
- source_index: int32 [1024], P('fiber'), parts along dimension 0, may hold values from 0 to 511
- channel_mask: int32 [1024], P(('fiber', 'chan')), parts along dimension 0, may hold values 0 or 1
Outputs:
- correlations: bfloat16 [1024, 512, 256], P('fiber', 'chan'), parts along dimension 0
There are 2 independent parts, one for each index of `fiber`. A program takes and returns all parts, laid end to end along the dimension named above; each array names one. Nothing has to cross between parts.
Inputs may be any that keep to these rules, and one draw needn't show every extreme that they name: `source_index`: indices of virtual-source channels of this fiber; they may repeat and may name bad channels. `channel_mask`: one flag for each channel.
All inputs are finite; a program needn't handle non-finite values. No bound on the sum of `channel_mask` on one device may be relied on, other than what follows from the above.
Results may differ from a plain program's by a relative error of at most 0.0092.
Values may be sent and summed in bfloat16 or wider, within the bound.
No kernel may reach another device: no remote copies, remote signals or barrier semaphores. Data moves between devices by JAX's collectives and lax.ppermute only.
A program may use at most 128 MiB of HBM per device.

v0:
```python
import math

import jax
import jax.numpy as jnp
from jax import lax
from jax.sharding import PartitionSpec as P

SEGS = 8
NSEG = 512
NF = 192
FBASE = 4
LAGS = 256
TAPS = 64
SOURCES = 512


def from_behind(block, axis, distance):
    devices = range(lax.axis_size(axis))
    route = [(i - distance, i) for i in devices if i - distance in devices]
    return lax.ppermute(block, axis, route)


def lowpass_taps():
    offsets = jnp.arange(TAPS, dtype=jnp.float32) - (TAPS - 1) / 2.0
    cutoff = 0.1
    window = 0.5 - 0.5 * jnp.cos(2.0 * math.pi * (jnp.arange(TAPS, dtype=jnp.float32) + 0.5) / TAPS)
    kernel = 2.0 * cutoff * jnp.sinc(2.0 * cutoff * offsets) * window
    kernel = kernel / jnp.sum(kernel)
    return kernel[::-1].astype(jnp.bfloat16)


def decimate(padded, reversed_taps, out_length):
    summed = jnp.zeros((padded.shape[0], out_length), jnp.float32)
    for stride in range(TAPS // 4):
        window_rows = padded[:, 4 * stride : 4 * stride + 4 * out_length].reshape(
            padded.shape[0], out_length, 4
        )
        weights = reversed_taps[4 * stride : 4 * stride + 4]
        summed = summed + jnp.einsum(
            "ctq,q->ct", window_rows, weights, preferred_element_type=jnp.float32
        )
    return summed.astype(jnp.bfloat16)


def fourier_table():
    sample = jnp.arange(NSEG, dtype=jnp.int32)[:, None]
    frequency = FBASE + jnp.arange(NF, dtype=jnp.int32)[None, :]
    angles = 2.0 * math.pi * (sample * frequency % NSEG).astype(jnp.float32) / NSEG
    return jnp.concatenate([jnp.cos(angles), -jnp.sin(angles)], axis=1).astype(jnp.bfloat16)


def delay_table():
    frequency = FBASE + jnp.arange(NF, dtype=jnp.int32)[:, None]
    delays = jnp.arange(LAGS, dtype=jnp.int32)[None, :] - LAGS // 2
    angles = 2.0 * math.pi * (frequency * delays % NSEG).astype(jnp.float32) / NSEG
    return jnp.concatenate([jnp.cos(angles), -jnp.sin(angles)], axis=0).astype(jnp.bfloat16)


def whiten(spectrum):
    real_part = spectrum[:, :NF]
    imag_part = spectrum[:, NF:]
    power = real_part * real_part + imag_part * imag_part
    average = jnp.mean(power, axis=1, keepdims=True)
    factor = lax.rsqrt(power + 0.1 * average + 1e-05)
    return jnp.concatenate([real_part * factor, imag_part * factor], axis=1).astype(jnp.bfloat16)


def correlate(chosen, receivers, delays):
    source_real = chosen[..., :NF]
    source_imag = chosen[..., NF:]
    recv_real = receivers[..., :NF]
    recv_imag = receivers[..., NF:]
    cross_real = jnp.einsum(
        "swf,rwf->srf", source_real, recv_real, preferred_element_type=jnp.float32
    )
    cross_real = cross_real + jnp.einsum(
        "swf,rwf->srf", source_imag, recv_imag, preferred_element_type=jnp.float32
    )
    cross_imag = jnp.einsum(
        "swf,rwf->srf", source_imag, recv_real, preferred_element_type=jnp.float32
    )
    cross_imag = cross_imag - jnp.einsum(
        "swf,rwf->srf", source_real, recv_imag, preferred_element_type=jnp.float32
    )
    cross = jnp.concatenate([cross_real, cross_imag], axis=2).astype(jnp.bfloat16)
    source_count = chosen.shape[0]
    recv_count = receivers.shape[0]
    lagged = jnp.dot(
        cross.reshape(source_count * recv_count, 2 * NF), delays, preferred_element_type=jnp.float32
    )
    lagged = lagged.reshape(source_count, recv_count, LAGS) * (1.0 / math.sqrt(SEGS * NF))
    return lagged.astype(jnp.bfloat16)


def body(recording, source_index, channel_mask):
    channels, raw_count = recording.shape
    devices = lax.axis_size("chan")
    per_device = channels // devices
    dec_length = raw_count // 4
    trailing = recording[:, raw_count - (TAPS - 4) :]
    earlier = from_behind(trailing, "chan", 1)
    padded = jnp.concatenate([earlier, recording], axis=1)
    decimated = decimate(padded, lowpass_taps(), dec_length)
    grouped = decimated.reshape(devices, per_device, dec_length)
    fourier = fourier_table()
    block = lax.all_to_all(grouped, "chan", split_axis=0, concat_axis=2, tiled=True)
    members = block.shape[1]
    segments = block.reshape(members * SEGS, NSEG)
    spectrum = jnp.dot(segments, fourier, preferred_element_type=jnp.float32)
    whitened = whiten(spectrum).reshape(members, SEGS, 2 * NF)
    whitened = whitened * channel_mask.astype(jnp.bfloat16)[:, None, None]
    initial = jnp.zeros((SOURCES, SEGS, 2 * NF), jnp.bfloat16)
    shard_rows = lax.all_gather(whitened, "chan", axis=0, tiled=True)
    row_count = shard_rows.shape[0]
    inside = (source_index >= 0) & (source_index < row_count)
    picked_rows = jnp.take(shard_rows, jnp.clip(source_index, 0, row_count - 1), axis=0)
    chosen = jnp.where(inside[:, None, None], picked_rows, initial)
    delays = delay_table()

    def one_block(chosen_block):
        return correlate(chosen_block, whitened, delays)

    blocks = chosen.reshape(4, SOURCES // 4, SEGS, 2 * NF)
    result = lax.map(one_block, blocks)
    return result.reshape(SOURCES, per_device, LAGS)


def solution(mesh):
    placed = (P("fiber", "chan"), P("fiber"), P(("fiber", "chan")))
    return jax.shard_map(
        body, mesh=mesh, in_specs=placed, out_specs=P("fiber", "chan", None), check_vma=False
    )
```

profile of v0, /device:TPU:0, one launch (start us, length us, event | category | flops | bytes accessed | tf_op | source)
XLA Modules:
  0.0 241.7 jit_solution(927293739654847084)
XLA Ops:
  7.5 2.4 collective-permute-start
  15.2 5.0 %fusion.27 = (bf16[512,1024]{1,0:T(8,128)(2,1)}, bf16[512,1024]{1,0:T(8,128)(2,1)}, bf16[512,1024]{1,0:T(8,128)(2,1)}, bf16[512,1024]{1,0:T(8,128)(2,1)}, bf16[5...) fusion(bf16[512,60]{1,0:T(8,128)(2,1)S(1)} %collective-permute-, ...), kind=kLoop, calls=%fused_computation.46 | loop fusion | flops 18874368 | bytes 10547200 | tf_op jit(solution)/shard_map/concatenate | solution.py:102
  69.2 3.5 %fusion.36 = (bf16[512,1024]{1,0:T(8,128)(2,1)}, bf16[512,1024]{1,0:T(8,128)(2,1)}, bf16[512,1024]{1,0:T(8,128)(2,1)}, bf16[512,1024]{1,0:T(8,128)(2,1)S(1)}, bf...) fusion(bf16[512,60]{1,0:T(8,128)(2,1)S(1)} %collective-permute-done, bf16[512,1024]{1,0:T(8,128)(2,1)S(1)} %copy-done), kind=kLoop, calls=%fused_computation.55 | loop fusion | flops 12582912 | bytes 7401472 | tf_op jit(solution)/shard_map/concatenate | solution.py:102
  77.3 2.8 %fusion.76 = f32[1,512,256]{1,0,2:T(1,128)} fusion(bf16[512,256,4]{0,2,1:T(4,128)(2,1)} %reshape.118, bf16[64]{0:T(256)(128)(2,1)S(1)} %divide_convert_fusion), kind=kOutput, calls=%fused_computation.162 | convolution fusion | flops 1048576 | bytes 1572992 | tf_op jit(solution)/shard_map/ctq,q->ct/dot_general | solution.py:39
  85.5 2.8 %fusion.71 = f32[1,512,256]{1,0,2:T(1,128)} fusion(bf16[512,256,4]{0,2,1:T(4,128)(2,1)} %reshape.113, bf16[64]{0:T(256)(128)(2,1)S(1)} %divide_convert_fusion), kind=kOutput, calls=%fused_computation.157 | convolution fusion | flops 1048576 | bytes 1572992 | tf_op jit(solution)/shard_map/ctq,q->ct/dot_general | solution.py:39
  93.8 2.8 %fusion.72 = f32[1,512,256]{1,0,2:T(1,128)} fusion(bf16[512,256,4]{0,2,1:T(4,128)(2,1)} %reshape.114, bf16[64]{0:T(256)(128)(2,1)S(1)} %divide_convert_fusion), kind=kOutput, calls=%fused_computation.158 | convolution fusion | flops 1048576 | bytes 1572992 | tf_op jit(solution)/shard_map/ctq,q->ct/dot_general | solution.py:39
  109.1 2.9 %fusion.75 = f32[1,512,256]{1,0,2:T(1,128)} fusion(bf16[512,256,4]{0,2,1:T(4,128)(2,1)} %reshape.117, bf16[64]{0:T(256)(128)(2,1)S(1)} %divide_convert_fusion), kind=kOutput, calls=%fused_computation.161 | convolution fusion | flops 1048576 | bytes 1572992 | tf_op jit(solution)/shard_map/ctq,q->ct/dot_general | solution.py:39
  114.0 3.6 %fusion.43 = bf16[512,256]{1,0:T(8,128)(2,1)} fusion(f32[1,512,256]{2,1,0:T(8,128)S(1)} %copy-done.5, f32[1,512,256]{2,1,0:T(8,128)} %copy.100, f32[1,512,256]{2,1,0:T(8,128)} %copy.99, f32[1,512,256]{2,1,0:T(8,128)} %copy.98, f32[1,512,256]{2,1,0:T(8,128)} %copy.97, f32[1,512,256]{2,1,0:T(8,128)} %copy.96, f32[1,512,256]{2,1,0:T(8,128)} %copy.95, ...), kind=kLoop, calls=%fused_computation.67 | loop fusion | flops 2097152 | bytes 8650752 | tf_op jit(solution)/shard_map/convert_element_type | solution.py:42
  117.6 7.2 %all-to-all-start = ((bf16[16,32,256]{2,1,0:T(8,128)(2,1)}), bf16[16,32,256]{2,1,0:T(8,128)(2,1)S(1)}, u32[]{:S(2)}, u32[]{:S(2)}) async-start(bf16[16,32,256]{2,1,0:T(8,128)(2,1)} %bitcast.39), calls=%async_computation | async-start | bytes 524288 | tf_op jit(solution)/shard_map/all_to_all | solution.py:106
  124.9 2.5 %cosine_convert_fusion = (bf16[512,192]{1,0:T(8,128)(2,1)S(1)}, bf16[512,192]{1,0:T(8,128)(2,1)S(1)}) fusion(s32[192]{0:T(256)S(1)} %iota_add_fusion.1), kind=kLoop, calls=%fused_computation.83 | loop fusion | flops 1671168 | bytes 393984 | tf_op jit(solution)/shard_map/convert.10
  127.4 7.5 %all-to-all-done = bf16[16,32,256]{2,1,0:T(8,128)(2,1)S(1)} async-done(((bf16[16,32,256]{2,1,0:T(8,128)(2,1)}), bf16[16,32,256]{2,1,0:T(8,128)(2,1)S(1)}, u32[]{:S(2)}, u32[]{:S(2)}) %all-to-all-start) | async-done | bytes 262176 | tf_op jit(solution)/shard_map/all_to_all | solution.py:106
  139.3 41.3 %all-gather.2.cloned.1.call-done = bf16[512,8,384]{2,1,0:T(8,128)(2,1)} async-done(((bf16[32,8,384]{2,1,0:T(8,128)(2,1)}), bf16[512,8,384]{2,1,0:T(8,128)(2,1)}) %all-gather.2.cloned.1.call-update) | async-done | bytes 3145744 | tf_op jit(solution)/shard_map/all_gather | solution.py:113
  180.6 4.8 %gather_fusion = bf16[512,8,384]{2,1,0:T(8,128)(2,1)} fusion(bf16[512,8,384]{2,1,0:T(8,128)(2,1)} %all-gather.2.cloned.1.call-done, s32[1024]{0:T(1024)S(1)} %pad_clamp_fusion), kind=kCustom, calls=%fused_computation | custom fusion | bytes 6293504 | tf_op jit(solution)/shard_map/jit(_take)/gather | solution.py:116
  185.4 5.3 %copy.83 = bf16[4,128,8,384]{1,2,3,0:T(8,128)(2,1)} copy(bf16[4,128,8,384]{3,2,1,0:T(8,128)(2,1)} %bitcast.237) | data formatting | bytes 6291456 | tf_op jit(solution)/shard_map/jit(_take)/gather | solution.py:116
  190.7 3.9 %select_select_fusion = bf16[4,128,8,384]{1,2,3,0:T(8,128)(2,1)} fusion(bf16[4,128,8,384]{1,2,3,0:T(8,128)(2,1)} %copy.83, pred[4,128]{1,0:T(4,128)(4,1)S(1)} %get-tuple-element.73, pred[4,128]{1,0:T(4,128)(4,1)S(1)} %get-tuple-element.72), kind=kLoop, calls=%fused_computation.44 | loop fusion | flops 3145728 | bytes 6292480 | tf_op jit(solution)/shard_map/jit(_where)/select_n | solution.py:117
  194.6 40.2 %while.10 = (s32[]{:T(128)}, bf16[4,128,32,256]{3,2,1,0:T(8,128)(2,1)}, bf16[4,128,8,384]{1,2,3,0:T(8,128)(2,1)}, bf16[32,8,384]{0,1,2:T(8,128)(2,1)S(1)}, bf16[384,256]{1,0:T(8,128)(2,1)S(1)}, /*index=5*/s32[]{:T(128)}) while((s32[]{:T(128)}, bf16[4,128,32,256]{3,2,1,0:T(8,128)(2,1)}, bf16[4,128,8,384]{1,2,3,0:T(8,128)(2,1)}, ...), condition=%wide.region_3.4_spmd, body=%wide.region_2.3_spmd.sunk | while | flops 862453760 | bytes 49448044 | solution.py:124
  198.9 3.2 %fusion.167 = bf16[1,128,32,256]{3,1,2,0:T(8,128)(2,1)S(1)} fusion(bf16[128,32,384]{0,1,2:T(8,128)(2,1)S(1)} %pad_maximum_fusion.4, bf16[384,256]{1,0:T(8,128)(2,1)S(1)} %get-tuple-element.123), kind=kOutput, calls=%fused_computation.7.clone.1 | convolution fusion | flops 807403520 | bytes 5439488 | tf_op jit(solution)/shard_map/while/body/eval_jaxpr/dot_general | solution.py:88
  202.2 2.5 %copy_dynamic-update-slice_fusion.2 = bf16[4,128,32,256]{3,2,1,0:T(8,128)(2,1)} fusion(bf16[4,128,32,256]{3,2,1,0:T(8,128)(2,1)} %get-tuple-element.114, s32[]{:T(128)} %get-tuple-element.113, bf16[1,128,32,256]{3,1,2,0:T(8,128)(2,1)S(1)} %fusion.167), kind=kLoop, calls=%fused_computation.8.clone.1 | loop fusion | bytes 4194816 | tf_op jit(solution)/shard_map/while/body/jit(dynamic_update_index_in_dim)/dynamic_update_slice | solution.py:124
  209.0 3.2 %fusion.167 = bf16[1,128,32,256]{3,1,2,0:T(8,128)(2,1)S(1)} fusion(bf16[128,32,384]{0,1,2:T(8,128)(2,1)S(1)} %pad_maximum_fusion.4, bf16[384,256]{1,0:T(8,128)(2,1)S(1)} %get-tuple-element.123), kind=kOutput, calls=%fused_computation.7.clone.1 | convolution fusion | flops 807403520 | bytes 5439488 | tf_op jit(solution)/shard_map/while/body/eval_jaxpr/dot_general | solution.py:88
  212.2 2.5 %copy_dynamic-update-slice_fusion.2 = bf16[4,128,32,256]{3,2,1,0:T(8,128)(2,1)} fusion(bf16[4,128,32,256]{3,2,1,0:T(8,128)(2,1)} %get-tuple-element.114, s32[]{:T(128)} %get-tuple-element.113, bf16[1,128,32,256]{3,1,2,0:T(8,128)(2,1)S(1)} %fusion.167), kind=kLoop, calls=%fused_computation.8.clone.1 | loop fusion | bytes 4194816 | tf_op jit(solution)/shard_map/while/body/jit(dynamic_update_index_in_dim)/dynamic_update_slice | solution.py:124
  219.1 3.2 %fusion.167 = bf16[1,128,32,256]{3,1,2,0:T(8,128)(2,1)S(1)} fusion(bf16[128,32,384]{0,1,2:T(8,128)(2,1)S(1)} %pad_maximum_fusion.4, bf16[384,256]{1,0:T(8,128)(2,1)S(1)} %get-tuple-element.123), kind=kOutput, calls=%fused_computation.7.clone.1 | convolution fusion | flops 807403520 | bytes 5439488 | tf_op jit(solution)/shard_map/while/body/eval_jaxpr/dot_general | solution.py:88
  222.3 2.5 %copy_dynamic-update-slice_fusion.2 = bf16[4,128,32,256]{3,2,1,0:T(8,128)(2,1)} fusion(bf16[4,128,32,256]{3,2,1,0:T(8,128)(2,1)} %get-tuple-element.114, s32[]{:T(128)} %get-tuple-element.113, bf16[1,128,32,256]{3,1,2,0:T(8,128)(2,1)S(1)} %fusion.167), kind=kLoop, calls=%fused_computation.8.clone.1 | loop fusion | bytes 4194816 | tf_op jit(solution)/shard_map/while/body/jit(dynamic_update_index_in_dim)/dynamic_update_slice | solution.py:124
  229.1 3.2 %fusion.167 = bf16[1,128,32,256]{3,1,2,0:T(8,128)(2,1)S(1)} fusion(bf16[128,32,384]{0,1,2:T(8,128)(2,1)S(1)} %pad_maximum_fusion.4, bf16[384,256]{1,0:T(8,128)(2,1)S(1)} %get-tuple-element.123), kind=kOutput, calls=%fused_computation.7.clone.1 | convolution fusion | flops 807403520 | bytes 5439488 | tf_op jit(solution)/shard_map/while/body/eval_jaxpr/dot_general | solution.py:88
  232.4 2.5 %copy_dynamic-update-slice_fusion.2 = bf16[4,128,32,256]{3,2,1,0:T(8,128)(2,1)} fusion(bf16[4,128,32,256]{3,2,1,0:T(8,128)(2,1)} %get-tuple-element.114, s32[]{:T(128)} %get-tuple-element.113, bf16[1,128,32,256]{3,1,2,0:T(8,128)(2,1)S(1)} %fusion.167), kind=kLoop, calls=%fused_computation.8.clone.1 | loop fusion | bytes 4194816 | tf_op jit(solution)/shard_map/while/body/jit(dynamic_update_index_in_dim)/dynamic_update_slice | solution.py:124
  (153 shorter events, 106.3 us)
Async XLA Ops:
  7.5 7.6 %collective-permute-start = (bf16[512,60]{1,0:T(8,128)(2,1)S(1)}, bf16[512,60]{1,0:T(8,128)(2,1)S(1)}, u32[]{:S(2)}, u32[]{:S(2)}) collective-permute-start(bf16[512,60]{1,0:T(8,128)(2,1)S(1)} %slice.114), channel_id=1, source_target_pairs={{0,1},{1,2},{2,3},{3,4},{4,5},{5,6},{6,7},{7,8},{8,9},{9,10},{10,1... | collective-permute-start | bytes 184328 | tf_op jit(solution)/shard_map/ppermute | solution.py:20
  12.3 2.9 %copy-start = (bf16[512,1024]{1,0:T(8,128)(2,1)S(1)}, bf16[512,1024]{1,0:T(8,128)(2,1)}, u32[]{:S(2)}) copy-start(bf16[512,1024]{1,0:T(8,128)(2,1)} %param.5) | copy-start | bytes 3145732
  75.0 6.9 %copy-start.3 = (bf16[512,1024]{1,0:T(8,128)(2,1)S(1)}, bf16[512,1024]{1,0:T(8,128)(2,1)}, u32[]{:S(2)}) copy-start(bf16[512,1024]{1,0:T(8,128)(2,1)} %get-tuple-element.62) | copy-start | bytes 3145732
  83.3 6.9 %copy-start.2 = (bf16[512,1024]{1,0:T(8,128)(2,1)S(1)}, bf16[512,1024]{1,0:T(8,128)(2,1)}, u32[]{:S(2)}) copy-start(bf16[512,1024]{1,0:T(8,128)(2,1)} %get-tuple-element.63) | copy-start | bytes 3145732
  91.5 7.0 %copy-start.1 = (bf16[512,1024]{1,0:T(8,128)(2,1)S(1)}, bf16[512,1024]{1,0:T(8,128)(2,1)}, u32[]{:S(2)}) copy-start(bf16[512,1024]{1,0:T(8,128)(2,1)} %get-tuple-element.64) | copy-start | bytes 3145732
  108.0 6.0 %copy-start.5 = (f32[1,512,256]{2,1,0:T(8,128)S(1)}, f32[1,512,256]{2,1,0:T(8,128)}, u32[]{:S(2)}) copy-start(f32[1,512,256]{2,1,0:T(8,128)} %copy.101) | copy-start | bytes 1572868
  108.0 6.0 %copy-start.6 = (f32[1,512,256]{2,1,0:T(8,128)S(1)}, f32[1,512,256]{2,1,0:T(8,128)}, u32[]{:S(2)}) copy-start(f32[1,512,256]{2,1,0:T(8,128)} %copy.86) | copy-start | bytes 1572868
  108.0 6.0 %copy-start.7 = (f32[1,512,256]{2,1,0:T(8,128)S(1)}, f32[1,512,256]{2,1,0:T(8,128)}, u32[]{:S(2)}) copy-start(f32[1,512,256]{2,1,0:T(8,128)} %copy.87) | copy-start | bytes 1572868
  108.0 6.0 %copy-start.8 = (f32[1,512,256]{2,1,0:T(8,128)S(1)}, f32[1,512,256]{2,1,0:T(8,128)}, u32[]{:S(2)}) copy-start(f32[1,512,256]{2,1,0:T(8,128)} %copy.88) | copy-start | bytes 1572868
  109.1 4.9 %copy-start.9 = (f32[1,512,256]{2,1,0:T(8,128)S(1)}, f32[1,512,256]{2,1,0:T(8,128)}, u32[]{:S(2)}) copy-start(f32[1,512,256]{2,1,0:T(8,128)} %copy.89) | copy-start | bytes 1572868
  109.1 4.9 %copy-start.10 = (f32[1,512,256]{2,1,0:T(8,128)S(1)}, f32[1,512,256]{2,1,0:T(8,128)}, u32[]{:S(2)}) copy-start(f32[1,512,256]{2,1,0:T(8,128)} %copy.90) | copy-start | bytes 1572868
  114.0 10.9 %copy-start.12 = (s32[32]{0:T(128)S(1)}, s32[32]{0:T(128)}, u32[]{:S(2)}) copy-start(s32[32]{0:T(128)} %param.7) | copy-start | bytes 388
  117.6 17.2 %all-to-all-start = ((bf16[16,32,256]{2,1,0:T(8,128)(2,1)}), bf16[16,32,256]{2,1,0:T(8,128)(2,1)S(1)}, u32[]{:S(2)}, u32[]{:S(2)}) async-start(bf16[16,32,256]{2,1,0:T(8,128)(2,1)} %bitcast.39), calls=%async_computation | async-start | bytes 524288 | tf_op jit(solution)/shard_map/all_to_all | solution.py:106
  124.9 55.7 %all-gather.2.cloned.1.call-start = ((), (), s32[]{:S(2)}) async-start(), calls=%async_computation.1 | async-start | bytes 3342336 | tf_op jit(solution)/shard_map/all_gather | solution.py:113
  134.9 1.9 copy-start.11
  194.7 2.0 copy-start.4
  204.7 2.0 copy-start.4
  214.8 2.0 copy-start.4
  224.8 2.0 copy-start.4
Sparse Core Ops, SparseCore 0:
  136.9 43.6 all-gather.1
where the time goes:
time: 243 us; the launch traced here: 242 us
  local copies, waits for them, and re-layouts  87.2 us (36%)
  matrix products  58.7 us (24%)
  waiting for transfers between devices  48.8 us (20%)
  other arithmetic  23.2 us (10%)
  between operations  13.8 us (6%)
  starting transfers between devices  9.65 us (4%)
    all_gather x1, waiting for transfers between devices, body(): shard_rows = lax.all_gather(whitened, 'chan', axis=0, tiled=True)  41.3 us
    dot_general x16, matrix products, decimate(): jnp.einsum('ctq,q->ct', window_rows, weights, preferred_element_type=jnp....  30.8 us
    dot_general x16, local copies, waits for them, and re-layouts, decimate(): jnp.einsum('ctq,q->ct', window_rows, weights, preferred_element_type=jnp....  22.7 us
    slice x15, local copies, waits for them, and re-layouts, decimate(): padded[:, 4 * stride:4 * stride + 4 * out_length]  19.8 us
    reshape x16, local copies, waits for them, and re-layouts, decimate(): padded[:, 4 * stride:4 * stride + 4 * out_length]  18.9 us
    dot_general x4, matrix products, correlate(): jnp.dot(cross.reshape(source_count * recv_count, 2 * NF), delays, preferr...  13 us
    gather x2, local copies, waits for them, and re-layouts, body(): jnp.take(shard_rows, jnp.clip(source_index, 0, row_count - 1), axis=0)  10.2 us
    dynamic_update_slice x4, local copies, waits for them, and re-layouts, body(): result = lax.map(one_block, blocks)  10.1 us
  transfers between devices with their start and end apart: 3, of which 2 were waited for; matrix products, arithmetic and copies ran while one was open for 4% of the time, Pallas kernels for 0%

commit v1 on v0

--- a/solution.py
+++ b/solution.py
@@ -29,16 +29,20 @@
     return kernel[::-1].astype(jnp.bfloat16)
 
 
-def decimate(padded, reversed_taps, out_length):
-    summed = jnp.zeros((padded.shape[0], out_length), jnp.float32)
-    for stride in range(TAPS // 4):
-        window_rows = padded[:, 4 * stride : 4 * stride + 4 * out_length].reshape(
-            padded.shape[0], out_length, 4
-        )
-        weights = reversed_taps[4 * stride : 4 * stride + 4]
-        summed = summed + jnp.einsum(
-            "ctq,q->ct", window_rows, weights, preferred_element_type=jnp.float32
-        )
+def band_matrix(reversed_taps, rows, out_length):
+    index = lax.broadcasted_iota(jnp.int32, (rows, out_length), 0) - 4 * lax.broadcasted_iota(
+        jnp.int32, (rows, out_length), 1
+    )
+    inside = (index >= 0) & (index < TAPS)
+    picked = jnp.take(reversed_taps, jnp.clip(index, 0, TAPS - 1), axis=0)
+    return jnp.where(inside, picked, jnp.zeros_like(picked))
+
+
+def decimate(earlier, recording, reversed_taps, out_length):
+    head = earlier.shape[1]
+    band = band_matrix(reversed_taps, head + recording.shape[1], out_length)
+    summed = jnp.dot(earlier, band[:head], preferred_element_type=jnp.float32)
+    summed = summed + jnp.dot(recording, band[head:], preferred_element_type=jnp.float32)
     return summed.astype(jnp.bfloat16)
 
 
@@ -99,8 +103,7 @@
     dec_length = raw_count // 4
     trailing = recording[:, raw_count - (TAPS - 4) :]
     earlier = from_behind(trailing, "chan", 1)
-    padded = jnp.concatenate([earlier, recording], axis=1)
-    decimated = decimate(padded, lowpass_taps(), dec_length)
+    decimated = decimate(earlier, recording, lowpass_taps(), dec_length)
     grouped = decimated.reshape(devices, per_device, dec_length)
     fourier = fourier_table()
     block = lax.all_to_all(grouped, "chan", split_axis=0, concat_axis=2, tiled=True)
@@ -109,19 +112,10 @@
     spectrum = jnp.dot(segments, fourier, preferred_element_type=jnp.float32)
     whitened = whiten(spectrum).reshape(members, SEGS, 2 * NF)
     whitened = whitened * channel_mask.astype(jnp.bfloat16)[:, None, None]
-    initial = jnp.zeros((SOURCES, SEGS, 2 * NF), jnp.bfloat16)
     shard_rows = lax.all_gather(whitened, "chan", axis=0, tiled=True)
     row_count = shard_rows.shape[0]
-    inside = (source_index >= 0) & (source_index < row_count)
-    picked_rows = jnp.take(shard_rows, jnp.clip(source_index, 0, row_count - 1), axis=0)
-    chosen = jnp.where(inside[:, None, None], picked_rows, initial)
-    delays = delay_table()
-
-    def one_block(chosen_block):
-        return correlate(chosen_block, whitened, delays)
-
-    blocks = chosen.reshape(4, SOURCES // 4, SEGS, 2 * NF)
-    result = lax.map(one_block, blocks)
+    chosen = jnp.take(shard_rows, jnp.clip(source_index, 0, row_count - 1), axis=0)
+    result = correlate(chosen, whitened, delay_table())
     return result.reshape(SOURCES, per_device, LAGS)
 
 

time: 243 us -> 221 us (0.909); the launches traced: 242 us -> 217 us
  local copies, waits for them, and re-layouts: 87.2 us -> 26.2 us
  other arithmetic: 23.2 us -> 66.7 us
  matrix products: 58.7 us -> 53.4 us
    select_n x1, other arithmetic: 3.9 us -> 45.5 us  [band_matrix(): return jnp.where(inside, picked, jnp.zeros_like(picked))]
    dot_general x16 -> x2, matrix products: 30.8 us -> 0.74 us  [the longest x1 0.49 us: decimate(): jnp.dot(recording, band[head:], preferred_element_type=jnp.float32)]
    dot_general x32 -> x0, local copies, waits for them, and re-layouts: 23.2 us -> none  [the longest x16 22.7 us: decimate(): jnp.einsum('ctq,q->ct', window_rows, weights, preferred_element_type=jnp....]
    dot_general x4 -> x1, matrix products: 13 us -> 33.8 us  [correlate(): jnp.dot(cross.reshape(source_count * recv_count, 2 * NF), delays, preferr...]
    reshape x16 -> x0, local copies, waits for them, and re-layouts: 18.9 us -> none  [decimate(): padded[:, 4 * stride:4 * stride + 4 * out_length]]
    slice x15 -> x3, local copies, waits for them, and re-layouts: 19.8 us -> 2.33 us  [the longest x2 1.34 us: correlate(): recv_imag = receivers[..., NF:]]
    convert_element_type x0 -> x2, local copies, waits for them, and re-layouts: none -> 12.4 us  [the longest x1 11.5 us: correlate(): return lagged.astype(jnp.bfloat16)]
    concatenate x4 -> x1, other arithmetic: 1.09 us -> 12.5 us  [correlate(): jnp.concatenate([cross_real, cross_imag], axis=2).astype(jnp.bfloat16)]
  transfers between devices with their start and end apart: 3 -> 3, of which waited for: 2 -> 2; matrix products, arithmetic and copies ran while one was open for 4% -> 26% of each run, Pallas kernels for 0% -> 0%
where the time goes in v1:
time: 221 us; the launch traced here: 217 us
  other arithmetic  66.7 us (30%)
  matrix products  53.4 us (24%)
  waiting for transfers between devices  47.3 us (21%)
  local copies, waits for them, and re-layouts  26.2 us (12%)
  between operations  13.8 us (6%)
  starting transfers between devices  9.81 us (4%)
    select_n x1, other arithmetic, band_matrix(): return jnp.where(inside, picked, jnp.zeros_like(picked))  45.5 us
    all_gather x1, waiting for transfers between devices, body(): shard_rows = lax.all_gather(whitened, 'chan', axis=0, tiled=True)  39.8 us
    dot_general x1, matrix products, correlate(): jnp.dot(cross.reshape(source_count * recv_count, 2 * NF), delays, preferr...  33.8 us
    concatenate x1, other arithmetic, correlate(): jnp.concatenate([cross_real, cross_imag], axis=2).astype(jnp.bfloat16)  12.5 us
    convert_element_type x1, local copies, waits for them, and re-layouts, correlate(): return lagged.astype(jnp.bfloat16)  11.5 us
    all_to_all x1, waiting for transfers between devices, body(): lax.all_to_all(grouped, 'chan', split_axis=0, concat_axis=2, tiled=True)  7.52 us
    dot_general x1, matrix products, correlate(): jnp.einsum('swf,rwf->srf', source_imag, recv_imag, preferred_element_type...  7.29 us
    gather x2, local copies, waits for them, and re-layouts, body(): jnp.take(shard_rows, jnp.clip(source_index, 0, row_count - 1), axis=0)  7.2 us
  transfers between devices with their start and end apart: 3, of which 2 were waited for; matrix products, arithmetic and copies ran while one was open for 26% of the time, Pallas kernels for 0%

profile of v1, /device:TPU:0, one launch (start us, length us, event | category | flops | bytes accessed | tf_op | source)
XLA Modules:
  0.0 217.3 jit_solution(6153494781983788418)
XLA Ops:
  6.5 1.1 slice.28
  7.6 2.4 %collective-permute-start = (bf16[512,60]{1,0:T(8,128)(2,1)S(1)}, bf16[512,60]{1,0:T(8,128)(2,1)S(1)}, u32[]{:S(2)}, u32[]{:S(2)}) collective-permute-start(bf16[512,60]{1,0:T(8,128)(2,1)S(1)} %slice.28), channel_id=1, source_target_pairs={{0,1},{1,2},{2,3},{3,4},{4,5},{5,6},{6,7},{7,8},{8,9},{9,10},{10,1... | collective-permute-start | bytes 184328 | tf_op jit(solution)/shard_map/ppermute | solution.py:20
  11.5 0.7 fusion.239
  13.0 0.7 fusion.238
  14.4 45.5 %fusion.204 = bf16[1084,256]{1,0:T(8,128)(2,1)S(1)} fusion(s32[256]{0:T(256)S(1)} %iota_multiply_fusion, bf16[]{:T(256)} %bitcast.114, bf16[]{:T(256)} %bitcast.115, bf16[]{:T(256)} %bitcast.116, bf16[]{:T(256)} %bitcast.117, bf16[]{:T(256)} %bitcast.118, bf16[]{:T(256)} %bitcast.120, bf16[]{:T(256)} %bitcast.119, bf16[]{:T(256)} %bitcast.1, bf16[]{:T(256)} %bitcast.3, ...), kind=kLoop, calls=%fused_computation.212 | loop fusion | flops 39960576 | bytes 556160 | tf_op jit(solution)/shard_map/jit(_where)/select_n | solution.py:38
  60.7 0.8 copy.30
  61.5 7.2 %all-to-all-start = ((bf16[16,32,256]{2,1,0:T(8,128)(2,1)}), bf16[16,32,256]{2,1,0:T(8,128)(2,1)S(1)}, u32[]{:S(2)}, u32[]{:S(2)}) async-start(bf16[16,32,256]{2,1,0:T(8,128)(2,1)} %bitcast.123), calls=%async_computation | async-start | bytes 524288 | tf_op jit(solution)/shard_map/all_to_all | solution.py:109
  69.0 2.2 %cosine_convert_fusion = (bf16[512,192]{1,0:T(8,128)(2,1)S(1)}, bf16[512,192]{1,0:T(8,128)(2,1)S(1)}) fusion(s32[192]{0:T(256)S(1)} %iota_add_fusion.1), kind=kLoop, calls=%fused_computation.223 | loop fusion | flops 1671168 | bytes 393984 | tf_op jit(solution)/shard_map/convert.10
  71.2 7.5 %all-to-all-done = bf16[16,32,256]{2,1,0:T(8,128)(2,1)S(1)} async-done(((bf16[16,32,256]{2,1,0:T(8,128)(2,1)}), bf16[16,32,256]{2,1,0:T(8,128)(2,1)S(1)}, u32[]{:S(2)}, u32[]{:S(2)}) %all-to-all-start) | async-done | bytes 262176 | tf_op jit(solution)/shard_map/all_to_all | solution.py:109
  79.8 0.8 maximum_multiply_fusion
  80.7 1.6 cosine_convert_fusion.1
  82.3 1.1 fusion.236
  83.4 1.0 copy.33
  84.6 39.8 %all-gather.2.cloned.1.call-done = bf16[512,8,384]{2,1,0:T(8,128)(2,1)} async-done(((bf16[32,8,384]{2,1,0:T(8,128)(2,1)}), bf16[512,8,384]{2,1,0:T(8,128)(2,1)}) %all-gather.2.cloned.1.call-update) | async-done | bytes 3145744 | tf_op jit(solution)/shard_map/all_gather | solution.py:115
  124.4 3.4 %gather_fusion = bf16[512,8,384]{2,1,0:T(8,128)(2,1)S(1)} fusion(bf16[512,8,384]{2,1,0:T(8,128)(2,1)} %all-gather.2.cloned.1.call-done, s32[1024]{0:T(1024)S(1)} %pad_clamp_fusion), kind=kCustom, calls=%fused_computation | custom fusion | bytes 6293504 | tf_op jit(solution)/shard_map/jit(_take)/gather | solution.py:117
  127.8 3.8 %copy.32 = bf16[512,8,384]{0,1,2:T(8,128)(2,1)} copy(bf16[512,8,384]{2,1,0:T(8,128)(2,1)S(1)} %gather_fusion) | data formatting | bytes 6291456 | tf_op jit(solution)/shard_map/jit(_take)/gather | solution.py:117
  131.7 2.2 %broadcast_select_fusion = bf16[512,8,384]{0,1,2:T(8,128)(2,1)S(1)} fusion(bf16[512,8,384]{0,1,2:T(8,128)(2,1)} %copy.32, pred[512]{0:T(512)(128)(4,1)S(1)} %compare_and_fusion), kind=kLoop, calls=%fused_computation.11 | loop fusion | flops 1572864 | bytes 6291968 | tf_op jit(solution)/shard_map/jit(_take)/select_n | solution.py:117
  133.9 5.6 %fusion.10 = f32[192,32,512]{2,1,0:T(8,128)} fusion(bf16[32,8,192]{0,1,2:T(8,128)(2,1)S(1)} %copy-done, bf16[512,8,384]{0,1,2:T(8,128)(2,1)S(1)} %broadcast_select_fusion), kind=kOutput, calls=%fused_computation.16 | convolution fusion | flops 50331648 | bytes 14548992 | tf_op jit(solution)/shard_map/swf,rwf->srf/dot_general | solution.py:77
  139.5 1.8 fusion.6
  141.3 7.3 %fusion.4 = bf16[512,32,192]{0,1,2:T(8,128)(2,1)} fusion(f32[192,32,512]{2,1,0:T(8,128)} %fusion.10, bf16[32,8,192]{0,1,2:T(8,128)(2,1)S(1)} %copy.34, bf16[512,8,384]{0,1,2:T(8,128)(2,1)S(1)} %broadcast_select_fusion), kind=kOutput, calls=%fused_computation.7 | convolution fusion | flops 56623104 | bytes 20840448 | tf_op jit(solution)/shard_map/swf,rwf->srf/dot_general | solution.py:80
  148.6 3.7 %fusion.5 = bf16[512,32,192]{0,1,2:T(8,128)(2,1)} fusion(f32[192,32,512]{2,1,0:T(8,128)S(1)} %fusion.6, bf16[32,8,192]{0,1,2:T(8,128)(2,1)S(1)} %copy.34, bf16[512,8,384]{0,1,2:T(8,128)(2,1)S(1)} %broadcast_select_fusion), kind=kOutput, calls=%fused_computation.8 | convolution fusion | flops 56623104 | bytes 20840448 | tf_op jit(solution)/shard_map/swf,rwf->srf/dot_general | solution.py:86
  152.3 12.5 %pad_maximum_fusion = bf16[512,32,384]{0,1,2:T(8,128)(2,1)} fusion(bf16[512,32,192]{0,1,2:T(8,128)(2,1)} %fusion.5, bf16[512,32,192]{0,1,2:T(8,128)(2,1)} %fusion.4), kind=kLoop, calls=%fused_computation.2 | loop fusion | flops 6291456 | bytes 25165824 | tf_op jit(solution)/shard_map/concatenate | solution.py:89
  164.9 33.8 %multiply_convert_fusion = bf16[512,32,256]{2,0,1:T(8,128)(2,1)} fusion(bf16[512,32,384]{0,1,2:T(8,128)(2,1)} %pad_maximum_fusion, bf16[192,256]{1,0:T(8,128)(2,1)S(1)} %copy-done.2, bf16[192,256]{1,0:T(8,128)(2,1)S(1)} %copy-done.1), kind=kOutput, calls=%fused_computation.1 | convolution fusion | flops 3230007296 | bytes 21168128 | tf_op jit(solution)/shard_map/dot_general | solution.py:92
  198.7 11.5 %copy.38 = bf16[512,32,256]{2,1,0:T(8,128)(2,1)} copy(bf16[512,32,256]{2,0,1:T(8,128)(2,1)} %multiply_convert_fusion) | data formatting | bytes 16777216 | tf_op jit(solution)/shard_map/convert_element_type | solution.py:96
  (37 shorter events, 5.2 us)
Async XLA Ops:
  6.5 53.4 %copy-start.3 = (bf16[512,1024]{1,0:T(8,128)(2,1)S(1)}, bf16[512,1024]{1,0:T(8,128)(2,1)}, u32[]{:S(2)}) copy-start(bf16[512,1024]{1,0:T(8,128)(2,1)} %param.3) | copy-start | bytes 3145732
  7.6 52.8 %collective-permute-start = (bf16[512,60]{1,0:T(8,128)(2,1)S(1)}, bf16[512,60]{1,0:T(8,128)(2,1)S(1)}, u32[]{:S(2)}, u32[]{:S(2)}) collective-permute-start(bf16[512,60]{1,0:T(8,128)(2,1)S(1)} %slice.28), channel_id=1, source_target_pairs={{0,1},{1,2},{2,3},{3,4},{4,5},{5,6},{6,7},{7,8},{8,9},{9,10},{10,1... | collective-permute-start | bytes 184328 | tf_op jit(solution)/shard_map/ppermute | solution.py:20
  60.4 8.6 %copy-start.5 = (s32[32]{0:T(128)S(1)}, s32[32]{0:T(128)}, u32[]{:S(2)}) copy-start(s32[32]{0:T(128)} %param.5) | copy-start | bytes 388
  61.5 17.2 %all-to-all-start = ((bf16[16,32,256]{2,1,0:T(8,128)(2,1)}), bf16[16,32,256]{2,1,0:T(8,128)(2,1)S(1)}, u32[]{:S(2)}, u32[]{:S(2)}) async-start(bf16[16,32,256]{2,1,0:T(8,128)(2,1)} %bitcast.123), calls=%async_computation | async-start | bytes 524288 | tf_op jit(solution)/shard_map/all_to_all | solution.py:109
  68.7 55.7 %all-gather.2.cloned.1.call-start = ((), (), s32[]{:S(2)}) async-start(), calls=%async_computation.1 | async-start | bytes 3342336 | tf_op jit(solution)/shard_map/all_gather | solution.py:115
  79.4 1.3 copy-start.4
  131.7 2.3 %copy-start = (bf16[32,8,192]{0,1,2:T(8,128)(2,1)S(1)}, bf16[32,8,192]{0,1,2:T(8,128)(2,1)}, u32[]{:S(2)}) copy-start(bf16[32,8,192]{0,1,2:T(8,128)(2,1)} %copy.33) | copy-start | bytes 294916
  152.3 12.5 %copy-start.1 = (bf16[192,256]{1,0:T(8,128)(2,1)S(1)}, bf16[192,256]{1,0:T(8,128)(2,1)}, u32[]{:S(2)}) copy-start(bf16[192,256]{1,0:T(8,128)(2,1)} %get-tuple-element.9) | copy-start | bytes 294916
  152.3 12.5 %copy-start.2 = (bf16[192,256]{1,0:T(8,128)(2,1)S(1)}, bf16[192,256]{1,0:T(8,128)(2,1)}, u32[]{:S(2)}) copy-start(bf16[192,256]{1,0:T(8,128)(2,1)} %get-tuple-element.10) | copy-start | bytes 294916
Sparse Core Ops, SparseCore 0:
  80.8 43.6 all-gather.1

commit v2 on v1

--- a/solution.py
+++ b/solution.py
@@ -2,7 +2,10 @@
 
 import jax
 import jax.numpy as jnp
+import numpy as np
 from jax import lax
+from jax.experimental import pallas as pl
+from jax.experimental.pallas import tpu as pltpu
 from jax.sharding import PartitionSpec as P
 
 SEGS = 8
@@ -29,18 +32,18 @@
     return kernel[::-1].astype(jnp.bfloat16)
 
 
-def band_matrix(reversed_taps, rows, out_length):
-    index = lax.broadcasted_iota(jnp.int32, (rows, out_length), 0) - 4 * lax.broadcasted_iota(
-        jnp.int32, (rows, out_length), 1
-    )
+def band_matrix(rows, out_length):
+    with jax.ensure_compile_time_eval():
+        reversed_taps = np.asarray(lowpass_taps().astype(jnp.float32))
+    index = np.arange(rows)[:, None] - 4 * np.arange(out_length)[None, :]
     inside = (index >= 0) & (index < TAPS)
-    picked = jnp.take(reversed_taps, jnp.clip(index, 0, TAPS - 1), axis=0)
-    return jnp.where(inside, picked, jnp.zeros_like(picked))
+    band = np.where(inside, reversed_taps[np.clip(index, 0, TAPS - 1)], 0.0)
+    return jnp.asarray(band.astype(np.float32)).astype(jnp.bfloat16)
 
 
-def decimate(earlier, recording, reversed_taps, out_length):
+def decimate(earlier, recording, out_length):
     head = earlier.shape[1]
-    band = band_matrix(reversed_taps, head + recording.shape[1], out_length)
+    band = band_matrix(head + recording.shape[1], out_length)
     summed = jnp.dot(earlier, band[:head], preferred_element_type=jnp.float32)
     summed = summed + jnp.dot(recording, band[head:], preferred_element_type=jnp.float32)
     return summed.astype(jnp.bfloat16)
@@ -69,31 +72,50 @@
     return jnp.concatenate([real_part * factor, imag_part * factor], axis=1).astype(jnp.bfloat16)
 
 
-def correlate(chosen, receivers, delays):
-    source_real = chosen[..., :NF]
-    source_imag = chosen[..., NF:]
-    recv_real = receivers[..., :NF]
-    recv_imag = receivers[..., NF:]
-    cross_real = jnp.einsum(
-        "swf,rwf->srf", source_real, recv_real, preferred_element_type=jnp.float32
-    )
-    cross_real = cross_real + jnp.einsum(
-        "swf,rwf->srf", source_imag, recv_imag, preferred_element_type=jnp.float32
-    )
-    cross_imag = jnp.einsum(
-        "swf,rwf->srf", source_imag, recv_real, preferred_element_type=jnp.float32
-    )
-    cross_imag = cross_imag - jnp.einsum(
-        "swf,rwf->srf", source_real, recv_imag, preferred_element_type=jnp.float32
-    )
-    cross = jnp.concatenate([cross_real, cross_imag], axis=2).astype(jnp.bfloat16)
+def correlate_kernel(source_ref, plain_ref, swapped_ref, delays_ref, out_ref, cross_ref):
+    block = source_ref.shape[0]
+    receivers = plain_ref.shape[1]
+
+    def one_source(s, carry):
+        source = source_ref[s].astype(jnp.float32)
+        direct = jnp.zeros((receivers, 2 * NF), jnp.float32)
+        crossed = jnp.zeros((receivers, 2 * NF), jnp.float32)
+        for w in range(SEGS):
+            row = source[w : w + 1, :]
+            direct = direct + row * plain_ref[w]
+            crossed = crossed + row * swapped_ref[w]
+        cross = direct - pltpu.roll(crossed, NF, 1)
+        start = pl.multiple_of(s * receivers, receivers)
+        cross_ref[pl.ds(start, receivers), :] = cross.astype(jnp.bfloat16)
+        return carry
+
+    lax.fori_loop(0, block, one_source, 0, unroll=True)
+    lagged = jnp.dot(cross_ref[...], delays_ref[...], preferred_element_type=jnp.float32)
+    lagged = lagged * (1.0 / math.sqrt(SEGS * NF))
+    out_ref[...] = lagged.astype(jnp.bfloat16).reshape(out_ref.shape)
+
+
+def correlate(chosen, receivers, delays, block=32):
     source_count = chosen.shape[0]
     recv_count = receivers.shape[0]
-    lagged = jnp.dot(
-        cross.reshape(source_count * recv_count, 2 * NF), delays, preferred_element_type=jnp.float32
-    )
-    lagged = lagged.reshape(source_count, recv_count, LAGS) * (1.0 / math.sqrt(SEGS * NF))
-    return lagged.astype(jnp.bfloat16)
+    spectra = receivers.astype(jnp.float32).transpose(1, 0, 2)
+    real_part = spectra[..., :NF]
+    imag_part = spectra[..., NF:]
+    plain = jnp.concatenate([real_part, real_part], axis=-1)
+    swapped = jnp.concatenate([imag_part, -imag_part], axis=-1)
+    return pl.pallas_call(
+        correlate_kernel,
+        grid=(source_count // block,),
+        in_specs=[
+            pl.BlockSpec((block, SEGS, 2 * NF), lambda i: (i, 0, 0)),
+            pl.BlockSpec((SEGS, recv_count, 2 * NF), lambda i: (0, 0, 0)),
+            pl.BlockSpec((SEGS, recv_count, 2 * NF), lambda i: (0, 0, 0)),
+            pl.BlockSpec((2 * NF, LAGS), lambda i: (0, 0)),
+        ],
+        out_specs=pl.BlockSpec((block, recv_count, LAGS), lambda i: (i, 0, 0)),
+        out_shape=jax.ShapeDtypeStruct((source_count, recv_count, LAGS), jnp.bfloat16),
+        scratch_shapes=[pltpu.VMEM((block * recv_count, 2 * NF), jnp.bfloat16)],
+    )(chosen, plain, swapped, delays)
 
 
 def body(recording, source_index, channel_mask):
@@ -103,7 +125,7 @@
     dec_length = raw_count // 4
     trailing = recording[:, raw_count - (TAPS - 4) :]
     earlier = from_behind(trailing, "chan", 1)
-    decimated = decimate(earlier, recording, lowpass_taps(), dec_length)
+    decimated = decimate(earlier, recording, dec_length)
     grouped = decimated.reshape(devices, per_device, dec_length)
     fourier = fourier_table()
     block = lax.all_to_all(grouped, "chan", split_axis=0, concat_axis=2, tiled=True)
@@ -114,7 +136,7 @@
     whitened = whitened * channel_mask.astype(jnp.bfloat16)[:, None, None]
     shard_rows = lax.all_gather(whitened, "chan", axis=0, tiled=True)
     row_count = shard_rows.shape[0]
-    chosen = jnp.take(shard_rows, jnp.clip(source_index, 0, row_count - 1), axis=0)
+    chosen = jnp.take(shard_rows, jnp.clip(source_index, 0, row_count - 1), axis=0, mode="clip")
     result = correlate(chosen, whitened, delay_table())
     return result.reshape(SOURCES, per_device, LAGS)
 

time: 221 us -> 131 us (0.59); the launches traced: 217 us -> 131 us
  other arithmetic: 66.7 us -> 6.27 us
  matrix products: 53.4 us -> 3.24 us
  Pallas kernels: 0 us -> 38.1 us
  local copies, waits for them, and re-layouts: 26.2 us -> 9.02 us
    dot_general x5 -> x0, matrix products: 52.2 us -> none  [the longest x1 33.8 us: correlate(): jnp.dot(cross.reshape(source_count * recv_count, 2 * NF), delays, preferr...]
    select_n x3 -> x0, other arithmetic: 47.8 us -> none  [the longest x1 45.5 us: band_matrix(): return jnp.where(inside, picked, jnp.zeros_like(picked))]
    pallas_call x0 -> x1, Pallas kernels: none -> 38.1 us  [correlate(): pl.pallas_call(correlate_kernel, grid=(source_count // block,), in_specs=...]
    convert_element_type x1 -> x0, local copies, waits for them, and re-layouts: 11.5 us -> none  [correlate(): return lagged.astype(jnp.bfloat16)]
    concatenate x1 -> x2, other arithmetic: 12.5 us -> 1.79 us  [the longest x1 1.11 us: correlate(): plain = jnp.concatenate([real_part, real_part], axis=-1)]
    gather x6 -> x1, local copies, waits for them, and re-layouts: 10.1 us -> 3.12 us  [body(): jnp.take(shard_rows, jnp.clip(source_index, 0, row_count - 1), axis=0, mo...]
    all_gather x0 -> x1, local copies, waits for them, and re-layouts: none -> 3.74 us  [body(): shard_rows = lax.all_gather(whitened, 'chan', axis=0, tiled=True)]
    all_to_all x1, starting transfers between devices: 7.2 us -> 9.53 us  [body(): lax.all_to_all(grouped, 'chan', split_axis=0, concat_axis=2, tiled=True)]
  transfers between devices with their start and end apart: 3 -> 3, of which waited for: 2 -> 2; matrix products, arithmetic and copies ran while one was open for 26% -> 5% of each run, Pallas kernels for 0% -> 0%
where the time goes in v2:
time: 131 us
  waiting for transfers between devices  48.7 us (37%)
  Pallas kernels  38.1 us (29%)
  between operations  13.6 us (10%)
  starting transfers between devices  12 us (9%)
  local copies, waits for them, and re-layouts  9.02 us (7%)
  other arithmetic  6.27 us (5%)
  matrix products  3.24 us (2%)
    all_gather x1, waiting for transfers between devices, body(): shard_rows = lax.all_gather(whitened, 'chan', axis=0, tiled=True)  41 us
    pallas_call x1, Pallas kernels, correlate(): pl.pallas_call(correlate_kernel, grid=(source_count // block,), in_specs=...  38.1 us
    all_to_all x1, starting transfers between devices, body(): lax.all_to_all(grouped, 'chan', split_axis=0, concat_axis=2, tiled=True)  9.53 us
    all_to_all x1, waiting for transfers between devices, body(): lax.all_to_all(grouped, 'chan', split_axis=0, concat_axis=2, tiled=True)  7.69 us
    all_gather x1, local copies, waits for them, and re-layouts, body(): shard_rows = lax.all_gather(whitened, 'chan', axis=0, tiled=True)  3.74 us
    gather x1, local copies, waits for them, and re-layouts, body(): jnp.take(shard_rows, jnp.clip(source_index, 0, row_count - 1), axis=0, mo...  3.12 us
    another operation x2, other arithmetic  3.11 us
  transfers between devices with their start and end apart: 3, of which 2 were waited for; matrix products, arithmetic and copies ran while one was open for 5% of the time, Pallas kernels for 0%

profile of v2, /device:TPU:0, one launch (start us, length us, event | category | flops | bytes accessed | tf_op | source)
XLA Modules:
  0.0 130.8 jit_solution(14100049655412099417)
XLA Ops:
  6.5 1.0 slice.21
  7.6 2.4 %collective-permute-start = (bf16[512,60]{1,0:T(8,128)(2,1)S(1)}, bf16[512,60]{1,0:T(8,128)(2,1)S(1)}, u32[]{:S(2)}, u32[]{:S(2)}) collective-permute-start(bf16[512,60]{1,0:T(8,128)(2,1)S(1)} %slice.21), channel_id=1, source_target_pairs={{0,1},{1,2},{2,3},{3,4},{4,5},{5,6},{6,7},{7,8},{8,9},{9,10},{10,1... | collective-permute-start | bytes 184328 | tf_op jit(solution)/shard_map/ppermute | solution.py:23
  10.0 1.9 %fusion.20 = f32[256,512]{1,0:T(8,128)S(1)} fusion(bf16[1024,256]{1,0:T(8,128)(2,1)} %constant.54, bf16[512,1024]{1,0:T(8,128)(2,1)} %param.4), kind=kOutput, calls=%fused_computation.49 | convolution fusion | flops 268435456 | bytes 2097152 | tf_op jit(solution)/shard_map/dot_general | solution.py:48
  11.9 1.0 fusion.1
  12.9 0.8 copy.6
  13.7 9.5 %all-to-all-start = ((bf16[16,32,256]{2,1,0:T(8,128)(2,1)}), bf16[16,32,256]{2,1,0:T(8,128)(2,1)S(1)}, u32[]{:S(2)}, u32[]{:S(2)}) async-start(bf16[16,32,256]{2,1,0:T(8,128)(2,1)} %bitcast.1), calls=%async_computation | async-start | bytes 524288 | tf_op jit(solution)/shard_map/all_to_all | solution.py:131
  23.3 0.0 all-gather.2.cloned.1.call-start
  23.3 2.2 %cosine_convert_fusion = (bf16[512,192]{1,0:T(8,128)(2,1)S(1)}, bf16[512,192]{1,0:T(8,128)(2,1)S(1)}) fusion(s32[192]{0:T(256)S(1)} %iota_add_fusion.1), kind=kLoop, calls=%fused_computation.11 | loop fusion | flops 1671168 | bytes 393984 | tf_op jit(solution)/shard_map/convert.7
  25.6 7.7 %all-to-all-done = bf16[16,32,256]{2,1,0:T(8,128)(2,1)S(1)} async-done(((bf16[16,32,256]{2,1,0:T(8,128)(2,1)}), bf16[16,32,256]{2,1,0:T(8,128)(2,1)S(1)}, u32[]{:S(2)}, u32[]{:S(2)}) %all-to-all-start) | async-done | bytes 262176 | tf_op jit(solution)/shard_map/all_to_all | solution.py:131
  33.3 0.1 copy.7
  33.4 0.1 reshape.33
  33.5 0.4 fusion.8
  33.9 0.2 fusion.18
  34.1 0.2 fusion.15
  34.4 0.8 convert_bitcast_fusion
  35.2 0.0 all-gather.2.cloned.1.call-update
  35.3 0.9 cosine_convert_fusion.1
  36.1 0.7 pad_maximum_fusion.2.delays_ref
  36.8 0.1 fusion.19
  37.0 1.1 pad_maximum_fusion
  38.1 41.0 %all-gather.2.cloned.1.call-done = bf16[512,8,384]{2,0,1:T(8,128)(2,1)} async-done(((bf16[32,8,384]{2,0,1:T(8,128)(2,1)}), bf16[512,8,384]{2,0,1:T(8,128)(2,1)}) %all-gather.2.cloned.1.call-update) | async-done | bytes 3145744 | tf_op jit(solution)/shard_map/all_gather | solution.py:137
  79.0 3.7 %copy.10 = bf16[512,8,384]{2,1,0:T(8,128)(2,1)S(1)} copy(bf16[512,8,384]{2,0,1:T(8,128)(2,1)} %all-gather.2.cloned.1.call-done) | data formatting | bytes 6291456 | tf_op jit(solution)/shard_map/all_gather | solution.py:137
  82.8 3.1 %gather_fusion = bf16[512,8,384]{2,1,0:T(8,128)(2,1)} fusion(bf16[512,8,384]{2,1,0:T(8,128)(2,1)S(1)} %copy.10, s32[1024]{0:T(1024)S(1)} %pad_clamp_fusion), kind=kCustom, calls=%fused_computation | custom fusion | bytes 6293504 | tf_op jit(solution)/shard_map/jit(_take)/gather | solution.py:139
  85.9 38.1 %shard_map.46 = bf16[512,32,256]{2,1,0:T(8,128)(2,1)} custom-call(bf16[512,8,384]{2,1,0:T(8,128)(2,1)} %gather_fusion, f32[8,32,384]{2,1,0:T(8,128)} %get-tuple-element.16.plain_ref, f32[8,32,384]{2,1,0:T(8,128)} %get-tuple-element.17.swapped_ref, bf16[384,256]{1,0:T(8,128)(2,1)} %pad_maximum_fusion.2.delays_ref), custom_call_target="tpu_custom_call" | custom-call | tf_op jit(solution)/shard_map/pallas_call | solution.py:106
  (13 shorter events, 0.1 us)
Async XLA Ops:
  6.5 16.8 %copy-start.1 = (s32[32]{0:T(128)S(1)}, s32[32]{0:T(128)}, u32[]{:S(2)}) copy-start(s32[32]{0:T(128)} %param.6) | copy-start | bytes 388
  7.6 4.3 %collective-permute-start = (bf16[512,60]{1,0:T(8,128)(2,1)S(1)}, bf16[512,60]{1,0:T(8,128)(2,1)S(1)}, u32[]{:S(2)}, u32[]{:S(2)}) collective-permute-start(bf16[512,60]{1,0:T(8,128)(2,1)S(1)} %slice.21), channel_id=1, source_target_pairs={{0,1},{1,2},{2,3},{3,4},{4,5},{5,6},{6,7},{7,8},{8,9},{9,10},{10,1... | collective-permute-start | bytes 184328 | tf_op jit(solution)/shard_map/ppermute | solution.py:23
  13.7 21.5 %copy-start = (s32[512]{0:T(512)S(1)}, s32[512]{0:T(512)}, u32[]{:S(2)}) copy-start(s32[512]{0:T(512)} %param.5) | copy-start | bytes 6148
  13.7 19.6 %all-to-all-start = ((bf16[16,32,256]{2,1,0:T(8,128)(2,1)}), bf16[16,32,256]{2,1,0:T(8,128)(2,1)S(1)}, u32[]{:S(2)}, u32[]{:S(2)}) async-start(bf16[16,32,256]{2,1,0:T(8,128)(2,1)} %bitcast.1), calls=%async_computation | async-start | bytes 524288 | tf_op jit(solution)/shard_map/all_to_all | solution.py:131
  23.3 55.8 %all-gather.2.cloned.1.call-start = ((), (), s32[]{:S(2)}) async-start(), calls=%async_computation.1 | async-start | bytes 3342336 | tf_op jit(solution)/shard_map/all_gather | solution.py:137
Sparse Core Ops, SparseCore 0:
  35.3 43.6 all-gather.1

commit v3 on v2

--- a/solution.py
+++ b/solution.py
@@ -73,15 +73,14 @@
 
 
 def correlate_kernel(source_ref, plain_ref, swapped_ref, delays_ref, out_ref, cross_ref):
-    block = source_ref.shape[0]
+    block = source_ref.shape[1]
     receivers = plain_ref.shape[1]
 
     def one_source(s, carry):
-        source = source_ref[s].astype(jnp.float32)
         direct = jnp.zeros((receivers, 2 * NF), jnp.float32)
         crossed = jnp.zeros((receivers, 2 * NF), jnp.float32)
         for w in range(SEGS):
-            row = source[w : w + 1, :]
+            row = source_ref[w, pl.ds(s, 1), :].astype(jnp.float32)
             direct = direct + row * plain_ref[w]
             crossed = crossed + row * swapped_ref[w]
         cross = direct - pltpu.roll(crossed, NF, 1)
@@ -96,7 +95,7 @@
 
 
 def correlate(chosen, receivers, delays, block=32):
-    source_count = chosen.shape[0]
+    source_count = chosen.shape[1]
     recv_count = receivers.shape[0]
     spectra = receivers.astype(jnp.float32).transpose(1, 0, 2)
     real_part = spectra[..., :NF]
@@ -107,7 +106,7 @@
         correlate_kernel,
         grid=(source_count // block,),
         in_specs=[
-            pl.BlockSpec((block, SEGS, 2 * NF), lambda i: (i, 0, 0)),
+            pl.BlockSpec((SEGS, block, 2 * NF), lambda i: (0, i, 0)),
             pl.BlockSpec((SEGS, recv_count, 2 * NF), lambda i: (0, 0, 0)),
             pl.BlockSpec((SEGS, recv_count, 2 * NF), lambda i: (0, 0, 0)),
             pl.BlockSpec((2 * NF, LAGS), lambda i: (0, 0)),
@@ -134,10 +133,20 @@
     spectrum = jnp.dot(segments, fourier, preferred_element_type=jnp.float32)
     whitened = whiten(spectrum).reshape(members, SEGS, 2 * NF)
     whitened = whitened * channel_mask.astype(jnp.bfloat16)[:, None, None]
-    shard_rows = lax.all_gather(whitened, "chan", axis=0, tiled=True)
-    row_count = shard_rows.shape[0]
-    chosen = jnp.take(shard_rows, jnp.clip(source_index, 0, row_count - 1), axis=0, mode="clip")
-    result = correlate(chosen, whitened, delay_table())
+    half = members // 2
+    delays = delay_table()
+    parts = []
+    for rows in (whitened[:half], whitened[half:]):
+        gathered = lax.all_gather(rows, "chan", axis=0, tiled=True)
+        parts.append(correlate(gathered.transpose(1, 0, 2), whitened, delays))
+    table = jnp.concatenate(parts, axis=0)
+    channel = jnp.clip(source_index, 0, devices * members - 1)
+    owner = channel // members
+    local = channel % members
+    position = jnp.where(
+        local < half, owner * half + local, devices * half + owner * (members - half) + local - half
+    )
+    result = jnp.take(table, position, axis=0, mode="clip")
     return result.reshape(SOURCES, per_device, LAGS)
 
 

time: 131 us -> 173 us (1.32)
  local copies, waits for them, and re-layouts: 9.02 us -> 25.9 us
  waiting for transfers between devices: 48.7 us -> 62.7 us
  other arithmetic: 6.27 us -> 13.7 us
  Pallas kernels: 38.1 us -> 41.2 us
    gather x1, local copies, waits for them, and re-layouts: 3.12 us -> 23 us  [body(): result = jnp.take(table, position, axis=0, mode='clip')]
    all_gather x1 -> x2, waiting for transfers between devices: 41 us -> 54.9 us  [body(): gathered = lax.all_gather(rows, 'chan', axis=0, tiled=True)]
    concatenate x0 -> x1, other arithmetic: none -> 7.41 us  [body(): table = jnp.concatenate(parts, axis=0)]
    all_gather x1 -> x0, local copies, waits for them, and re-layouts: 3.74 us -> none  [body(): shard_rows = lax.all_gather(whitened, 'chan', axis=0, tiled=True)]
    pallas_call x1 -> x2, Pallas kernels: 38.1 us -> 41.2 us  [correlate(): pl.pallas_call(correlate_kernel, grid=(source_count // block,), in_specs=...]
  transfers between devices with their start and end apart: 3 -> 4, of which waited for: 2 -> 3; matrix products, arithmetic and copies ran while one was open for 5% -> 4% of each run, Pallas kernels for 0% -> 12%
where the time goes in v3:
time: 173 us; the launch traced here: 172 us
  waiting for transfers between devices  62.7 us (36%)
  Pallas kernels  41.2 us (24%)
  local copies, waits for them, and re-layouts  25.9 us (15%)
  other arithmetic  13.7 us (8%)
  between operations  13.6 us (8%)
  starting transfers between devices  11.9 us (7%)
  matrix products  3.24 us (2%)
    all_gather x2, waiting for transfers between devices, body(): gathered = lax.all_gather(rows, 'chan', axis=0, tiled=True)  54.9 us
    pallas_call x2, Pallas kernels, correlate(): pl.pallas_call(correlate_kernel, grid=(source_count // block,), in_specs=...  41.2 us
    gather x1, local copies, waits for them, and re-layouts, body(): result = jnp.take(table, position, axis=0, mode='clip')  23 us
    all_to_all x1, starting transfers between devices, body(): lax.all_to_all(grouped, 'chan', split_axis=0, concat_axis=2, tiled=True)  9.4 us
    concatenate x1, other arithmetic, body(): table = jnp.concatenate(parts, axis=0)  7.41 us
    all_to_all x1, waiting for transfers between devices, body(): lax.all_to_all(grouped, 'chan', split_axis=0, concat_axis=2, tiled=True)  7.08 us
  transfers between devices with their start and end apart: 4, of which 3 were waited for; matrix products, arithmetic and copies ran while one was open for 4% of the time, Pallas kernels for 12%

profile of v3, /device:TPU:0, one launch (start us, length us, event | category | flops | bytes accessed | tf_op | source)
XLA Modules:
  0.0 172.2 jit_solution(7010334124985096679)
XLA Ops:
  6.5 1.0 slice.29
  7.6 2.4 %collective-permute-start = (bf16[512,60]{1,0:T(8,128)(2,1)S(1)}, bf16[512,60]{1,0:T(8,128)(2,1)S(1)}, u32[]{:S(2)}, u32[]{:S(2)}) collective-permute-start(bf16[512,60]{1,0:T(8,128)(2,1)S(1)} %slice.29), channel_id=1, source_target_pairs={{0,1},{1,2},{2,3},{3,4},{4,5},{5,6},{6,7},{7,8},{8,9},{9,10},{10,1... | collective-permute-start | bytes 184328 | tf_op jit(solution)/shard_map/ppermute | solution.py:23
  10.0 1.9 %fusion.24 = f32[256,512]{1,0:T(8,128)S(1)} fusion(bf16[1024,256]{1,0:T(8,128)(2,1)} %constant.87, bf16[512,1024]{1,0:T(8,128)(2,1)} %param.4), kind=kOutput, calls=%fused_computation.60 | convolution fusion | flops 268435456 | bytes 2097152 | tf_op jit(solution)/shard_map/dot_general | solution.py:48
  11.9 1.0 fusion.1
  12.9 0.8 copy.5
  13.7 9.4 %all-to-all-start = ((bf16[16,32,256]{2,1,0:T(8,128)(2,1)}), bf16[16,32,256]{2,1,0:T(8,128)(2,1)S(1)}, u32[]{:S(2)}, u32[]{:S(2)}) async-start(bf16[16,32,256]{2,1,0:T(8,128)(2,1)} %bitcast.1), calls=%async_computation | async-start | bytes 524288 | tf_op jit(solution)/shard_map/all_to_all | solution.py:130
  23.2 0.7 convert_element_type.28
  23.8 2.2 %cosine_convert_fusion = (bf16[512,192]{1,0:T(8,128)(2,1)S(1)}, bf16[512,192]{1,0:T(8,128)(2,1)S(1)}) fusion(s32[192]{0:T(256)S(1)} %iota_add_fusion.1), kind=kLoop, calls=%fused_computation.12 | loop fusion | flops 1671168 | bytes 393984 | tf_op jit(solution)/shard_map/convert.7
  26.1 7.1 %all-to-all-done = bf16[16,32,256]{2,1,0:T(8,128)(2,1)S(1)} async-done(((bf16[16,32,256]{2,1,0:T(8,128)(2,1)}), bf16[16,32,256]{2,1,0:T(8,128)(2,1)S(1)}, u32[]{:S(2)}, u32[]{:S(2)}) %all-to-all-start) | async-done | bytes 262176 | tf_op jit(solution)/shard_map/all_to_all | solution.py:130
  33.1 0.1 copy.6
  33.4 0.4 fusion.8
  33.8 0.2 fusion.21
  34.0 0.2 fusion.15
  34.4 0.7 fusion.23
  35.2 0.7 all-gather.3.cloned.1.call-update
  35.9 0.9 cosine_convert_fusion.1
  36.8 0.7 pad_maximum_fusion.3.delays_ref
  37.6 1.1 pad_maximum_fusion.1
  38.7 34.6 %all-gather.5.cloned.1.call-done = bf16[256,8,384]{2,0,1:T(8,128)(2,1)} async-done(((bf16[16,8,384]{2,0,1:T(8,128)(2,1)}), bf16[256,8,384]{2,0,1:T(8,128)(2,1)}) %all-gather.5.cloned.1.call-update) | async-done | bytes 1572880 | tf_op jit(solution)/shard_map/all_gather | solution.py:140
  73.3 20.6 %shard_map.47 = bf16[256,32,256]{2,1,0:T(8,128)(2,1)} custom-call(bf16[8,256,384]{2,1,0:T(8,128)(2,1)} %bitcast.21, f32[8,32,384]{2,1,0:T(8,128)} %get-tuple-element.18.plain_ref, f32[8,32,384]{2,1,0:T(8,128)} %get-tuple-element.19.swapped_ref, bf16[384,256]{1,0:T(8,128)(2,1)} %pad_maximum_fusion.3.delays_ref), custom_call_target="tpu_custom_call" | custom-call | tf_op jit(solution)/shard_map/pallas_call | solution.py:105
  93.9 20.4 %all-gather.3.cloned.1.call-done = bf16[256,8,384]{2,0,1:T(8,128)(2,1)} async-done(((bf16[16,8,384]{2,0,1:T(8,128)(2,1)}), bf16[256,8,384]{2,0,1:T(8,128)(2,1)}) %all-gather.3.cloned.1.call-update) | async-done | bytes 1572880 | tf_op jit(solution)/shard_map/all_gather | solution.py:140
  114.3 20.6 %shard_map.46 = bf16[256,32,256]{2,1,0:T(8,128)(2,1)} custom-call(bf16[8,256,384]{2,1,0:T(8,128)(2,1)} %bitcast.22, f32[8,32,384]{2,1,0:T(8,128)} %get-tuple-element.18.plain_ref, f32[8,32,384]{2,1,0:T(8,128)} %get-tuple-element.19.swapped_ref, bf16[384,256]{1,0:T(8,128)(2,1)} %pad_maximum_fusion.3.delays_ref), custom_call_target="tpu_custom_call" | custom-call | tf_op jit(solution)/shard_map/pallas_call | solution.py:105
  134.9 7.4 %pad_maximum_fusion = bf16[512,32,256]{2,1,0:T(8,128)(2,1)} fusion(bf16[256,32,256]{2,1,0:T(8,128)(2,1)} %shard_map.47, bf16[256,32,256]{2,1,0:T(8,128)(2,1)} %shard_map.46), kind=kLoop, calls=%fused_computation.1 | loop fusion | flops 4194304 | bytes 16777216 | tf_op jit(solution)/shard_map/concatenate | solution.py:142
  142.3 23.0 %gather_fusion = bf16[512,32,256]{2,1,0:T(8,128)(2,1)} fusion(bf16[512,32,256]{2,1,0:T(8,128)(2,1)} %pad_maximum_fusion, s32[1024]{0:T(1024)S(1)} %pad_clamp_fusion), kind=kCustom, calls=%fused_computation | custom fusion | bytes 16779264 | tf_op jit(solution)/shard_map/jit(_take)/gather | solution.py:149
  (16 shorter events, 0.5 us)
Async XLA Ops:
  6.5 29.3 %copy-start = (s32[512]{0:T(512)S(1)}, s32[512]{0:T(512)}, u32[]{:S(2)}) copy-start(s32[512]{0:T(512)} %param.5) | copy-start | bytes 6148
  7.6 4.3 %collective-permute-start = (bf16[512,60]{1,0:T(8,128)(2,1)S(1)}, bf16[512,60]{1,0:T(8,128)(2,1)S(1)}, u32[]{:S(2)}, u32[]{:S(2)}) collective-permute-start(bf16[512,60]{1,0:T(8,128)(2,1)S(1)} %slice.29), channel_id=1, source_target_pairs={{0,1},{1,2},{2,3},{3,4},{4,5},{5,6},{6,7},{7,8},{8,9},{9,10},{10,1... | collective-permute-start | bytes 184328 | tf_op jit(solution)/shard_map/ppermute | solution.py:23
  13.7 19.4 %all-to-all-start = ((bf16[16,32,256]{2,1,0:T(8,128)(2,1)}), bf16[16,32,256]{2,1,0:T(8,128)(2,1)S(1)}, u32[]{:S(2)}, u32[]{:S(2)}) async-start(bf16[16,32,256]{2,1,0:T(8,128)(2,1)} %bitcast.1), calls=%async_computation | async-start | bytes 524288 | tf_op jit(solution)/shard_map/all_to_all | solution.py:130
  23.1 50.2 %all-gather.5.cloned.1.call-start = ((), (), s32[]{:S(2)}) async-start(), calls=%async_computation.2 | async-start | bytes 1671168 | tf_op jit(solution)/shard_map/all_gather | solution.py:140
  35.1 79.2 %all-gather.3.cloned.1.call-start = ((), (), s32[]{:S(2)}) async-start(), calls=%async_computation.1 | async-start | bytes 1671168 | tf_op jit(solution)/shard_map/all_gather | solution.py:140
Sparse Core Ops, SparseCore 0:
  35.2 38.0 all-gather.4
  75.5 38.7 all-gather.2

commit v4 on v2

--- a/solution.py
+++ b/solution.py
@@ -73,15 +73,14 @@
 
 
 def correlate_kernel(source_ref, plain_ref, swapped_ref, delays_ref, out_ref, cross_ref):
-    block = source_ref.shape[0]
+    block = source_ref.shape[1]
     receivers = plain_ref.shape[1]
 
     def one_source(s, carry):
-        source = source_ref[s].astype(jnp.float32)
         direct = jnp.zeros((receivers, 2 * NF), jnp.float32)
         crossed = jnp.zeros((receivers, 2 * NF), jnp.float32)
         for w in range(SEGS):
-            row = source[w : w + 1, :]
+            row = source_ref[w, pl.ds(s, 1), :].astype(jnp.float32)
             direct = direct + row * plain_ref[w]
             crossed = crossed + row * swapped_ref[w]
         cross = direct - pltpu.roll(crossed, NF, 1)
@@ -96,9 +95,9 @@
 
 
 def correlate(chosen, receivers, delays, block=32):
-    source_count = chosen.shape[0]
-    recv_count = receivers.shape[0]
-    spectra = receivers.astype(jnp.float32).transpose(1, 0, 2)
+    source_count = chosen.shape[1]
+    recv_count = receivers.shape[1]
+    spectra = receivers.astype(jnp.float32)
     real_part = spectra[..., :NF]
     imag_part = spectra[..., NF:]
     plain = jnp.concatenate([real_part, real_part], axis=-1)
@@ -107,7 +106,7 @@
         correlate_kernel,
         grid=(source_count // block,),
         in_specs=[
-            pl.BlockSpec((block, SEGS, 2 * NF), lambda i: (i, 0, 0)),
+            pl.BlockSpec((SEGS, block, 2 * NF), lambda i: (0, i, 0)),
             pl.BlockSpec((SEGS, recv_count, 2 * NF), lambda i: (0, 0, 0)),
             pl.BlockSpec((SEGS, recv_count, 2 * NF), lambda i: (0, 0, 0)),
             pl.BlockSpec((2 * NF, LAGS), lambda i: (0, 0)),
@@ -121,23 +120,40 @@
 def body(recording, source_index, channel_mask):
     channels, raw_count = recording.shape
     devices = lax.axis_size("chan")
+    me = lax.axis_index("chan")
     per_device = channels // devices
     dec_length = raw_count // 4
+    sharing = devices // SEGS
+    span = channels // sharing
     trailing = recording[:, raw_count - (TAPS - 4) :]
     earlier = from_behind(trailing, "chan", 1)
     decimated = decimate(earlier, recording, dec_length)
-    grouped = decimated.reshape(devices, per_device, dec_length)
-    fourier = fourier_table()
-    block = lax.all_to_all(grouped, "chan", split_axis=0, concat_axis=2, tiled=True)
-    members = block.shape[1]
-    segments = block.reshape(members * SEGS, NSEG)
-    spectrum = jnp.dot(segments, fourier, preferred_element_type=jnp.float32)
-    whitened = whiten(spectrum).reshape(members, SEGS, 2 * NF)
-    whitened = whitened * channel_mask.astype(jnp.bfloat16)[:, None, None]
-    shard_rows = lax.all_gather(whitened, "chan", axis=0, tiled=True)
-    row_count = shard_rows.shape[0]
-    chosen = jnp.take(shard_rows, jnp.clip(source_index, 0, row_count - 1), axis=0, mode="clip")
-    result = correlate(chosen, whitened, delay_table())
+    slot = me % sharing
+    rows = lax.dynamic_slice_in_dim(fourier_table(), slot * dec_length, dec_length, axis=0)
+    partial = jnp.dot(decimated, rows, preferred_element_type=jnp.float32)
+    pieces = partial.reshape(sharing, span, 2 * NF)
+    spectrum = lax.dynamic_index_in_dim(pieces, slot, 0, keepdims=False)
+    for step in range(1, sharing):
+        route = [
+            (group * sharing + i, group * sharing + (i + step) % sharing)
+            for group in range(devices // sharing)
+            for i in range(sharing)
+        ]
+        outgoing = lax.dynamic_index_in_dim(pieces, (slot + step) % sharing, 0, keepdims=False)
+        spectrum = spectrum + lax.ppermute(outgoing, "chan", route)
+    whitened = whiten(spectrum)
+    flags = channel_mask.astype(jnp.bfloat16)
+    flag_rows = jnp.zeros((16, 2 * NF), jnp.bfloat16).at[0, :per_device].set(flags)
+    piece = jnp.concatenate([whitened, flag_rows], axis=0)
+    gathered = lax.all_gather(piece, "chan", axis=0, tiled=False)
+    table = gathered[:, :span].reshape(SEGS, channels, 2 * NF)
+    flags_all = gathered[:, span, :per_device].reshape(channels)
+    receivers = lax.dynamic_slice_in_dim(table, me * per_device, per_device, axis=1)
+    receivers = receivers * flags[None, :, None]
+    picked = jnp.clip(source_index, 0, channels - 1)
+    chosen = jnp.take(table, picked, axis=1, mode="clip")
+    chosen = chosen * jnp.take(flags_all, picked, mode="clip")[None, :, None]
+    result = correlate(chosen, receivers, delay_table())
     return result.reshape(SOURCES, per_device, LAGS)
 
 

time: 131 us -> 135 us (1.031)
  local copies, waits for them, and re-layouts: 9.02 us -> 16 us
  starting transfers between devices: 12 us -> 5.09 us
  other arithmetic: 6.27 us -> 10.5 us
  waiting for transfers between devices: 48.7 us -> 46.7 us
    all_to_all x1 -> x0, starting transfers between devices: 9.53 us -> none  [body(): lax.all_to_all(grouped, 'chan', split_axis=0, concat_axis=2, tiled=True)]
    all_to_all x1 -> x0, waiting for transfers between devices: 7.69 us -> none  [body(): lax.all_to_all(grouped, 'chan', split_axis=0, concat_axis=2, tiled=True)]
    gather x1 -> x2, local copies, waits for them, and re-layouts: 3.12 us -> 8.31 us  [the longest x1 4.81 us: body(): chosen = jnp.take(table, picked, axis=1, mode='clip')]
    all_gather x1, waiting for transfers between devices: 41 us -> 45.3 us  [body(): gathered = lax.all_gather(piece, 'chan', axis=0, tiled=False)]
    mul x0 -> x1, other arithmetic: none -> 4.16 us  [body(): chosen = chosen * jnp.take(flags_all, picked, mode='clip')[None, :, None]]
    all_gather x1 -> x0, local copies, waits for them, and re-layouts: 3.74 us -> none  [body(): shard_rows = lax.all_gather(whitened, 'chan', axis=0, tiled=True)]
    reshape x1, local copies, waits for them, and re-layouts: 0.09 us -> 3.52 us  [body(): table = gathered[:, :span].reshape(SEGS, channels, 2 * NF)]
    slice x0 -> x2, local copies, waits for them, and re-layouts: none -> 3.06 us  [the longest x1 2.27 us: body(): table = gathered[:, :span].reshape(SEGS, channels, 2 * NF)]
  transfers between devices with their start and end apart: 3 -> 3, of which waited for: 2 -> 2; matrix products, arithmetic and copies ran while one was open for 5% -> 4% of each run, Pallas kernels for 0% -> 0%
where the time goes in v4:
time: 135 us; the launch traced here: 134 us
  waiting for transfers between devices  46.7 us (35%)
  Pallas kernels  39.2 us (29%)
  local copies, waits for them, and re-layouts  16 us (12%)
  between operations  13.6 us (10%)
  other arithmetic  10.5 us (8%)
  starting transfers between devices  5.09 us (4%)
  matrix products  3.19 us (2%)
    all_gather x1, waiting for transfers between devices, body(): gathered = lax.all_gather(piece, 'chan', axis=0, tiled=False)  45.3 us
    pallas_call x1, Pallas kernels, correlate(): pl.pallas_call(correlate_kernel, grid=(source_count // block,), in_specs=...  39.2 us
    gather x1, local copies, waits for them, and re-layouts, body(): chosen = jnp.take(table, picked, axis=1, mode='clip')  4.81 us
    mul x1, other arithmetic, body(): chosen = chosen * jnp.take(flags_all, picked, mode='clip')[None, :, None]  4.16 us
    reshape x1, local copies, waits for them, and re-layouts, body(): table = gathered[:, :span].reshape(SEGS, channels, 2 * NF)  3.52 us
    gather x1, local copies, waits for them, and re-layouts, body(): chosen = chosen * jnp.take(flags_all, picked, mode='clip')[None, :, None]  3.5 us
    another operation x3, other arithmetic  3.3 us
  transfers between devices with their start and end apart: 3, of which 2 were waited for; matrix products, arithmetic and copies ran while one was open for 4% of the time, Pallas kernels for 0%

profile of v4, /device:TPU:0, one launch (start us, length us, event | category | flops | bytes accessed | tf_op | source)
XLA Modules:
  0.0 134.3 jit_solution(8001881839768559147)
XLA Ops:
  6.5 1.0 slice.43
  7.6 2.4 %collective-permute-start = (bf16[512,60]{1,0:T(8,128)(2,1)S(1)}, bf16[512,60]{1,0:T(8,128)(2,1)S(1)}, u32[]{:S(2)}, u32[]{:S(2)}) collective-permute-start(bf16[512,60]{1,0:T(8,128)(2,1)S(1)} %slice.43), channel_id=1, source_target_pairs={{0,1},{1,2},{2,3},{3,4},{4,5},{5,6},{6,7},{7,8},{8,9},{9,10},{10,1... | collective-permute-start | bytes 184328 | tf_op jit(solution)/shard_map/ppermute | solution.py:23
  10.0 1.9 %fusion.21 = f32[256,512]{1,0:T(8,128)S(1)} fusion(bf16[1024,256]{1,0:T(8,128)(2,1)} %constant.114, bf16[512,1024]{1,0:T(8,128)(2,1)} %param.6), kind=kOutput, calls=%fused_computation.57 | convolution fusion | flops 268435456 | bytes 2097152 | tf_op jit(solution)/shard_map/dot_general | solution.py:48
  11.9 2.2 %negate_convert_fusion = (bf16[512,192]{1,0:T(8,128)(2,1)S(1)}, bf16[512,192]{1,0:T(8,128)(2,1)S(1)}) fusion(s32[192]{0:T(256)S(1)} %iota_add_fusion.1), kind=kLoop, calls=%fused_computation.13 | loop fusion | flops 1671168 | bytes 393984 | tf_op jit(solution)/shard_map/convert.5
  14.2 1.3 fusion.2
  15.5 2.7 %collective-permute-start.1 = (f32[256,384]{1,0:T(8,128)S(1)}, f32[256,384]{1,0:T(8,128)S(1)}, u32[]{:S(2)}, u32[]{:S(2)}) collective-permute-start(f32[256,384]{1,0:T(8,128)S(1)} %dynamic-slice_bitcast_fusion), channel_id=1, source_target_pairs={{0,1},{1,0},{2,3},{3,2},{4,5},{5,4},{6,7},{7,6},{8,9},{9,8},{10,11... | collective-permute-start | bytes 1179656 | tf_op jit(solution)/shard_map/ppermute | solution.py:143
  18.2 1.3 collective-permute-done.1
  19.6 0.2 fusion.18
  19.8 0.2 multiply_convert_fusion.1
  20.0 0.8 fusion.10
  20.9 0.9 cosine_convert_fusion.1
  21.8 0.7 pad_maximum_fusion.2.delays_ref
  22.4 45.3 %all-gather.3.cloned.1.call-done = bf16[4352,384]{1,0:T(8,128)(2,1)} async-done(((bf16[272,384]{1,0:T(8,128)(2,1)}), bf16[4352,384]{1,0:T(8,128)(2,1)}) %all-gather.3.cloned.1.call-update) | async-done | bytes 3342352 | tf_op jit(solution)/shard_map/all_gather | solution.py:148
  67.8 0.8 slice_reduce_fusion
  68.6 2.3 %slice.58 = bf16[16,256,384]{2,1,0:T(8,128)(2,1)S(1)} slice(bf16[16,272,384]{2,1,0:T(8,128)(2,1)} %bitcast.20), slice={[0:16], [0:256], [0:384]} | slice | bytes 6291456 | tf_op jit(solution)/shard_map/slice | solution.py:149
  70.8 0.1 reshape_squeeze.3
  70.9 3.5 %copy.8 = bf16[8,512,384]{2,0,1:T(8,128)(2,1)} copy(bf16[8,512,384]{2,1,0:T(8,128)(2,1)S(1)} %bitcast.15) | data formatting | bytes 6291456 | tf_op jit(solution)/shard_map/reshape | solution.py:149
  74.4 3.5 %gather_fusion.1 = bf16[512]{0:T(512)(128)(2,1)S(1)} fusion(bf16[512]{0:T(512)(128)(2,1)S(1)} %reshape_squeeze.3, s32[1024]{0:T(1024)S(1)} %pad_clamp_fusion), kind=kCustom, calls=%fused_computation.1 | custom fusion | bytes 4096 | tf_op jit(solution)/shard_map/jit(_take)/gather | solution.py:155
  78.0 4.8 %gather_fusion = bf16[512,8,384]{2,1,0:T(8,128)(2,1)} fusion(bf16[8,512,384]{2,0,1:T(8,128)(2,1)} %copy.8, s32[1024]{0:T(1024)S(1)} %pad_clamp_fusion), kind=kCustom, calls=%fused_computation | custom fusion | bytes 6293504 | tf_op jit(solution)/shard_map/jit(_take)/gather | solution.py:154
  82.8 0.1 multiply_convert_fusion.2
  82.9 0.1 fusion.19
  83.0 4.2 %fusion.source_ref = bf16[8,512,384]{2,1,0:T(8,128)(2,1)} fusion(bf16[512,8,384]{2,1,0:T(8,128)(2,1)} %gather_fusion, bf16[512]{0:T(512)(128)(2,1)S(1)} %gather_fusion.1), kind=kLoop, calls=%fused_computation.3 | loop fusion | flops 1572864 | bytes 6292480 | tf_op jit(solution)/shard_map/mul | solution.py:155
  87.2 1.1 pad_maximum_fusion
  88.3 39.2 %shard_map.46 = bf16[512,32,256]{2,1,0:T(8,128)(2,1)} custom-call(bf16[8,512,384]{2,1,0:T(8,128)(2,1)} %fusion.source_ref, f32[8,32,384]{2,1,0:T(8,128)} %get-tuple-element.28.plain_ref, f32[8,32,384]{2,1,0:T(8,128)} %get-tuple-element.29.swapped_ref, bf16[384,256]{1,0:T(8,128)(2,1)} %pad_maximum_fusion.2.delays_ref), custom_call_target="tpu_custom_call" | custom-call | tf_op jit(solution)/shard_map/pallas_call | solution.py:105
  (15 shorter events, 0.1 us)
Async XLA Ops:
  6.5 11.7 %copy-start.1 = (s32[32]{0:T(128)S(1)}, s32[32]{0:T(128)}, u32[]{:S(2)}) copy-start(s32[32]{0:T(128)} %param.8) | copy-start | bytes 388
  6.5 61.2 %all-gather.3.cloned.1.call-start = ((), (), s32[]{:S(2)}) async-start(), calls=%async_computation | async-start | bytes 3551232 | tf_op jit(solution)/shard_map/all_gather | solution.py:148
  7.6 6.6 %collective-permute-start = (bf16[512,60]{1,0:T(8,128)(2,1)S(1)}, bf16[512,60]{1,0:T(8,128)(2,1)S(1)}, u32[]{:S(2)}, u32[]{:S(2)}) collective-permute-start(bf16[512,60]{1,0:T(8,128)(2,1)S(1)} %slice.43), channel_id=1, source_target_pairs={{0,1},{1,2},{2,3},{3,4},{4,5},{5,6},{6,7},{7,8},{8,9},{9,10},{10,1... | collective-permute-start | bytes 184328 | tf_op jit(solution)/shard_map/ppermute | solution.py:23
  14.1 6.7 %copy-start = (s32[512]{0:T(512)S(1)}, s32[512]{0:T(512)}, u32[]{:S(2)}) copy-start(s32[512]{0:T(512)} %param.7) | copy-start | bytes 6148
  15.5 4.0 %collective-permute-start.1 = (f32[256,384]{1,0:T(8,128)S(1)}, f32[256,384]{1,0:T(8,128)S(1)}, u32[]{:S(2)}, u32[]{:S(2)}) collective-permute-start(f32[256,384]{1,0:T(8,128)S(1)} %dynamic-slice_bitcast_fusion), channel_id=1, source_target_pairs={{0,1},{1,0},{2,3},{3,2},{4,5},{5,4},{6,7},{7,6},{8,9},{9,8},{10,11... | collective-permute-start | bytes 1179656 | tf_op jit(solution)/shard_map/ppermute | solution.py:143
Sparse Core Ops, SparseCore 0:
  21.0 46.7 all-gather.2

commit v5 on v4

--- a/solution.py
+++ b/solution.py
@@ -72,7 +72,7 @@
     return jnp.concatenate([real_part * factor, imag_part * factor], axis=1).astype(jnp.bfloat16)
 
 
-def correlate_kernel(source_ref, plain_ref, swapped_ref, delays_ref, out_ref, cross_ref):
+def correlate_kernel(flags_ref, source_ref, plain_ref, swapped_ref, delays_ref, out_ref, cross_ref):
     block = source_ref.shape[1]
     receivers = plain_ref.shape[1]
 
@@ -83,7 +83,8 @@
             row = source_ref[w, pl.ds(s, 1), :].astype(jnp.float32)
             direct = direct + row * plain_ref[w]
             crossed = crossed + row * swapped_ref[w]
-        cross = direct - pltpu.roll(crossed, NF, 1)
+        flag = flags_ref[pl.program_id(0) * block + s].astype(jnp.float32)
+        cross = (direct - pltpu.roll(crossed, NF, 1)) * flag
         start = pl.multiple_of(s * receivers, receivers)
         cross_ref[pl.ds(start, receivers), :] = cross.astype(jnp.bfloat16)
         return carry
@@ -94,7 +95,7 @@
     out_ref[...] = lagged.astype(jnp.bfloat16).reshape(out_ref.shape)
 
 
-def correlate(chosen, receivers, delays, block=32):
+def correlate(chosen, source_flags, receivers, delays, block=32):
     source_count = chosen.shape[1]
     recv_count = receivers.shape[1]
     spectra = receivers.astype(jnp.float32)
@@ -102,19 +103,23 @@
     imag_part = spectra[..., NF:]
     plain = jnp.concatenate([real_part, real_part], axis=-1)
     swapped = jnp.concatenate([imag_part, -imag_part], axis=-1)
+    grid_spec = pltpu.PrefetchScalarGridSpec(
+        num_scalar_prefetch=1,
+        grid=(source_count // block,),
+        in_specs=[
+            pl.BlockSpec((SEGS, block, 2 * NF), lambda i, flags: (0, i, 0)),
+            pl.BlockSpec((SEGS, recv_count, 2 * NF), lambda i, flags: (0, 0, 0)),
+            pl.BlockSpec((SEGS, recv_count, 2 * NF), lambda i, flags: (0, 0, 0)),
+            pl.BlockSpec((2 * NF, LAGS), lambda i, flags: (0, 0)),
+        ],
+        out_specs=pl.BlockSpec((block, recv_count, LAGS), lambda i, flags: (i, 0, 0)),
+        scratch_shapes=[pltpu.VMEM((block * recv_count, 2 * NF), jnp.bfloat16)],
+    )
     return pl.pallas_call(
         correlate_kernel,
-        grid=(source_count // block,),
-        in_specs=[
-            pl.BlockSpec((SEGS, block, 2 * NF), lambda i: (0, i, 0)),
-            pl.BlockSpec((SEGS, recv_count, 2 * NF), lambda i: (0, 0, 0)),
-            pl.BlockSpec((SEGS, recv_count, 2 * NF), lambda i: (0, 0, 0)),
-            pl.BlockSpec((2 * NF, LAGS), lambda i: (0, 0)),
-        ],
-        out_specs=pl.BlockSpec((block, recv_count, LAGS), lambda i: (i, 0, 0)),
+        grid_spec=grid_spec,
         out_shape=jax.ShapeDtypeStruct((source_count, recv_count, LAGS), jnp.bfloat16),
-        scratch_shapes=[pltpu.VMEM((block * recv_count, 2 * NF), jnp.bfloat16)],
-    )(chosen, plain, swapped, delays)
+    )(source_flags, chosen, plain, swapped, delays)
 
 
 def body(recording, source_index, channel_mask):
@@ -145,15 +150,20 @@
     flags = channel_mask.astype(jnp.bfloat16)
     flag_rows = jnp.zeros((16, 2 * NF), jnp.bfloat16).at[0, :per_device].set(flags)
     piece = jnp.concatenate([whitened, flag_rows], axis=0)
-    gathered = lax.all_gather(piece, "chan", axis=0, tiled=False)
-    table = gathered[:, :span].reshape(SEGS, channels, 2 * NF)
-    flags_all = gathered[:, span, :per_device].reshape(channels)
-    receivers = lax.dynamic_slice_in_dim(table, me * per_device, per_device, axis=1)
+    gathered = lax.all_gather(piece, "chan", axis=0, tiled=True)
+    height = piece.shape[0]
+    segment_base = jnp.arange(SEGS, dtype=jnp.int32)[:, None] * (sharing * height)
+    picked = jnp.clip(source_index, 0, channels - 1)
+    source_rows = segment_base + (picked // span * height + picked % span)[None, :]
+    chosen = jnp.take(gathered, source_rows, axis=0, mode="clip")
+    flag_rows_at = jnp.arange(devices, dtype=jnp.int32) * height + span
+    flags_all = jnp.take(gathered, flag_rows_at, axis=0, mode="clip")[:, :per_device]
+    source_flags = jnp.take(flags_all.reshape(channels), picked, mode="clip")
+    own = me * per_device + jnp.arange(per_device, dtype=jnp.int32)
+    receiver_rows = segment_base + (own // span * height + own % span)[None, :]
+    receivers = jnp.take(gathered, receiver_rows, axis=0, mode="clip")
     receivers = receivers * flags[None, :, None]
-    picked = jnp.clip(source_index, 0, channels - 1)
-    chosen = jnp.take(table, picked, axis=1, mode="clip")
-    chosen = chosen * jnp.take(flags_all, picked, mode="clip")[None, :, None]
-    result = correlate(chosen, receivers, delay_table())
+    result = correlate(chosen, source_flags.astype(jnp.int32), receivers, delay_table())
     return result.reshape(SOURCES, per_device, LAGS)
 
 

time: 135 us -> 145 us (1.074)
  local copies, waits for them, and re-layouts: 16 us -> 28.6 us
  other arithmetic: 10.5 us -> 8.81 us
    gather x2 -> x4, local copies, waits for them, and re-layouts: 8.31 us -> 27.4 us  [the longest x1 17.1 us: body(): chosen = jnp.take(gathered, source_rows, axis=0, mode='clip')]
    mul x1, other arithmetic: 4.16 us -> 0.01 us  [body(): jnp.arange(SEGS, dtype=jnp.int32)[:, None] * (sharing * height)]
    reshape x1, local copies, waits for them, and re-layouts: 3.52 us -> 0.09 us  [body(): source_flags = jnp.take(flags_all.reshape(channels), picked, mode='clip')]
    slice x2 -> x1, local copies, waits for them, and re-layouts: 3.06 us -> 0.01 us  [body(): jnp.take(gathered, flag_rows_at, axis=0, mode='clip')[:, :per_device]]
  transfers between devices with their start and end apart: 3 -> 3, of which waited for: 2 -> 2; matrix products, arithmetic and copies ran while one was open for 4% -> 5% of each run, Pallas kernels for 0% -> 0%
where the time goes in v5:
time: 145 us
  waiting for transfers between devices  45.3 us (31%)
  Pallas kernels  40.2 us (28%)
  local copies, waits for them, and re-layouts  28.6 us (20%)
  between operations  13.6 us (9%)
  other arithmetic  8.81 us (6%)
  starting transfers between devices  5.09 us (4%)
  matrix products  3.19 us (2%)
    all_gather x1, waiting for transfers between devices, body(): gathered = lax.all_gather(piece, 'chan', axis=0, tiled=True)  44.4 us
    pallas_call x1, Pallas kernels, correlate(): pl.pallas_call(correlate_kernel, grid_spec=grid_spec, out_shape=jax.Shape...  40.2 us
    gather x1, local copies, waits for them, and re-layouts, body(): chosen = jnp.take(gathered, source_rows, axis=0, mode='clip')  17.1 us
    gather x1, local copies, waits for them, and re-layouts, body(): receivers = jnp.take(gathered, receiver_rows, axis=0, mode='clip')  3.66 us
    gather x1, local copies, waits for them, and re-layouts, body(): source_flags = jnp.take(flags_all.reshape(channels), picked, mode='clip')  3.51 us
    another operation x3, other arithmetic  3.3 us
    gather x1, local copies, waits for them, and re-layouts, body(): jnp.take(gathered, flag_rows_at, axis=0, mode='clip')[:, :per_device]  3.12 us
  transfers between devices with their start and end apart: 3, of which 2 were waited for; matrix products, arithmetic and copies ran while one was open for 5% of the time, Pallas kernels for 0%

profile of v5, /device:TPU:0, one launch (start us, length us, event | category | flops | bytes accessed | tf_op | source)
XLA Modules:
  0.0 144.8 jit_solution(14235756515602756601)
XLA Ops:
  6.5 1.0 slice.40
  7.6 2.4 %collective-permute-start = (bf16[512,60]{1,0:T(8,128)(2,1)S(1)}, bf16[512,60]{1,0:T(8,128)(2,1)S(1)}, u32[]{:S(2)}, u32[]{:S(2)}) collective-permute-start(bf16[512,60]{1,0:T(8,128)(2,1)S(1)} %slice.40), channel_id=1, source_target_pairs={{0,1},{1,2},{2,3},{3,4},{4,5},{5,6},{6,7},{7,8},{8,9},{9,10},{10,1... | collective-permute-start | bytes 184328 | tf_op jit(solution)/shard_map/ppermute | solution.py:23
  10.0 1.9 %fusion.25 = f32[256,512]{1,0:T(8,128)S(1)} fusion(bf16[1024,256]{1,0:T(8,128)(2,1)} %constant.162, bf16[512,1024]{1,0:T(8,128)(2,1)} %param.6), kind=kOutput, calls=%fused_computation.79 | convolution fusion | flops 268435456 | bytes 2097152 | tf_op jit(solution)/shard_map/dot_general | solution.py:48
  11.9 2.2 %negate_convert_fusion = (bf16[512,192]{1,0:T(8,128)(2,1)S(1)}, bf16[512,192]{1,0:T(8,128)(2,1)S(1)}) fusion(s32[192]{0:T(256)S(1)} %iota_add_fusion.1), kind=kLoop, calls=%fused_computation.13 | loop fusion | flops 1671168 | bytes 393984 | tf_op jit(solution)/shard_map/convert.5
  14.2 1.3 fusion.1
  15.5 2.7 %collective-permute-start.1 = (f32[256,384]{1,0:T(8,128)S(1)}, f32[256,384]{1,0:T(8,128)S(1)}, u32[]{:S(2)}, u32[]{:S(2)}) collective-permute-start(f32[256,384]{1,0:T(8,128)S(1)} %dynamic-slice_bitcast_fusion), channel_id=1, source_target_pairs={{0,1},{1,0},{2,3},{3,2},{4,5},{5,4},{6,7},{7,6},{8,9},{9,8},{10,11... | collective-permute-start | bytes 1179656 | tf_op jit(solution)/shard_map/ppermute | solution.py:148
  18.2 0.5 fusion.24
  18.7 0.9 collective-permute-done.1
  19.6 0.2 fusion.22
  19.8 0.2 multiply_convert_fusion.1
  20.0 0.8 fusion.9
  21.1 0.6 pad_clamp_fusion
  21.8 0.9 cosine_convert_fusion.1
  22.6 0.7 pad_maximum_fusion.2.delays_ref
  23.3 44.4 %all-gather.2.cloned.1.call-done = bf16[4352,384]{1,0:T(8,128)(2,1)} async-done(((bf16[272,384]{1,0:T(8,128)(2,1)}), bf16[4352,384]{1,0:T(8,128)(2,1)}) %all-gather.2.cloned.1.call-update) | async-done | bytes 3342352 | tf_op jit(solution)/shard_map/all_gather | solution.py:153
  67.8 3.1 %gather_fusion = bf16[16,384]{1,0:T(8,128)(2,1)S(1)} fusion(bf16[4352,384]{1,0:T(8,128)(2,1)} %all-gather.2.cloned.1.call-done, s32[1024]{0:T(1024)S(1)} %pad_clamp_fusion.2), kind=kCustom, calls=%fused_computation | custom fusion | bytes 24640 | tf_op jit(solution)/shard_map/jit(_take)/gather | solution.py:160
  71.0 3.5 %gather_fusion.1 = bf16[512]{0:T(512)(128)(2,1)S(1)} fusion(bf16[512]{0:T(512)(128)(2,1)S(1)} %reshape.190, s32[1024]{0:T(1024)S(1)} %pad_clamp_fusion.1), kind=kCustom, calls=%fused_computation.1 | custom fusion | bytes 4096 | tf_op jit(solution)/shard_map/jit(_take)/gather | solution.py:161
  74.5 0.6 convert_element_type.32.flags_ref
  75.1 3.7 %gather_fusion.3 = bf16[256,384]{1,0:T(8,128)(2,1)S(1)} fusion(bf16[4352,384]{1,0:T(8,128)(2,1)} %all-gather.2.cloned.1.call-done, s32[1024]{0:T(1024)} %pad_clamp_fusion), kind=kCustom, calls=%fused_computation.3 | custom fusion | bytes 394240 | tf_op jit(solution)/shard_map/jit(_take)/gather | solution.py:164
  78.7 0.7 multiply_convert_fusion.2
  79.4 0.1 fusion.23
  79.5 1.1 pad_maximum_fusion
  80.7 17.1 %gather_fusion.2 = bf16[4096,384]{1,0:T(8,128)(2,1)} fusion(bf16[4352,384]{1,0:T(8,128)(2,1)S(1)} %copy-done, s32[4096]{0:T(1024)S(1)} %broadcast_clamp_fusion), kind=kCustom, calls=%fused_computation.2 | custom fusion | bytes 6307840 | tf_op jit(solution)/shard_map/jit(_take)/gather | solution.py:158
  97.8 40.2 %shard_map.46 = bf16[512,32,256]{2,1,0:T(8,128)(2,1)} custom-call(s32[512]{0:T(512)} %convert_element_type.32.flags_ref, bf16[8,512,384]{2,1,0:T(8,128)(2,1)} %bitcast.21, f32[8,32,384]{2,1,0:T(8,128)} %get-tuple-element.30.plain_ref, f32[8,32,384]{2,1,0:T(8,128)} %get-tuple-element.31.swapped_ref, bf16[384,256]{1,0:T(8,128)(2,1)} %pad_maximum_fusion.2.delays_ref), custom_call_target="tpu_custom_call" | custom-call | tf_op jit(solution)/shard_map/pallas_call | solution.py:118
  (27 shorter events, 0.5 us)
Async XLA Ops:
  6.5 11.7 %copy-start.2 = (s32[32]{0:T(128)S(1)}, s32[32]{0:T(128)}, u32[]{:S(2)}) copy-start(s32[32]{0:T(128)} %param.8) | copy-start | bytes 388
  6.5 61.2 %all-gather.2.cloned.1.call-start = ((), (), s32[]{:S(2)}) async-start(), calls=%async_computation | async-start | bytes 3551232 | tf_op jit(solution)/shard_map/all_gather | solution.py:153
  7.6 6.6 %collective-permute-start = (bf16[512,60]{1,0:T(8,128)(2,1)S(1)}, bf16[512,60]{1,0:T(8,128)(2,1)S(1)}, u32[]{:S(2)}, u32[]{:S(2)}) collective-permute-start(bf16[512,60]{1,0:T(8,128)(2,1)S(1)} %slice.40), channel_id=1, source_target_pairs={{0,1},{1,2},{2,3},{3,4},{4,5},{5,6},{6,7},{7,8},{8,9},{9,10},{10,1... | collective-permute-start | bytes 184328 | tf_op jit(solution)/shard_map/ppermute | solution.py:23
  11.9 9.2 %copy-start.1 = (s32[512]{0:T(512)S(1)}, s32[512]{0:T(512)}, u32[]{:S(2)}) copy-start(s32[512]{0:T(512)} %param.7) | copy-start | bytes 6148
  15.5 4.0 %collective-permute-start.1 = (f32[256,384]{1,0:T(8,128)S(1)}, f32[256,384]{1,0:T(8,128)S(1)}, u32[]{:S(2)}, u32[]{:S(2)}) collective-permute-start(f32[256,384]{1,0:T(8,128)S(1)} %dynamic-slice_bitcast_fusion), channel_id=1, source_target_pairs={{0,1},{1,0},{2,3},{3,2},{4,5},{5,4},{6,7},{7,6},{8,9},{9,8},{10,11... | collective-permute-start | bytes 1179656 | tf_op jit(solution)/shard_map/ppermute | solution.py:148
  67.8 12.9 %copy-start = (bf16[4352,384]{1,0:T(8,128)(2,1)S(1)}, bf16[4352,384]{1,0:T(8,128)(2,1)}, u32[]{:S(2)}) copy-start(bf16[4352,384]{1,0:T(8,128)(2,1)} %all-gather.2.cloned.1.call-done) | copy-start | bytes 10027012
Sparse Core Ops, SparseCore 0:
  21.0 46.7 all-gather.1

commit v6 on v5

--- a/solution.py
+++ b/solution.py
@@ -73,14 +73,15 @@
 
 
 def correlate_kernel(flags_ref, source_ref, plain_ref, swapped_ref, delays_ref, out_ref, cross_ref):
-    block = source_ref.shape[1]
+    block = source_ref.shape[0]
     receivers = plain_ref.shape[1]
 
     def one_source(s, carry):
+        source = source_ref[s].astype(jnp.float32)
         direct = jnp.zeros((receivers, 2 * NF), jnp.float32)
         crossed = jnp.zeros((receivers, 2 * NF), jnp.float32)
         for w in range(SEGS):
-            row = source_ref[w, pl.ds(s, 1), :].astype(jnp.float32)
+            row = source[w : w + 1, :]
             direct = direct + row * plain_ref[w]
             crossed = crossed + row * swapped_ref[w]
         flag = flags_ref[pl.program_id(0) * block + s].astype(jnp.float32)
@@ -96,7 +97,7 @@
 
 
 def correlate(chosen, source_flags, receivers, delays, block=32):
-    source_count = chosen.shape[1]
+    source_count = chosen.shape[0]
     recv_count = receivers.shape[1]
     spectra = receivers.astype(jnp.float32)
     real_part = spectra[..., :NF]
@@ -107,7 +108,7 @@
         num_scalar_prefetch=1,
         grid=(source_count // block,),
         in_specs=[
-            pl.BlockSpec((SEGS, block, 2 * NF), lambda i, flags: (0, i, 0)),
+            pl.BlockSpec((block, SEGS, 2 * NF), lambda i, flags: (i, 0, 0)),
             pl.BlockSpec((SEGS, recv_count, 2 * NF), lambda i, flags: (0, 0, 0)),
             pl.BlockSpec((SEGS, recv_count, 2 * NF), lambda i, flags: (0, 0, 0)),
             pl.BlockSpec((2 * NF, LAGS), lambda i, flags: (0, 0)),
@@ -150,20 +151,20 @@
     flags = channel_mask.astype(jnp.bfloat16)
     flag_rows = jnp.zeros((16, 2 * NF), jnp.bfloat16).at[0, :per_device].set(flags)
     piece = jnp.concatenate([whitened, flag_rows], axis=0)
-    gathered = lax.all_gather(piece, "chan", axis=0, tiled=True)
+    gathered = lax.all_gather(piece, "chan", axis=0, tiled=False)
     height = piece.shape[0]
-    segment_base = jnp.arange(SEGS, dtype=jnp.int32)[:, None] * (sharing * height)
+    blocks = gathered.reshape(SEGS, sharing, height, 2 * NF)
     picked = jnp.clip(source_index, 0, channels - 1)
-    source_rows = segment_base + (picked // span * height + picked % span)[None, :]
-    chosen = jnp.take(gathered, source_rows, axis=0, mode="clip")
-    flag_rows_at = jnp.arange(devices, dtype=jnp.int32) * height + span
-    flags_all = jnp.take(gathered, flag_rows_at, axis=0, mode="clip")[:, :per_device]
-    source_flags = jnp.take(flags_all.reshape(channels), picked, mode="clip")
-    own = me * per_device + jnp.arange(per_device, dtype=jnp.int32)
-    receiver_rows = segment_base + (own // span * height + own % span)[None, :]
-    receivers = jnp.take(gathered, receiver_rows, axis=0, mode="clip")
+    chosen = blocks[:, picked // span, picked % span].transpose(1, 0, 2)
+    flags_all = gathered[:, span, :per_device].reshape(channels).astype(jnp.int32)
+    hits = picked[:, None] == jnp.arange(channels, dtype=jnp.int32)[None, :]
+    source_flags = jnp.sum(jnp.where(hits, flags_all[None, :], 0), axis=1)
+    first = me * per_device
+    receivers = lax.dynamic_slice(
+        blocks, (0, first // span, first % span, 0), (SEGS, 1, per_device, 2 * NF)
+    ).reshape(SEGS, per_device, 2 * NF)
     receivers = receivers * flags[None, :, None]
-    result = correlate(chosen, source_flags.astype(jnp.int32), receivers, delay_table())
+    result = correlate(chosen, source_flags, receivers, delay_table())
     return result.reshape(SOURCES, per_device, LAGS)
 
 

time: 145 us -> 128 us (0.88)
  local copies, waits for them, and re-layouts: 28.6 us -> 9.88 us
  other arithmetic: 8.81 us -> 11 us
  Pallas kernels: 40.2 us -> 38.6 us
    gather x4 -> x1, local copies, waits for them, and re-layouts: 27.4 us -> 5.6 us  [body(): chosen = blocks[:, picked // span, picked % span].transpose(1, 0, 2)]
    reshape x1, local copies, waits for them, and re-layouts: 0.09 us -> 3.14 us  [body(): blocks = gathered.reshape(SEGS, sharing, height, 2 * NF)]
    pallas_call x1, Pallas kernels: 40.2 us -> 38.6 us  [correlate(): pl.pallas_call(correlate_kernel, grid_spec=grid_spec, out_shape=jax.Shape...]
  transfers between devices with their start and end apart: 3 -> 3, of which waited for: 2 -> 2; matrix products, arithmetic and copies ran while one was open for 5% -> 4% of each run, Pallas kernels for 0% -> 0%
where the time goes in v6:
time: 128 us
  waiting for transfers between devices  46.7 us (36%)
  Pallas kernels  38.6 us (30%)
  between operations  13.6 us (11%)
  other arithmetic  11 us (9%)
  local copies, waits for them, and re-layouts  9.88 us (8%)
  starting transfers between devices  5.09 us (4%)
  matrix products  3.19 us (2%)
    all_gather x1, waiting for transfers between devices, body(): gathered = lax.all_gather(piece, 'chan', axis=0, tiled=False)  45.3 us
    pallas_call x1, Pallas kernels, correlate(): pl.pallas_call(correlate_kernel, grid_spec=grid_spec, out_shape=jax.Shape...  38.6 us
    gather x1, local copies, waits for them, and re-layouts, body(): chosen = blocks[:, picked // span, picked % span].transpose(1, 0, 2)  5.6 us
    another operation x3, other arithmetic  3.3 us
    reshape x1, local copies, waits for them, and re-layouts, body(): blocks = gathered.reshape(SEGS, sharing, height, 2 * NF)  3.14 us
    ppermute x1, starting transfers between devices, body(): spectrum = spectrum + lax.ppermute(outgoing, 'chan', route)  2.68 us
  transfers between devices with their start and end apart: 3, of which 2 were waited for; matrix products, arithmetic and copies ran while one was open for 4% of the time, Pallas kernels for 0%

profile of v6, /device:TPU:0, one launch (start us, length us, event | category | flops | bytes accessed | tf_op | source)
XLA Modules:
  0.0 128.0 jit_solution(12574655670518670645)
XLA Ops:
  6.5 1.0 slice.40
  7.6 2.4 %collective-permute-start = (bf16[512,60]{1,0:T(8,128)(2,1)S(1)}, bf16[512,60]{1,0:T(8,128)(2,1)S(1)}, u32[]{:S(2)}, u32[]{:S(2)}) collective-permute-start(bf16[512,60]{1,0:T(8,128)(2,1)S(1)} %slice.40), channel_id=1, source_target_pairs={{0,1},{1,2},{2,3},{3,4},{4,5},{5,6},{6,7},{7,8},{8,9},{9,10},{10,1... | collective-permute-start | bytes 184328 | tf_op jit(solution)/shard_map/ppermute | solution.py:23
  10.0 1.9 %fusion.29 = f32[256,512]{1,0:T(8,128)S(1)} fusion(bf16[1024,256]{1,0:T(8,128)(2,1)} %constant.156, bf16[512,1024]{1,0:T(8,128)(2,1)} %param.6), kind=kOutput, calls=%fused_computation.72 | convolution fusion | flops 268435456 | bytes 2097152 | tf_op jit(solution)/shard_map/dot_general | solution.py:48
  11.9 2.2 %negate_convert_fusion = (bf16[512,192]{1,0:T(8,128)(2,1)S(1)}, bf16[512,192]{1,0:T(8,128)(2,1)S(1)}) fusion(s32[192]{0:T(256)S(1)} %iota_add_fusion.1), kind=kLoop, calls=%fused_computation.12 | loop fusion | flops 1671168 | bytes 393984 | tf_op jit(solution)/shard_map/convert.6
  14.1 0.0 copy-start
  14.2 1.3 %fusion.1 = f32[512,384]{1,0:T(8,128)S(1)} fusion(f32[256,512]{1,0:T(8,128)S(1)} %fusion.29, bf16[60,256]{1,0:T(8,128)(2,1)} %constant.155, bf16[512,60]{1,0:T(8,128)(2,1)S(1)} %collective-permute-done, s32[]{:T(128)S(6)} %select_n.74, bf16[512,192]{1,0:T(8,128)(2,1)S(1)} %get-tuple-element.27, bf16[512,192]{1,0:T(8,128)(2,1)S(1)} %get-tuple-element.26), kind=kOutput, calls=%fused_computation.3 | convolution fusion | flops 117047296 | bytes 1796100 | tf_op jit(solution)/shard_map/dot_general | solution.py:139
  15.5 2.7 %collective-permute-start.1 = (f32[256,384]{1,0:T(8,128)S(1)}, f32[256,384]{1,0:T(8,128)S(1)}, u32[]{:S(2)}, u32[]{:S(2)}) collective-permute-start(f32[256,384]{1,0:T(8,128)S(1)} %dynamic-slice_bitcast_fusion), channel_id=1, source_target_pairs={{0,1},{1,0},{2,3},{3,2},{4,5},{5,4},{6,7},{7,6},{8,9},{9,8},{10,11... | collective-permute-start | bytes 1179656 | tf_op jit(solution)/shard_map/ppermute | solution.py:149
  18.2 1.3 %collective-permute-done.1 = f32[256,384]{1,0:T(8,128)S(1)} collective-permute-done((f32[256,384]{1,0:T(8,128)S(1)}, f32[256,384]{1,0:T(8,128)S(1)}, u32[]{:S(2)}, u32[]{:S(2)}) %collective-permute-start.1) | collective-permute-done | bytes 393248 | tf_op jit(solution)/shard_map/ppermute | solution.py:149
  19.6 0.2 fusion.26
  19.8 0.2 multiply_convert_fusion.1
  20.0 0.8 fusion.9
  20.8 0.0 all-gather.3.cloned.1.call-update
  20.9 0.9 cosine_convert_fusion.1
  21.8 0.7 pad_maximum_fusion.2.delays_ref
  22.5 45.3 %all-gather.3.cloned.1.call-done = bf16[4352,384]{1,0:T(8,128)(2,1)} async-done(((bf16[272,384]{1,0:T(8,128)(2,1)}), bf16[4352,384]{1,0:T(8,128)(2,1)}) %all-gather.3.cloned.1.call-update) | async-done | bytes 3342352 | tf_op jit(solution)/shard_map/all_gather | solution.py:154
  67.8 0.8 fusion.16
  68.6 0.1 reshape.71
  68.6 3.1 %copy.6 = bf16[8,2,272,384]{3,0,2,1:T(8,128)(2,1)S(1)} copy(bf16[8,2,272,384]{3,2,1,0:T(8,128)(2,1)} %bitcast.18) | data formatting | bytes 6684672 | tf_op jit(solution)/shard_map/reshape | solution.py:156
  71.8 1.0 fusion.15
  72.8 1.0 fusion.27
  73.8 0.8 select_reduce_fusion.flags_ref
  74.7 5.6 %gather_fusion = bf16[512,8,384]{2,1,0:T(8,128)(2,1)} fusion(bf16[8,2,272,384]{3,0,2,1:T(8,128)(2,1)S(1)} %copy.6, s32[512]{0:T(512)S(1)} %get-tuple-element.24), kind=kCustom, calls=%fused_computation | custom fusion | bytes 6295552 | tf_op jit(solution)/shard_map/gather | solution.py:158
  80.3 2.3 %pad_maximum_fusion = (f32[8,32,384]{2,1,0:T(8,128)}, f32[8,32,384]{2,1,0:T(8,128)}) fusion(f32[8,32,192]{2,1,0:T(8,128)} %get-tuple-element.21, f32[8,32,192]{2,1,0:T(8,128)} %get-tuple-element.20, f32[8,32,192]{2,1,0:T(8,128)} %get-tuple-element.19), kind=kLoop, calls=%fused_computation.21 | loop fusion | flops 196608 | bytes 1376256 | tf_op jit(solution)/shard_map/concatenate | solution.py:105
  82.5 38.6 %shard_map.46 = bf16[512,32,256]{2,1,0:T(8,128)(2,1)} custom-call(s32[512]{0:T(512)} %select_reduce_fusion.flags_ref, bf16[512,8,384]{2,1,0:T(8,128)(2,1)} %gather_fusion, f32[8,32,384]{2,1,0:T(8,128)} %get-tuple-element.30.plain_ref, f32[8,32,384]{2,1,0:T(8,128)} %get-tuple-element.31.swapped_ref, bf16[384,256]{1,0:T(8,128)(2,1)} %pad_maximum_fusion.2.delays_ref), custom_call_target="tpu_custom_call" | custom-call | tf_op jit(solution)/shard_map/pallas_call | solution.py:119
  (12 shorter events, 0.1 us)
Async XLA Ops:
  6.5 11.7 %copy-start.1 = (s32[32]{0:T(128)S(1)}, s32[32]{0:T(128)}, u32[]{:S(2)}) copy-start(s32[32]{0:T(128)} %param.8) | copy-start | bytes 388
  6.5 61.2 %all-gather.3.cloned.1.call-start = ((), (), s32[]{:S(2)}) async-start(), calls=%async_computation | async-start | bytes 3551232 | tf_op jit(solution)/shard_map/all_gather | solution.py:154
  7.6 6.6 %collective-permute-start = (bf16[512,60]{1,0:T(8,128)(2,1)S(1)}, bf16[512,60]{1,0:T(8,128)(2,1)S(1)}, u32[]{:S(2)}, u32[]{:S(2)}) collective-permute-start(bf16[512,60]{1,0:T(8,128)(2,1)S(1)} %slice.40), channel_id=1, source_target_pairs={{0,1},{1,2},{2,3},{3,4},{4,5},{5,6},{6,7},{7,8},{8,9},{9,10},{10,1... | collective-permute-start | bytes 184328 | tf_op jit(solution)/shard_map/ppermute | solution.py:23
  14.1 8.4 %copy-start = (s32[512]{0:T(512)S(1)}, s32[512]{0:T(512)}, u32[]{:S(2)}) copy-start(s32[512]{0:T(512)} %param.7) | copy-start | bytes 6148
  15.5 4.0 %collective-permute-start.1 = (f32[256,384]{1,0:T(8,128)S(1)}, f32[256,384]{1,0:T(8,128)S(1)}, u32[]{:S(2)}, u32[]{:S(2)}) collective-permute-start(f32[256,384]{1,0:T(8,128)S(1)} %dynamic-slice_bitcast_fusion), channel_id=1, source_target_pairs={{0,1},{1,0},{2,3},{3,2},{4,5},{5,4},{6,7},{7,6},{8,9},{9,8},{10,11... | collective-permute-start | bytes 1179656 | tf_op jit(solution)/shard_map/ppermute | solution.py:149
Sparse Core Ops, SparseCore 0:
  21.0 46.7 all-gather.2

commit v7 on v6

--- a/solution.py
+++ b/solution.py
@@ -72,9 +72,18 @@
     return jnp.concatenate([real_part * factor, imag_part * factor], axis=1).astype(jnp.bfloat16)
 
 
-def correlate_kernel(flags_ref, source_ref, plain_ref, swapped_ref, delays_ref, out_ref, cross_ref):
+def correlate_kernel(flags_ref, source_ref, recv_ref, delays_ref, out_ref, plain_ref, swapped_ref, cross_ref):
     block = source_ref.shape[0]
-    receivers = plain_ref.shape[1]
+    receivers = recv_ref.shape[1]
+
+    @pl.when(pl.program_id(0) == 0)
+    def _():
+        lower = lax.broadcasted_iota(jnp.int32, (receivers, 2 * NF), 1) < NF
+        for w in range(SEGS):
+            spectra = recv_ref[w].astype(jnp.float32)
+            turned = pltpu.roll(spectra, NF, 1)
+            plain_ref[w] = jnp.where(lower, spectra, turned)
+            swapped_ref[w] = jnp.where(lower, turned, -spectra)
 
     def one_source(s, carry):
         source = source_ref[s].astype(jnp.float32)
@@ -99,28 +108,27 @@
 def correlate(chosen, source_flags, receivers, delays, block=32):
     source_count = chosen.shape[0]
     recv_count = receivers.shape[1]
-    spectra = receivers.astype(jnp.float32)
-    real_part = spectra[..., :NF]
-    imag_part = spectra[..., NF:]
-    plain = jnp.concatenate([real_part, real_part], axis=-1)
-    swapped = jnp.concatenate([imag_part, -imag_part], axis=-1)
     grid_spec = pltpu.PrefetchScalarGridSpec(
         num_scalar_prefetch=1,
         grid=(source_count // block,),
         in_specs=[
             pl.BlockSpec((block, SEGS, 2 * NF), lambda i, flags: (i, 0, 0)),
             pl.BlockSpec((SEGS, recv_count, 2 * NF), lambda i, flags: (0, 0, 0)),
-            pl.BlockSpec((SEGS, recv_count, 2 * NF), lambda i, flags: (0, 0, 0)),
             pl.BlockSpec((2 * NF, LAGS), lambda i, flags: (0, 0)),
         ],
         out_specs=pl.BlockSpec((block, recv_count, LAGS), lambda i, flags: (i, 0, 0)),
-        scratch_shapes=[pltpu.VMEM((block * recv_count, 2 * NF), jnp.bfloat16)],
+        scratch_shapes=[
+            pltpu.VMEM((SEGS, recv_count, 2 * NF), jnp.float32),
+            pltpu.VMEM((SEGS, recv_count, 2 * NF), jnp.float32),
+            pltpu.VMEM((block * recv_count, 2 * NF), jnp.bfloat16),
+        ],
     )
     return pl.pallas_call(
         correlate_kernel,
         grid_spec=grid_spec,
         out_shape=jax.ShapeDtypeStruct((source_count, recv_count, LAGS), jnp.bfloat16),
-    )(source_flags, chosen, plain, swapped, delays)
+        compiler_params=pltpu.CompilerParams(dimension_semantics=("arbitrary",)),
+    )(source_flags, chosen, receivers, delays)
 
 
 def body(recording, source_index, channel_mask):

time: 128 us -> 126 us (0.984)
  other arithmetic: 11 us -> 8.39 us
    concatenate x1 -> x0, other arithmetic: 2.27 us -> none  [correlate(): plain = jnp.concatenate([real_part, real_part], axis=-1)]
    mul x0 -> x1, other arithmetic: none -> 1.7 us  [body(): receivers = receivers * flags[None, :, None]]
  transfers between devices with their start and end apart: 3 -> 3, of which waited for: 2 -> 2; matrix products, arithmetic and copies ran while one was open for 4% -> 5% of each run, Pallas kernels for 0% -> 0%
where the time goes in v7:
time: 126 us; the launch traced here: 125 us
  waiting for transfers between devices  46.7 us (37%)
  Pallas kernels  38.4 us (30%)
  between operations  13.6 us (11%)
  local copies, waits for them, and re-layouts  9.88 us (8%)
  other arithmetic  8.39 us (7%)
  starting transfers between devices  5.09 us (4%)
  matrix products  3.19 us (3%)
    all_gather x1, waiting for transfers between devices, body(): gathered = lax.all_gather(piece, 'chan', axis=0, tiled=False)  45.3 us
    pallas_call x1, Pallas kernels, correlate(): pl.pallas_call(correlate_kernel, grid_spec=grid_spec, out_shape=jax.Shape...  38.4 us
    gather x1, local copies, waits for them, and re-layouts, body(): chosen = blocks[:, picked // span, picked % span].transpose(1, 0, 2)  5.6 us
    another operation x3, other arithmetic  3.3 us
    reshape x1, local copies, waits for them, and re-layouts, body(): blocks = gathered.reshape(SEGS, sharing, height, 2 * NF)  3.14 us
    ppermute x1, starting transfers between devices, body(): spectrum = spectrum + lax.ppermute(outgoing, 'chan', route)  2.68 us
  transfers between devices with their start and end apart: 3, of which 2 were waited for; matrix products, arithmetic and copies ran while one was open for 5% of the time, Pallas kernels for 0%

profile of v7, /device:TPU:0, one launch (start us, length us, event | category | flops | bytes accessed | tf_op | source)
XLA Modules:
  0.0 125.1 jit_solution(9962541190765801771)
XLA Ops:
  6.5 0.0 all-gather.3.cloned.1.call-start
  6.5 1.0 slice.34
  7.6 2.4 %collective-permute-start = (bf16[512,60]{1,0:T(8,128)(2,1)S(1)}, bf16[512,60]{1,0:T(8,128)(2,1)S(1)}, u32[]{:S(2)}, u32[]{:S(2)}) collective-permute-start(bf16[512,60]{1,0:T(8,128)(2,1)S(1)} %slice.34), channel_id=1, source_target_pairs={{0,1},{1,2},{2,3},{3,4},{4,5},{5,6},{6,7},{7,8},{8,9},{9,10},{10,1... | collective-permute-start | bytes 184328 | tf_op jit(solution)/shard_map/ppermute | solution.py:23
  10.0 1.9 %fusion.27 = f32[256,512]{1,0:T(8,128)S(1)} fusion(bf16[1024,256]{1,0:T(8,128)(2,1)} %constant.156, bf16[512,1024]{1,0:T(8,128)(2,1)} %param.6), kind=kOutput, calls=%fused_computation.67 | convolution fusion | flops 268435456 | bytes 2097152 | tf_op jit(solution)/shard_map/dot_general | solution.py:48
  11.9 2.2 %negate_convert_fusion = (bf16[512,192]{1,0:T(8,128)(2,1)S(1)}, bf16[512,192]{1,0:T(8,128)(2,1)S(1)}) fusion(s32[192]{0:T(256)S(1)} %iota_add_fusion.1), kind=kLoop, calls=%fused_computation.12 | loop fusion | flops 1671168 | bytes 393984 | tf_op jit(solution)/shard_map/convert.6
  14.1 0.0 copy-start
  14.1 0.0 collective-permute-done
  14.2 1.3 %fusion.1 = f32[512,384]{1,0:T(8,128)S(1)} fusion(f32[256,512]{1,0:T(8,128)S(1)} %fusion.27, bf16[60,256]{1,0:T(8,128)(2,1)} %constant.155, bf16[512,60]{1,0:T(8,128)(2,1)S(1)} %collective-permute-done, s32[]{:T(128)S(6)} %select_n.74, bf16[512,192]{1,0:T(8,128)(2,1)S(1)} %get-tuple-element.24, bf16[512,192]{1,0:T(8,128)(2,1)S(1)} %get-tuple-element.23), kind=kOutput, calls=%fused_computation.3 | convolution fusion | flops 117047296 | bytes 1796100 | tf_op jit(solution)/shard_map/dot_general | solution.py:147
  15.5 2.7 %collective-permute-start.1 = (f32[256,384]{1,0:T(8,128)S(1)}, f32[256,384]{1,0:T(8,128)S(1)}, u32[]{:S(2)}, u32[]{:S(2)}) collective-permute-start(f32[256,384]{1,0:T(8,128)S(1)} %dynamic-slice_bitcast_fusion), channel_id=1, source_target_pairs={{0,1},{1,0},{2,3},{3,2},{4,5},{5,4},{6,7},{7,6},{8,9},{9,8},{10,11... | collective-permute-start | bytes 1179656 | tf_op jit(solution)/shard_map/ppermute | solution.py:157
  18.2 1.3 %collective-permute-done.1 = f32[256,384]{1,0:T(8,128)S(1)} collective-permute-done((f32[256,384]{1,0:T(8,128)S(1)}, f32[256,384]{1,0:T(8,128)S(1)}, u32[]{:S(2)}, u32[]{:S(2)}) %collective-permute-start.1) | collective-permute-done | bytes 393248 | tf_op jit(solution)/shard_map/ppermute | solution.py:157
  19.6 0.2 fusion.25
  19.8 0.2 multiply_convert_fusion.1
  20.0 0.8 fusion.9
  20.8 0.0 all-gather.3.cloned.1.call-update
  20.9 0.9 cosine_convert_fusion.1
  21.8 0.7 pad_maximum_fusion.delays_ref
  22.5 45.3 %all-gather.3.cloned.1.call-done = bf16[4352,384]{1,0:T(8,128)(2,1)} async-done(((bf16[272,384]{1,0:T(8,128)(2,1)}), bf16[4352,384]{1,0:T(8,128)(2,1)}) %all-gather.3.cloned.1.call-update) | async-done | bytes 3342352 | tf_op jit(solution)/shard_map/all_gather | solution.py:162
  67.8 0.8 fusion.15
  68.6 0.1 reshape.71
  68.6 3.1 %copy.6 = bf16[8,2,272,384]{3,0,2,1:T(8,128)(2,1)S(1)} copy(bf16[8,2,272,384]{3,2,1,0:T(8,128)(2,1)} %bitcast.16) | data formatting | bytes 6684672 | tf_op jit(solution)/shard_map/reshape | solution.py:164
  71.8 0.8 select_reduce_fusion.flags_ref
  72.6 5.6 %gather_fusion = bf16[512,8,384]{2,1,0:T(8,128)(2,1)} fusion(bf16[8,2,272,384]{3,0,2,1:T(8,128)(2,1)S(1)} %copy.6, s32[512]{0:T(512)S(1)} %get-tuple-element.21), kind=kCustom, calls=%fused_computation | custom fusion | bytes 6295552 | tf_op jit(solution)/shard_map/gather | solution.py:166
  78.2 1.7 %bitcast_multiply_fusion.recv_ref = bf16[8,32,384]{2,1,0:T(8,128)(2,1)} fusion(bf16[8,2,272,384]{3,2,1,0:T(8,128)(2,1)} %bitcast.17, s32[]{:T(128)S(6)} %select_n.84, s32[]{:T(128)S(6)} %select_n.86, bf16[32]{0:T(256)(128)(2,1)S(1)} %get-tuple-element.25), kind=kLoop, calls=%fused_computation.38 | loop fusion | flops 393216 | bytes 393288 | tf_op jit(solution)/shard_map/mul | solution.py:174
  79.9 38.4 %shard_map.46 = bf16[512,32,256]{2,1,0:T(8,128)(2,1)} custom-call(s32[512]{0:T(512)} %select_reduce_fusion.flags_ref, bf16[512,8,384]{2,1,0:T(8,128)(2,1)} %gather_fusion, bf16[8,32,384]{2,1,0:T(8,128)(2,1)} %bitcast_multiply_fusion.recv_ref, bf16[384,256]{1,0:T(8,128)(2,1)} %pad_maximum_fusion.delays_ref), custom_call_target="tpu_custom_call" | custom-call | tf_op jit(solution)/shard_map/pallas_call | solution.py:126
  (10 shorter events, 0.1 us)
Async XLA Ops:
  6.5 11.7 %copy-start.1 = (s32[32]{0:T(128)S(1)}, s32[32]{0:T(128)}, u32[]{:S(2)}) copy-start(s32[32]{0:T(128)} %param.8) | copy-start | bytes 388
  6.5 61.2 %all-gather.3.cloned.1.call-start = ((), (), s32[]{:S(2)}) async-start(), calls=%async_computation | async-start | bytes 3551232 | tf_op jit(solution)/shard_map/all_gather | solution.py:162
  7.6 6.6 %collective-permute-start = (bf16[512,60]{1,0:T(8,128)(2,1)S(1)}, bf16[512,60]{1,0:T(8,128)(2,1)S(1)}, u32[]{:S(2)}, u32[]{:S(2)}) collective-permute-start(bf16[512,60]{1,0:T(8,128)(2,1)S(1)} %slice.34), channel_id=1, source_target_pairs={{0,1},{1,2},{2,3},{3,4},{4,5},{5,6},{6,7},{7,8},{8,9},{9,10},{10,1... | collective-permute-start | bytes 184328 | tf_op jit(solution)/shard_map/ppermute | solution.py:23
  14.1 8.3 %copy-start = (s32[512]{0:T(512)S(1)}, s32[512]{0:T(512)}, u32[]{:S(2)}) copy-start(s32[512]{0:T(512)} %param.7) | copy-start | bytes 6148
  15.5 4.0 %collective-permute-start.1 = (f32[256,384]{1,0:T(8,128)S(1)}, f32[256,384]{1,0:T(8,128)S(1)}, u32[]{:S(2)}, u32[]{:S(2)}) collective-permute-start(f32[256,384]{1,0:T(8,128)S(1)} %dynamic-slice_bitcast_fusion), channel_id=1, source_target_pairs={{0,1},{1,0},{2,3},{3,2},{4,5},{5,4},{6,7},{7,6},{8,9},{9,8},{10,11... | collective-permute-start | bytes 1179656 | tf_op jit(solution)/shard_map/ppermute | solution.py:157
Sparse Core Ops, SparseCore 0:
  21.0 46.7 all-gather.2

commit v8 on v7

--- a/solution.py
+++ b/solution.py
@@ -50,17 +50,23 @@
 
 
 def fourier_table():
-    sample = jnp.arange(NSEG, dtype=jnp.int32)[:, None]
-    frequency = FBASE + jnp.arange(NF, dtype=jnp.int32)[None, :]
-    angles = 2.0 * math.pi * (sample * frequency % NSEG).astype(jnp.float32) / NSEG
-    return jnp.concatenate([jnp.cos(angles), -jnp.sin(angles)], axis=1).astype(jnp.bfloat16)
+    with jax.ensure_compile_time_eval():
+        sample = jnp.arange(NSEG, dtype=jnp.int32)[:, None]
+        frequency = FBASE + jnp.arange(NF, dtype=jnp.int32)[None, :]
+        angles = 2.0 * math.pi * (sample * frequency % NSEG).astype(jnp.float32) / NSEG
+        table = jnp.concatenate([jnp.cos(angles), -jnp.sin(angles)], axis=1)
+        table = np.asarray(table.astype(jnp.bfloat16).astype(jnp.float32))
+    return jnp.asarray(table).astype(jnp.bfloat16)
 
 
 def delay_table():
-    frequency = FBASE + jnp.arange(NF, dtype=jnp.int32)[:, None]
-    delays = jnp.arange(LAGS, dtype=jnp.int32)[None, :] - LAGS // 2
-    angles = 2.0 * math.pi * (frequency * delays % NSEG).astype(jnp.float32) / NSEG
-    return jnp.concatenate([jnp.cos(angles), -jnp.sin(angles)], axis=0).astype(jnp.bfloat16)
+    with jax.ensure_compile_time_eval():
+        frequency = FBASE + jnp.arange(NF, dtype=jnp.int32)[:, None]
+        delays = jnp.arange(LAGS, dtype=jnp.int32)[None, :] - LAGS // 2
+        angles = 2.0 * math.pi * (frequency * delays % NSEG).astype(jnp.float32) / NSEG
+        table = jnp.concatenate([jnp.cos(angles), -jnp.sin(angles)], axis=0)
+        table = np.asarray(table.astype(jnp.bfloat16).astype(jnp.float32))
+    return jnp.asarray(table).astype(jnp.bfloat16)
 
 
 def whiten(spectrum):

time: 126 us -> 126 us (level)
  other arithmetic: 8.39 us -> 4.59 us
  waiting for transfers between devices: 46.7 us -> 50.3 us
    all_gather x1, waiting for transfers between devices: 45.3 us -> 49 us  [body(): gathered = lax.all_gather(piece, 'chan', axis=0, tiled=False)]
    another operation x3 -> x1, other arithmetic: 3.3 us -> 0.19 us
  transfers between devices with their start and end apart: 3 -> 3, of which waited for: 2 -> 2; matrix products, arithmetic and copies ran while one was open for 5% -> 2% of each run, Pallas kernels for 0% -> 0%
where the time goes in v8:
time: 126 us; the launch traced here: 125 us
  waiting for transfers between devices  50.3 us (40%)
  Pallas kernels  38.4 us (30%)
  between operations  13.5 us (11%)
  local copies, waits for them, and re-layouts  9.87 us (8%)
  starting transfers between devices  5.09 us (4%)
  other arithmetic  4.59 us (4%)
  matrix products  3.38 us (3%)
    all_gather x1, waiting for transfers between devices, body(): gathered = lax.all_gather(piece, 'chan', axis=0, tiled=False)  49 us
    pallas_call x1, Pallas kernels, correlate(): pl.pallas_call(correlate_kernel, grid_spec=grid_spec, out_shape=jax.Shape...  38.4 us
    gather x1, local copies, waits for them, and re-layouts, body(): chosen = blocks[:, picked // span, picked % span].transpose(1, 0, 2)  5.59 us
    reshape x1, local copies, waits for them, and re-layouts, body(): blocks = gathered.reshape(SEGS, sharing, height, 2 * NF)  3.14 us
    ppermute x1, starting transfers between devices, body(): spectrum = spectrum + lax.ppermute(outgoing, 'chan', route)  2.68 us
  transfers between devices with their start and end apart: 3, of which 2 were waited for; matrix products, arithmetic and copies ran while one was open for 2% of the time, Pallas kernels for 0%

profile of v8, /device:TPU:0, one launch (start us, length us, event | category | flops | bytes accessed | tf_op | source)
XLA Modules:
  0.0 125.2 jit_solution(7080638100684310348)
XLA Ops:
  6.5 0.0 copy-start.1
  6.5 0.0 all-gather.3.cloned.1.call-start
  6.5 1.0 slice.34
  7.6 2.4 %collective-permute-start = (bf16[512,60]{1,0:T(8,128)(2,1)S(1)}, bf16[512,60]{1,0:T(8,128)(2,1)S(1)}, u32[]{:S(2)}, u32[]{:S(2)}) collective-permute-start(bf16[512,60]{1,0:T(8,128)(2,1)S(1)} %slice.34), channel_id=1, source_target_pairs={{0,1},{1,2},{2,3},{3,4},{4,5},{5,6},{6,7},{7,8},{8,9},{9,10},{10,1... | collective-permute-start | bytes 184328 | tf_op jit(solution)/shard_map/ppermute | solution.py:23
  10.0 1.9 %fusion.16 = f32[256,512]{1,0:T(8,128)S(1)} fusion(bf16[1024,256]{1,0:T(8,128)(2,1)} %constant.128, bf16[512,1024]{1,0:T(8,128)(2,1)} %param.8), kind=kOutput, calls=%fused_computation.40 | convolution fusion | flops 268435456 | bytes 2097152 | tf_op jit(solution)/shard_map/dot_general | solution.py:48
  11.9 0.0 copy-start
  11.9 0.0 collective-permute-done
  11.9 1.5 %fusion.1 = f32[512,384]{1,0:T(8,128)S(1)} fusion(f32[256,512]{1,0:T(8,128)S(1)} %fusion.16, bf16[60,256]{1,0:T(8,128)(2,1)} %constant.127, bf16[512,60]{1,0:T(8,128)(2,1)S(1)} %collective-permute-done, bf16[512,384]{1,0:T(8,128)(2,1)} %constant.129, s32[]{:T(128)S(6)} %select_n.57), kind=kOutput, calls=%fused_computation.3 | convolution fusion | flops 116654080 | bytes 1601540 | tf_op jit(solution)/shard_map/dot_general | solution.py:153
  13.5 2.7 %collective-permute-start.1 = (f32[256,384]{1,0:T(8,128)S(1)}, f32[256,384]{1,0:T(8,128)S(1)}, u32[]{:S(2)}, u32[]{:S(2)}) collective-permute-start(f32[256,384]{1,0:T(8,128)S(1)} %dynamic-slice_bitcast_fusion), channel_id=1, source_target_pairs={{0,1},{1,0},{2,3},{3,2},{4,5},{5,4},{6,7},{7,6},{8,9},{9,8},{10,11... | collective-permute-start | bytes 1179656 | tf_op jit(solution)/shard_map/ppermute | solution.py:163
  16.1 0.0 copy-done.1
  16.1 1.3 %collective-permute-done.1 = f32[256,384]{1,0:T(8,128)S(1)} collective-permute-done((f32[256,384]{1,0:T(8,128)S(1)}, f32[256,384]{1,0:T(8,128)S(1)}, u32[]{:S(2)}, u32[]{:S(2)}) %collective-permute-start.1) | collective-permute-done | bytes 393248 | tf_op jit(solution)/shard_map/ppermute | solution.py:163
  17.5 0.2 fusion.14
  17.8 0.2 multiply_convert_fusion.1
  18.0 0.8 fusion.3
  18.7 0.0 all-gather.3.cloned.1.call-update
  18.8 0.0 copy-done
  18.8 49.0 %all-gather.3.cloned.1.call-done = bf16[4352,384]{1,0:T(8,128)(2,1)} async-done(((bf16[272,384]{1,0:T(8,128)(2,1)}), bf16[4352,384]{1,0:T(8,128)(2,1)}) %all-gather.3.cloned.1.call-update) | async-done | bytes 3342352 | tf_op jit(solution)/shard_map/all_gather | solution.py:168
  67.8 0.8 fusion.5
  68.6 0.1 reshape.56
  68.7 3.1 %copy.8 = bf16[8,2,272,384]{3,0,2,1:T(8,128)(2,1)S(1)} copy(bf16[8,2,272,384]{3,2,1,0:T(8,128)(2,1)} %bitcast.16) | data formatting | bytes 6684672 | tf_op jit(solution)/shard_map/reshape | solution.py:170
  71.8 0.8 select_reduce_fusion.flags_ref
  72.7 5.6 %gather_fusion = bf16[512,8,384]{2,1,0:T(8,128)(2,1)} fusion(bf16[8,2,272,384]{3,0,2,1:T(8,128)(2,1)S(1)} %copy.8, s32[512]{0:T(512)S(1)} %get-tuple-element.19), kind=kCustom, calls=%fused_computation | custom fusion | bytes 6295552 | tf_op jit(solution)/shard_map/gather | solution.py:172
  78.2 1.7 %bitcast_multiply_fusion.recv_ref = bf16[8,32,384]{2,1,0:T(8,128)(2,1)} fusion(bf16[8,2,272,384]{3,2,1,0:T(8,128)(2,1)} %bitcast.17, s32[]{:T(128)S(6)} %select_n.67, s32[]{:T(128)S(6)} %select_n.69, bf16[32]{0:T(256)(128)(2,1)S(1)} %get-tuple-element.21), kind=kLoop, calls=%fused_computation.15 | loop fusion | flops 393216 | bytes 393288 | tf_op jit(solution)/shard_map/mul | solution.py:180
  80.0 38.4 %shard_map.64 = bf16[512,32,256]{2,1,0:T(8,128)(2,1)} custom-call(s32[512]{0:T(512)} %select_reduce_fusion.flags_ref, bf16[512,8,384]{2,1,0:T(8,128)(2,1)} %gather_fusion, bf16[8,32,384]{2,1,0:T(8,128)(2,1)} %bitcast_multiply_fusion.recv_ref, bf16[384,256]{1,0:T(8,128)(2,1)} %constant.130.delays_ref), custom_call_target="tpu_custom_call" | custom-call | tf_op jit(solution)/shard_map/pallas_call | solution.py:132
  (5 shorter events, 0.1 us)
Async XLA Ops:
  6.5 9.6 %copy-start.1 = (s32[32]{0:T(128)S(1)}, s32[32]{0:T(128)}, u32[]{:S(2)}) copy-start(s32[32]{0:T(128)} %param.10) | copy-start | bytes 388
  6.5 61.3 %all-gather.3.cloned.1.call-start = ((), (), s32[]{:S(2)}) async-start(), calls=%async_computation | async-start | bytes 3551232 | tf_op jit(solution)/shard_map/all_gather | solution.py:168
  7.6 4.3 %collective-permute-start = (bf16[512,60]{1,0:T(8,128)(2,1)S(1)}, bf16[512,60]{1,0:T(8,128)(2,1)S(1)}, u32[]{:S(2)}, u32[]{:S(2)}) collective-permute-start(bf16[512,60]{1,0:T(8,128)(2,1)S(1)} %slice.34), channel_id=1, source_target_pairs={{0,1},{1,2},{2,3},{3,4},{4,5},{5,6},{6,7},{7,8},{8,9},{9,10},{10,1... | collective-permute-start | bytes 184328 | tf_op jit(solution)/shard_map/ppermute | solution.py:23
  11.9 7.0 %copy-start = (s32[512]{0:T(512)S(1)}, s32[512]{0:T(512)}, u32[]{:S(2)}) copy-start(s32[512]{0:T(512)} %param.9) | copy-start | bytes 6148
  13.5 4.0 %collective-permute-start.1 = (f32[256,384]{1,0:T(8,128)S(1)}, f32[256,384]{1,0:T(8,128)S(1)}, u32[]{:S(2)}, u32[]{:S(2)}) collective-permute-start(f32[256,384]{1,0:T(8,128)S(1)} %dynamic-slice_bitcast_fusion), channel_id=1, source_target_pairs={{0,1},{1,0},{2,3},{3,2},{4,5},{5,4},{6,7},{7,6},{8,9},{9,8},{10,11... | collective-permute-start | bytes 1179656 | tf_op jit(solution)/shard_map/ppermute | solution.py:163
Sparse Core Ops, SparseCore 0:
  18.9 48.8 all-gather.2

commit v9 on v8

--- a/solution.py
+++ b/solution.py
@@ -78,9 +78,10 @@
     return jnp.concatenate([real_part * factor, imag_part * factor], axis=1).astype(jnp.bfloat16)
 
 
-def correlate_kernel(flags_ref, source_ref, recv_ref, delays_ref, out_ref, plain_ref, swapped_ref, cross_ref):
+def correlate_kernel(flags_ref, source_ref, recv_ref, delays_ref, out_ref, plain_ref, swapped_ref, *cross_refs):
     block = source_ref.shape[0]
     receivers = recv_ref.shape[1]
+    share = block // len(cross_refs)
 
     @pl.when(pl.program_id(0) == 0)
     def _():
@@ -91,27 +92,32 @@
             plain_ref[w] = jnp.where(lower, spectra, turned)
             swapped_ref[w] = jnp.where(lower, turned, -spectra)
 
-    def one_source(s, carry):
-        source = source_ref[s].astype(jnp.float32)
-        direct = jnp.zeros((receivers, 2 * NF), jnp.float32)
-        crossed = jnp.zeros((receivers, 2 * NF), jnp.float32)
-        for w in range(SEGS):
-            row = source[w : w + 1, :]
-            direct = direct + row * plain_ref[w]
-            crossed = crossed + row * swapped_ref[w]
-        flag = flags_ref[pl.program_id(0) * block + s].astype(jnp.float32)
-        cross = (direct - pltpu.roll(crossed, NF, 1)) * flag
-        start = pl.multiple_of(s * receivers, receivers)
-        cross_ref[pl.ds(start, receivers), :] = cross.astype(jnp.bfloat16)
-        return carry
+    for part, cross_ref in enumerate(cross_refs):
 
-    lax.fori_loop(0, block, one_source, 0, unroll=True)
-    lagged = jnp.dot(cross_ref[...], delays_ref[...], preferred_element_type=jnp.float32)
-    lagged = lagged * (1.0 / math.sqrt(SEGS * NF))
-    out_ref[...] = lagged.astype(jnp.bfloat16).reshape(out_ref.shape)
+        def one_source(s, carry):
+            at = part * share + s
+            source = source_ref[at].astype(jnp.float32)
+            direct = jnp.zeros((receivers, 2 * NF), jnp.float32)
+            crossed = jnp.zeros((receivers, 2 * NF), jnp.float32)
+            for w in range(SEGS):
+                row = source[w : w + 1, :]
+                direct = direct + row * plain_ref[w]
+                crossed = crossed + row * swapped_ref[w]
+            flag = flags_ref[pl.program_id(0) * block + at].astype(jnp.float32)
+            cross = (direct - pltpu.roll(crossed, NF, 1)) * flag
+            start = pl.multiple_of(s * receivers, receivers)
+            cross_ref[pl.ds(start, receivers), :] = cross.astype(jnp.bfloat16)
+            return carry
+
+        lax.fori_loop(0, share, one_source, 0, unroll=True)
+        lagged = jnp.dot(cross_ref[...], delays_ref[...], preferred_element_type=jnp.float32)
+        lagged = lagged * (1.0 / math.sqrt(SEGS * NF))
+        out_ref[part * share : (part + 1) * share] = lagged.astype(jnp.bfloat16).reshape(
+            share, receivers, LAGS
+        )
 
 
-def correlate(chosen, source_flags, receivers, delays, block=32):
+def correlate(chosen, source_flags, receivers, delays, block=64, parts=2):
     source_count = chosen.shape[0]
     recv_count = receivers.shape[1]
     grid_spec = pltpu.PrefetchScalarGridSpec(
@@ -126,8 +132,8 @@
         scratch_shapes=[
             pltpu.VMEM((SEGS, recv_count, 2 * NF), jnp.float32),
             pltpu.VMEM((SEGS, recv_count, 2 * NF), jnp.float32),
-            pltpu.VMEM((block * recv_count, 2 * NF), jnp.bfloat16),
-        ],
+        ]
+        + [pltpu.VMEM((block // parts * recv_count, 2 * NF), jnp.bfloat16)] * parts,
     )
     return pl.pallas_call(
         correlate_kernel,

time: 126 us -> 125 us (level)
  no operation moved by 1% of the time
where the time goes in v9:
time: 125 us
  waiting for transfers between devices  50.3 us (40%)
  Pallas kernels  37.7 us (30%)
  between operations  13.5 us (11%)
  local copies, waits for them, and re-layouts  9.86 us (8%)
  starting transfers between devices  5.09 us (4%)
  other arithmetic  4.59 us (4%)
  matrix products  3.38 us (3%)
    all_gather x1, waiting for transfers between devices, body(): gathered = lax.all_gather(piece, 'chan', axis=0, tiled=False)  49 us
    pallas_call x1, Pallas kernels, correlate(): pl.pallas_call(correlate_kernel, grid_spec=grid_spec, out_shape=jax.Shape...  37.7 us
    gather x1, local copies, waits for them, and re-layouts, body(): chosen = blocks[:, picked // span, picked % span].transpose(1, 0, 2)  5.59 us
    reshape x1, local copies, waits for them, and re-layouts, body(): blocks = gathered.reshape(SEGS, sharing, height, 2 * NF)  3.14 us
    ppermute x1, starting transfers between devices, body(): spectrum = spectrum + lax.ppermute(outgoing, 'chan', route)  2.68 us
  transfers between devices with their start and end apart: 3, of which 2 were waited for; matrix products, arithmetic and copies ran while one was open for 2% of the time, Pallas kernels for 0%

profile of v9, /device:TPU:0, one launch (start us, length us, event | category | flops | bytes accessed | tf_op | source)
XLA Modules:
  0.0 124.5 jit_solution(10917252201493210220)
XLA Ops:
  6.5 0.0 copy-start.1
  6.5 0.0 all-gather.3.cloned.1.call-start
  6.5 1.0 slice.34
  7.6 2.4 %collective-permute-start = (bf16[512,60]{1,0:T(8,128)(2,1)S(1)}, bf16[512,60]{1,0:T(8,128)(2,1)S(1)}, u32[]{:S(2)}, u32[]{:S(2)}) collective-permute-start(bf16[512,60]{1,0:T(8,128)(2,1)S(1)} %slice.34), channel_id=1, source_target_pairs={{0,1},{1,2},{2,3},{3,4},{4,5},{5,6},{6,7},{7,8},{8,9},{9,10},{10,1... | collective-permute-start | bytes 184328 | tf_op jit(solution)/shard_map/ppermute | solution.py:23
  10.0 1.9 %fusion.16 = f32[256,512]{1,0:T(8,128)S(1)} fusion(bf16[1024,256]{1,0:T(8,128)(2,1)} %constant.128, bf16[512,1024]{1,0:T(8,128)(2,1)} %param.8), kind=kOutput, calls=%fused_computation.40 | convolution fusion | flops 268435456 | bytes 2097152 | tf_op jit(solution)/shard_map/dot_general | solution.py:48
  11.9 0.0 copy-start
  11.9 0.0 collective-permute-done
  11.9 1.5 %fusion.1 = f32[512,384]{1,0:T(8,128)S(1)} fusion(f32[256,512]{1,0:T(8,128)S(1)} %fusion.16, bf16[60,256]{1,0:T(8,128)(2,1)} %constant.127, bf16[512,60]{1,0:T(8,128)(2,1)S(1)} %collective-permute-done, bf16[512,384]{1,0:T(8,128)(2,1)} %constant.129, s32[]{:T(128)S(6)} %select_n.57), kind=kOutput, calls=%fused_computation.3 | convolution fusion | flops 116654080 | bytes 1601540 | tf_op jit(solution)/shard_map/dot_general | solution.py:159
  13.5 2.7 %collective-permute-start.1 = (f32[256,384]{1,0:T(8,128)S(1)}, f32[256,384]{1,0:T(8,128)S(1)}, u32[]{:S(2)}, u32[]{:S(2)}) collective-permute-start(f32[256,384]{1,0:T(8,128)S(1)} %dynamic-slice_bitcast_fusion), channel_id=1, source_target_pairs={{0,1},{1,0},{2,3},{3,2},{4,5},{5,4},{6,7},{7,6},{8,9},{9,8},{10,11... | collective-permute-start | bytes 1179656 | tf_op jit(solution)/shard_map/ppermute | solution.py:169
  16.1 0.0 copy-done.1
  16.1 1.3 %collective-permute-done.1 = f32[256,384]{1,0:T(8,128)S(1)} collective-permute-done((f32[256,384]{1,0:T(8,128)S(1)}, f32[256,384]{1,0:T(8,128)S(1)}, u32[]{:S(2)}, u32[]{:S(2)}) %collective-permute-start.1) | collective-permute-done | bytes 393248 | tf_op jit(solution)/shard_map/ppermute | solution.py:169
  17.5 0.2 fusion.14
  17.8 0.2 multiply_convert_fusion.1
  18.0 0.8 fusion.3
  18.7 0.0 all-gather.3.cloned.1.call-update
  18.8 0.0 copy-done
  18.8 49.0 %all-gather.3.cloned.1.call-done = bf16[4352,384]{1,0:T(8,128)(2,1)} async-done(((bf16[272,384]{1,0:T(8,128)(2,1)}), bf16[4352,384]{1,0:T(8,128)(2,1)}) %all-gather.3.cloned.1.call-update) | async-done | bytes 3342352 | tf_op jit(solution)/shard_map/all_gather | solution.py:174
  67.8 0.8 fusion.5
  68.6 0.1 reshape.56
  68.7 3.1 %copy.8 = bf16[8,2,272,384]{3,0,2,1:T(8,128)(2,1)S(1)} copy(bf16[8,2,272,384]{3,2,1,0:T(8,128)(2,1)} %bitcast.16) | data formatting | bytes 6684672 | tf_op jit(solution)/shard_map/reshape | solution.py:176
  71.8 0.8 select_reduce_fusion.flags_ref
  72.7 5.6 %gather_fusion = bf16[512,8,384]{2,1,0:T(8,128)(2,1)} fusion(bf16[8,2,272,384]{3,0,2,1:T(8,128)(2,1)S(1)} %copy.8, s32[512]{0:T(512)S(1)} %get-tuple-element.19), kind=kCustom, calls=%fused_computation | custom fusion | bytes 6295552 | tf_op jit(solution)/shard_map/gather | solution.py:178
  78.2 1.7 %bitcast_multiply_fusion.recv_ref = bf16[8,32,384]{2,1,0:T(8,128)(2,1)} fusion(bf16[8,2,272,384]{3,2,1,0:T(8,128)(2,1)} %bitcast.17, s32[]{:T(128)S(6)} %select_n.67, s32[]{:T(128)S(6)} %select_n.69, bf16[32]{0:T(256)(128)(2,1)S(1)} %get-tuple-element.21), kind=kLoop, calls=%fused_computation.15 | loop fusion | flops 393216 | bytes 393288 | tf_op jit(solution)/shard_map/mul | solution.py:186
  79.9 37.7 %shard_map.64 = bf16[512,32,256]{2,1,0:T(8,128)(2,1)} custom-call(s32[512]{0:T(512)} %select_reduce_fusion.flags_ref, bf16[512,8,384]{2,1,0:T(8,128)(2,1)} %gather_fusion, bf16[8,32,384]{2,1,0:T(8,128)(2,1)} %bitcast_multiply_fusion.recv_ref, bf16[384,256]{1,0:T(8,128)(2,1)} %constant.130.delays_ref), custom_call_target="tpu_custom_call" | custom-call | tf_op jit(solution)/shard_map/pallas_call | solution.py:138
  (5 shorter events, 0.1 us)
Async XLA Ops:
  6.5 9.6 %copy-start.1 = (s32[32]{0:T(128)S(1)}, s32[32]{0:T(128)}, u32[]{:S(2)}) copy-start(s32[32]{0:T(128)} %param.10) | copy-start | bytes 388
  6.5 61.3 %all-gather.3.cloned.1.call-start = ((), (), s32[]{:S(2)}) async-start(), calls=%async_computation | async-start | bytes 3551232 | tf_op jit(solution)/shard_map/all_gather | solution.py:174
  7.6 4.3 %collective-permute-start = (bf16[512,60]{1,0:T(8,128)(2,1)S(1)}, bf16[512,60]{1,0:T(8,128)(2,1)S(1)}, u32[]{:S(2)}, u32[]{:S(2)}) collective-permute-start(bf16[512,60]{1,0:T(8,128)(2,1)S(1)} %slice.34), channel_id=1, source_target_pairs={{0,1},{1,2},{2,3},{3,4},{4,5},{5,6},{6,7},{7,8},{8,9},{9,10},{10,1... | collective-permute-start | bytes 184328 | tf_op jit(solution)/shard_map/ppermute | solution.py:23
  11.9 7.0 %copy-start = (s32[512]{0:T(512)S(1)}, s32[512]{0:T(512)}, u32[]{:S(2)}) copy-start(s32[512]{0:T(512)} %param.9) | copy-start | bytes 6148
  13.5 4.0 %collective-permute-start.1 = (f32[256,384]{1,0:T(8,128)S(1)}, f32[256,384]{1,0:T(8,128)S(1)}, u32[]{:S(2)}, u32[]{:S(2)}) collective-permute-start(f32[256,384]{1,0:T(8,128)S(1)} %dynamic-slice_bitcast_fusion), channel_id=1, source_target_pairs={{0,1},{1,0},{2,3},{3,2},{4,5},{5,4},{6,7},{7,6},{8,9},{9,8},{10,11... | collective-permute-start | bytes 1179656 | tf_op jit(solution)/shard_map/ppermute | solution.py:169
Sparse Core Ops, SparseCore 0:
  18.9 48.8 all-gather.2

commit v10 on v9

--- a/solution.py
+++ b/solution.py
@@ -78,16 +78,20 @@
     return jnp.concatenate([real_part * factor, imag_part * factor], axis=1).astype(jnp.bfloat16)
 
 
-def correlate_kernel(flags_ref, source_ref, recv_ref, delays_ref, out_ref, plain_ref, swapped_ref, *cross_refs):
+def correlate_kernel(
+    flags_ref, picked_ref, place_ref, source_ref, recv_ref, own_ref, delays_ref, out_ref,
+    plain_ref, swapped_ref, *cross_refs,
+):
     block = source_ref.shape[0]
-    receivers = recv_ref.shape[1]
+    receivers = recv_ref.shape[2]
     share = block // len(cross_refs)
 
     @pl.when(pl.program_id(0) == 0)
     def _():
         lower = lax.broadcasted_iota(jnp.int32, (receivers, 2 * NF), 1) < NF
+        own = own_ref[...]
         for w in range(SEGS):
-            spectra = recv_ref[w].astype(jnp.float32)
+            spectra = recv_ref[w, 0].astype(jnp.float32) * own
             turned = pltpu.roll(spectra, NF, 1)
             plain_ref[w] = jnp.where(lower, spectra, turned)
             swapped_ref[w] = jnp.where(lower, turned, -spectra)
@@ -103,7 +107,7 @@
                 row = source[w : w + 1, :]
                 direct = direct + row * plain_ref[w]
                 crossed = crossed + row * swapped_ref[w]
-            flag = flags_ref[pl.program_id(0) * block + at].astype(jnp.float32)
+            flag = flags_ref[picked_ref[pl.program_id(0) * block + at]].astype(jnp.float32)
             cross = (direct - pltpu.roll(crossed, NF, 1)) * flag
             start = pl.multiple_of(s * receivers, receivers)
             cross_ref[pl.ds(start, receivers), :] = cross.astype(jnp.bfloat16)
@@ -117,18 +121,19 @@
         )
 
 
-def correlate(chosen, source_flags, receivers, delays, block=64, parts=2):
+def correlate(chosen, flags_all, picked, place, blocks, own_flags, delays, block=64, parts=2):
     source_count = chosen.shape[0]
-    recv_count = receivers.shape[1]
+    recv_count = own_flags.shape[0]
     grid_spec = pltpu.PrefetchScalarGridSpec(
-        num_scalar_prefetch=1,
+        num_scalar_prefetch=3,
         grid=(source_count // block,),
         in_specs=[
-            pl.BlockSpec((block, SEGS, 2 * NF), lambda i, flags: (i, 0, 0)),
-            pl.BlockSpec((SEGS, recv_count, 2 * NF), lambda i, flags: (0, 0, 0)),
-            pl.BlockSpec((2 * NF, LAGS), lambda i, flags: (0, 0)),
+            pl.BlockSpec((block, SEGS, 2 * NF), lambda i, f, p, q: (i, 0, 0)),
+            pl.BlockSpec((SEGS, 1, recv_count, 2 * NF), lambda i, f, p, q: (0, q[0], q[1], 0)),
+            pl.BlockSpec((recv_count, 1), lambda i, f, p, q: (0, 0)),
+            pl.BlockSpec((2 * NF, LAGS), lambda i, f, p, q: (0, 0)),
         ],
-        out_specs=pl.BlockSpec((block, recv_count, LAGS), lambda i, flags: (i, 0, 0)),
+        out_specs=pl.BlockSpec((block, recv_count, LAGS), lambda i, f, p, q: (i, 0, 0)),
         scratch_shapes=[
             pltpu.VMEM((SEGS, recv_count, 2 * NF), jnp.float32),
             pltpu.VMEM((SEGS, recv_count, 2 * NF), jnp.float32),
@@ -140,7 +145,7 @@
         grid_spec=grid_spec,
         out_shape=jax.ShapeDtypeStruct((source_count, recv_count, LAGS), jnp.bfloat16),
         compiler_params=pltpu.CompilerParams(dimension_semantics=("arbitrary",)),
-    )(source_flags, chosen, receivers, delays)
+    )(flags_all, picked, place, chosen, blocks, own_flags, delays)
 
 
 def body(recording, source_index, channel_mask):
@@ -177,14 +182,10 @@
     picked = jnp.clip(source_index, 0, channels - 1)
     chosen = blocks[:, picked // span, picked % span].transpose(1, 0, 2)
     flags_all = gathered[:, span, :per_device].reshape(channels).astype(jnp.int32)
-    hits = picked[:, None] == jnp.arange(channels, dtype=jnp.int32)[None, :]
-    source_flags = jnp.sum(jnp.where(hits, flags_all[None, :], 0), axis=1)
     first = me * per_device
-    receivers = lax.dynamic_slice(
-        blocks, (0, first // span, first % span, 0), (SEGS, 1, per_device, 2 * NF)
-    ).reshape(SEGS, per_device, 2 * NF)
-    receivers = receivers * flags[None, :, None]
-    result = correlate(chosen, source_flags, receivers, delay_table())
+    place = jnp.stack([first // span, first % span // per_device]).astype(jnp.int32)
+    own_flags = channel_mask.astype(jnp.float32)[:, None]
+    result = correlate(chosen, flags_all, picked, place, blocks, own_flags, delay_table())
     return result.reshape(SOURCES, per_device, LAGS)
 
 

time: 125 us -> 123 us (0.984)
  waiting for transfers between devices: 50.3 us -> 48.5 us
  other arithmetic: 4.59 us -> 3.18 us
  local copies, waits for them, and re-layouts: 9.86 us -> 11.2 us
    all_gather x1, waiting for transfers between devices: 49 us -> 47.2 us  [body(): gathered = lax.all_gather(piece, 'chan', axis=0, tiled=False)]
    mul x1 -> x0, other arithmetic: 1.7 us -> none  [body(): receivers = receivers * flags[None, :, None]]
  transfers between devices with their start and end apart: 3 -> 3, of which waited for: 2 -> 2; matrix products, arithmetic and copies ran while one was open for 2% -> 3% of each run, Pallas kernels for 0% -> 0%
where the time goes in v10:
time: 123 us
  waiting for transfers between devices  48.5 us (39%)
  Pallas kernels  38.1 us (31%)
  between operations  13.5 us (11%)
  local copies, waits for them, and re-layouts  11.2 us (9%)
  starting transfers between devices  5.09 us (4%)
  matrix products  3.38 us (3%)
  other arithmetic  3.18 us (3%)
    all_gather x1, waiting for transfers between devices, body(): gathered = lax.all_gather(piece, 'chan', axis=0, tiled=False)  47.2 us
    pallas_call x1, Pallas kernels, correlate(): pl.pallas_call(correlate_kernel, grid_spec=grid_spec, out_shape=jax.Shape...  38.1 us
    gather x1, local copies, waits for them, and re-layouts, body(): chosen = blocks[:, picked // span, picked % span].transpose(1, 0, 2)  5.63 us
    reshape x1, local copies, waits for them, and re-layouts, body(): blocks = gathered.reshape(SEGS, sharing, height, 2 * NF)  3.14 us
    ppermute x1, starting transfers between devices, body(): spectrum = spectrum + lax.ppermute(outgoing, 'chan', route)  2.68 us
  transfers between devices with their start and end apart: 3, of which 2 were waited for; matrix products, arithmetic and copies ran while one was open for 3% of the time, Pallas kernels for 0%

profile of v10, /device:TPU:0, one launch (start us, length us, event | category | flops | bytes accessed | tf_op | source)
XLA Modules:
  0.0 122.9 jit_solution(11126971893230845458)
XLA Ops:
  6.5 0.0 all-gather.3.cloned.1.call-start
  6.5 1.0 slice.34
  7.6 2.4 %collective-permute-start = (bf16[512,60]{1,0:T(8,128)(2,1)S(1)}, bf16[512,60]{1,0:T(8,128)(2,1)S(1)}, u32[]{:S(2)}, u32[]{:S(2)}) collective-permute-start(bf16[512,60]{1,0:T(8,128)(2,1)S(1)} %slice.34), channel_id=1, source_target_pairs={{0,1},{1,2},{2,3},{3,4},{4,5},{5,6},{6,7},{7,8},{8,9},{9,10},{10,1... | collective-permute-start | bytes 184328 | tf_op jit(solution)/shard_map/ppermute | solution.py:23
  10.0 1.9 %fusion.15 = f32[256,512]{1,0:T(8,128)S(1)} fusion(bf16[1024,256]{1,0:T(8,128)(2,1)} %constant.137, bf16[512,1024]{1,0:T(8,128)(2,1)} %param.8), kind=kOutput, calls=%fused_computation.38 | convolution fusion | flops 268435456 | bytes 2097152 | tf_op jit(solution)/shard_map/dot_general | solution.py:48
  11.9 0.0 copy-start
  11.9 0.0 collective-permute-done
  11.9 1.5 %fusion.1 = f32[512,384]{1,0:T(8,128)S(1)} fusion(f32[256,512]{1,0:T(8,128)S(1)} %fusion.15, bf16[60,256]{1,0:T(8,128)(2,1)} %constant.136, bf16[512,60]{1,0:T(8,128)(2,1)S(1)} %collective-permute-done, bf16[512,384]{1,0:T(8,128)(2,1)} %constant.138, s32[]{:T(128)S(6)} %select_n.50), kind=kOutput, calls=%fused_computation.3 | convolution fusion | flops 116654080 | bytes 1601540 | tf_op jit(solution)/shard_map/dot_general | solution.py:164
  13.5 2.7 %collective-permute-start.1 = (f32[256,384]{1,0:T(8,128)S(1)}, f32[256,384]{1,0:T(8,128)S(1)}, u32[]{:S(2)}, u32[]{:S(2)}) collective-permute-start(f32[256,384]{1,0:T(8,128)S(1)} %dynamic-slice_bitcast_fusion), channel_id=1, source_target_pairs={{0,1},{1,0},{2,3},{3,2},{4,5},{5,4},{6,7},{7,6},{8,9},{9,8},{10,11... | collective-permute-start | bytes 1179656 | tf_op jit(solution)/shard_map/ppermute | solution.py:174
  16.1 0.0 copy-done.1
  16.1 1.3 %collective-permute-done.1 = f32[256,384]{1,0:T(8,128)S(1)} collective-permute-done((f32[256,384]{1,0:T(8,128)S(1)}, f32[256,384]{1,0:T(8,128)S(1)}, u32[]{:S(2)}, u32[]{:S(2)}) %collective-permute-start.1) | collective-permute-done | bytes 393248 | tf_op jit(solution)/shard_map/ppermute | solution.py:174
  17.5 0.2 fusion.14
  17.8 0.2 multiply_convert_fusion.1
  18.0 0.8 fusion.3
  18.7 0.0 all-gather.3.cloned.1.call-update
  18.8 0.7 copy.10.own_ref
  19.5 0.6 pad_add_fusion.place_ref
  20.1 0.0 copy-done
  20.1 0.5 fusion.8
  20.6 47.2 %all-gather.3.cloned.1.call-done = bf16[4352,384]{1,0:T(8,128)(2,1)} async-done(((bf16[272,384]{1,0:T(8,128)(2,1)}), bf16[4352,384]{1,0:T(8,128)(2,1)}) %all-gather.3.cloned.1.call-update) | async-done | bytes 3342352 | tf_op jit(solution)/shard_map/all_gather | solution.py:179
  67.8 0.8 fusion.5
  68.6 0.7 reshape.45.flags_ref
  69.3 3.1 %copy.9 = bf16[8,2,272,384]{3,0,2,1:T(8,128)(2,1)S(1)} copy(bf16[8,2,272,384]{3,2,1,0:T(8,128)(2,1)} %bitcast.18) | data formatting | bytes 6684672 | tf_op jit(solution)/shard_map/reshape | solution.py:181
  72.4 5.6 %gather_fusion = bf16[512,8,384]{2,1,0:T(8,128)(2,1)} fusion(bf16[8,2,272,384]{3,0,2,1:T(8,128)(2,1)S(1)} %copy.9, s32[512]{0:T(512)S(1)} %get-tuple-element.19), kind=kCustom, calls=%fused_computation | custom fusion | bytes 6295552 | tf_op jit(solution)/shard_map/gather | solution.py:183
  78.0 38.1 %shard_map.64 = bf16[512,32,256]{2,1,0:T(8,128)(2,1)} custom-call(s32[512]{0:T(512)} %reshape.45.flags_ref, s32[512]{0:T(512)} %get-tuple-element.20.picked_ref, s32[2]{0:T(128)} %pad_add_fusion.place_ref, bf16[512,8,384]{2,1,0:T(8,128)(2,1)} %gather_fusion, bf16[8,2,272,384]{3,2,1,0:T(8,128)(2,1)} %bitcast.19, f32[32,1]{1,0:T(8,128)} %copy.10.own_ref, ...), custom_call_target="tpu_custom_call" | custom-call | tf_op jit(solution)/shard_map/pallas_call | solution.py:143
  (5 shorter events, 0.1 us)
Async XLA Ops:
  6.5 9.6 %copy-start.1 = (s32[32]{0:T(128)S(1)}, s32[32]{0:T(128)}, u32[]{:S(2)}) copy-start(s32[32]{0:T(128)} %param.10) | copy-start | bytes 388
  6.5 61.3 %all-gather.3.cloned.1.call-start = ((), (), s32[]{:S(2)}) async-start(), calls=%async_computation | async-start | bytes 3551232 | tf_op jit(solution)/shard_map/all_gather | solution.py:179
  7.6 4.3 %collective-permute-start = (bf16[512,60]{1,0:T(8,128)(2,1)S(1)}, bf16[512,60]{1,0:T(8,128)(2,1)S(1)}, u32[]{:S(2)}, u32[]{:S(2)}) collective-permute-start(bf16[512,60]{1,0:T(8,128)(2,1)S(1)} %slice.34), channel_id=1, source_target_pairs={{0,1},{1,2},{2,3},{3,4},{4,5},{5,6},{6,7},{7,8},{8,9},{9,10},{10,1... | collective-permute-start | bytes 184328 | tf_op jit(solution)/shard_map/ppermute | solution.py:23
  11.9 8.2 %copy-start = (s32[512]{0:T(512)S(1)}, s32[512]{0:T(512)}, u32[]{:S(2)}) copy-start(s32[512]{0:T(512)} %param.9) | copy-start | bytes 6148
  13.5 4.0 %collective-permute-start.1 = (f32[256,384]{1,0:T(8,128)S(1)}, f32[256,384]{1,0:T(8,128)S(1)}, u32[]{:S(2)}, u32[]{:S(2)}) collective-permute-start(f32[256,384]{1,0:T(8,128)S(1)} %dynamic-slice_bitcast_fusion), channel_id=1, source_target_pairs={{0,1},{1,0},{2,3},{3,2},{4,5},{5,4},{6,7},{7,6},{8,9},{9,8},{10,11... | collective-permute-start | bytes 1179656 | tf_op jit(solution)/shard_map/ppermute | solution.py:174
Sparse Core Ops, SparseCore 0:
  18.9 48.8 all-gather.2

commit v11 on v10

--- a/solution.py
+++ b/solution.py
@@ -79,10 +79,10 @@
 
 
 def correlate_kernel(
-    flags_ref, picked_ref, place_ref, source_ref, recv_ref, own_ref, delays_ref, out_ref,
+    flags_ref, picked_ref, rows_ref, place_ref, source_ref, recv_ref, own_ref, delays_ref, out_ref,
     plain_ref, swapped_ref, *cross_refs,
 ):
-    block = source_ref.shape[0]
+    block = out_ref.shape[0]
     receivers = recv_ref.shape[2]
     share = block // len(cross_refs)
 
@@ -100,11 +100,11 @@
 
         def one_source(s, carry):
             at = part * share + s
-            source = source_ref[at].astype(jnp.float32)
+            line = rows_ref[pl.program_id(0) * block + at]
             direct = jnp.zeros((receivers, 2 * NF), jnp.float32)
             crossed = jnp.zeros((receivers, 2 * NF), jnp.float32)
             for w in range(SEGS):
-                row = source[w : w + 1, :]
+                row = source_ref[w, pl.ds(line, 1), :]
                 direct = direct + row * plain_ref[w]
                 crossed = crossed + row * swapped_ref[w]
             flag = flags_ref[picked_ref[pl.program_id(0) * block + at]].astype(jnp.float32)
@@ -121,19 +121,19 @@
         )
 
 
-def correlate(chosen, flags_all, picked, place, blocks, own_flags, delays, block=64, parts=2):
-    source_count = chosen.shape[0]
+def correlate(table, flags_all, picked, rows, place, blocks, own_flags, delays, block=64, parts=2):
+    source_count = picked.shape[0]
     recv_count = own_flags.shape[0]
     grid_spec = pltpu.PrefetchScalarGridSpec(
-        num_scalar_prefetch=3,
+        num_scalar_prefetch=4,
         grid=(source_count // block,),
         in_specs=[
-            pl.BlockSpec((block, SEGS, 2 * NF), lambda i, f, p, q: (i, 0, 0)),
-            pl.BlockSpec((SEGS, 1, recv_count, 2 * NF), lambda i, f, p, q: (0, q[0], q[1], 0)),
-            pl.BlockSpec((recv_count, 1), lambda i, f, p, q: (0, 0)),
-            pl.BlockSpec((2 * NF, LAGS), lambda i, f, p, q: (0, 0)),
+            pl.BlockSpec(table.shape, lambda i, f, p, r, q: (0, 0, 0)),
+            pl.BlockSpec((SEGS, 1, recv_count, 2 * NF), lambda i, f, p, r, q: (0, q[0], q[1], 0)),
+            pl.BlockSpec((recv_count, 1), lambda i, f, p, r, q: (0, 0)),
+            pl.BlockSpec((2 * NF, LAGS), lambda i, f, p, r, q: (0, 0)),
         ],
-        out_specs=pl.BlockSpec((block, recv_count, LAGS), lambda i, f, p, q: (i, 0, 0)),
+        out_specs=pl.BlockSpec((block, recv_count, LAGS), lambda i, f, p, r, q: (i, 0, 0)),
         scratch_shapes=[
             pltpu.VMEM((SEGS, recv_count, 2 * NF), jnp.float32),
             pltpu.VMEM((SEGS, recv_count, 2 * NF), jnp.float32),
@@ -144,8 +144,10 @@
         correlate_kernel,
         grid_spec=grid_spec,
         out_shape=jax.ShapeDtypeStruct((source_count, recv_count, LAGS), jnp.bfloat16),
-        compiler_params=pltpu.CompilerParams(dimension_semantics=("arbitrary",)),
-    )(flags_all, picked, place, chosen, blocks, own_flags, delays)
+        compiler_params=pltpu.CompilerParams(
+            dimension_semantics=("arbitrary",), vmem_limit_bytes=48 * 1024 * 1024
+        ),
+    )(flags_all, picked, rows, place, table, blocks, own_flags, delays)
 
 
 def body(recording, source_index, channel_mask):
@@ -180,12 +182,13 @@
     height = piece.shape[0]
     blocks = gathered.reshape(SEGS, sharing, height, 2 * NF)
     picked = jnp.clip(source_index, 0, channels - 1)
-    chosen = blocks[:, picked // span, picked % span].transpose(1, 0, 2)
+    rows = picked // span * height + picked % span
+    table = blocks.reshape(SEGS, sharing * height, 2 * NF).astype(jnp.float32)
     flags_all = gathered[:, span, :per_device].reshape(channels).astype(jnp.int32)
     first = me * per_device
     place = jnp.stack([first // span, first % span // per_device]).astype(jnp.int32)
     own_flags = channel_mask.astype(jnp.float32)[:, None]
-    result = correlate(chosen, flags_all, picked, place, blocks, own_flags, delay_table())
+    result = correlate(table, flags_all, picked, rows, place, blocks, own_flags, delay_table())
     return result.reshape(SOURCES, per_device, LAGS)
 
 

time: 123 us -> 129 us (1.049)
  local copies, waits for them, and re-layouts: 11.2 us -> 2.52 us
  Pallas kernels: 38.1 us -> 45.5 us
  other arithmetic: 3.18 us -> 9.86 us
    pallas_call x1, Pallas kernels: 38.1 us -> 45.5 us  [correlate(): pl.pallas_call(correlate_kernel, grid_spec=grid_spec, out_shape=jax.Shape...]
    gather x1 -> x0, local copies, waits for them, and re-layouts: 5.63 us -> none  [body(): chosen = blocks[:, picked // span, picked % span].transpose(1, 0, 2)]
    convert_element_type x0 -> x1, other arithmetic: none -> 5.13 us  [body(): table = blocks.reshape(SEGS, sharing * height, 2 * NF).astype(jnp.float32)]
    reshape x1 -> x0, local copies, waits for them, and re-layouts: 3.14 us -> none  [body(): blocks = gathered.reshape(SEGS, sharing, height, 2 * NF)]
where the time goes in v11:
time: 129 us; the launch traced here: 128 us
  waiting for transfers between devices  48.3 us (37%)
  Pallas kernels  45.5 us (35%)
  between operations  13.6 us (11%)
  other arithmetic  9.86 us (8%)
  starting transfers between devices  5.09 us (4%)
  matrix products  3.38 us (3%)
  local copies, waits for them, and re-layouts  2.52 us (2%)
    all_gather x1, waiting for transfers between devices, body(): gathered = lax.all_gather(piece, 'chan', axis=0, tiled=False)  47.7 us
    pallas_call x1, Pallas kernels, correlate(): pl.pallas_call(correlate_kernel, grid_spec=grid_spec, out_shape=jax.Shape...  45.5 us
    convert_element_type x1, other arithmetic, body(): table = blocks.reshape(SEGS, sharing * height, 2 * NF).astype(jnp.float32)  5.13 us
    ppermute x1, starting transfers between devices, body(): spectrum = spectrum + lax.ppermute(outgoing, 'chan', route)  2.68 us
  transfers between devices with their start and end apart: 3, of which 2 were waited for; matrix products, arithmetic and copies ran while one was open for 3% of the time, Pallas kernels for 0%

profile of v11, /device:TPU:0, one launch (start us, length us, event | category | flops | bytes accessed | tf_op | source)
XLA Modules:
  0.0 128.2 jit_solution(4674279810146179813)
XLA Ops:
  6.5 1.0 slice.34
  7.6 2.4 %collective-permute-start = (bf16[512,60]{1,0:T(8,128)(2,1)S(1)}, bf16[512,60]{1,0:T(8,128)(2,1)S(1)}, u32[]{:S(2)}, u32[]{:S(2)}) collective-permute-start(bf16[512,60]{1,0:T(8,128)(2,1)S(1)} %slice.34), channel_id=1, source_target_pairs={{0,1},{1,2},{2,3},{3,4},{4,5},{5,6},{6,7},{7,8},{8,9},{9,10},{10,1... | collective-permute-start | bytes 184328 | tf_op jit(solution)/shard_map/ppermute | solution.py:23
  10.0 1.9 %fusion.12 = f32[256,512]{1,0:T(8,128)S(1)} fusion(bf16[1024,256]{1,0:T(8,128)(2,1)} %constant.135, bf16[512,1024]{1,0:T(8,128)(2,1)} %param.8), kind=kOutput, calls=%fused_computation.32 | convolution fusion | flops 268435456 | bytes 2097152 | tf_op jit(solution)/shard_map/dot_general | solution.py:48
  11.9 0.0 collective-permute-done
  11.9 1.5 %fusion.1 = f32[512,384]{1,0:T(8,128)S(1)} fusion(f32[256,512]{1,0:T(8,128)S(1)} %fusion.12, bf16[60,256]{1,0:T(8,128)(2,1)} %constant.134, bf16[512,60]{1,0:T(8,128)(2,1)S(1)} %collective-permute-done, bf16[512,384]{1,0:T(8,128)(2,1)} %constant.136, s32[]{:T(128)S(6)} %select_n.44), kind=kOutput, calls=%fused_computation.2 | convolution fusion | flops 116654080 | bytes 1601540 | tf_op jit(solution)/shard_map/dot_general | solution.py:166
  13.4 0.0 copy-start.1
  13.5 2.7 %collective-permute-start.1 = (f32[256,384]{1,0:T(8,128)S(1)}, f32[256,384]{1,0:T(8,128)S(1)}, u32[]{:S(2)}, u32[]{:S(2)}) collective-permute-start(f32[256,384]{1,0:T(8,128)S(1)} %dynamic-slice_bitcast_fusion), channel_id=1, source_target_pairs={{0,1},{1,0},{2,3},{3,2},{4,5},{5,4},{6,7},{7,6},{8,9},{9,8},{10,11... | collective-permute-start | bytes 1179656 | tf_op jit(solution)/shard_map/ppermute | solution.py:176
  16.1 0.7 convert_bitcast_fusion
  16.9 0.6 collective-permute-done.1
  17.5 0.2 fusion.11
  17.8 0.2 multiply_convert_fusion.1
  18.0 0.8 fusion.3
  18.7 0.0 all-gather.3.cloned.1.call-update
  18.8 0.1 copy.7.own_ref
  18.9 0.6 pad_add_fusion.place_ref
  19.5 0.0 copy-done.6
  19.5 0.6 fusion.7
  20.1 47.7 %all-gather.3.cloned.1.call-done = bf16[4352,384]{1,0:T(8,128)(2,1)} async-done(((bf16[272,384]{1,0:T(8,128)(2,1)}), bf16[4352,384]{1,0:T(8,128)(2,1)}) %all-gather.3.cloned.1.call-update) | async-done | bytes 3342352 | tf_op jit(solution)/shard_map/all_gather | solution.py:181
  67.8 1.5 %fusion.5 = s32[16,32]{1,0:T(8,128)} fusion(bf16[16,272,384]{2,1,0:T(8,128)(2,1)} %bitcast.20), kind=kLoop, calls=%fused_computation.14 | loop fusion | flops 512 | bytes 3072 | tf_op jit(solution)/shard_map/convert_element_type | solution.py:187
  69.4 1.4 %reshape.47.flags_ref = s32[512]{0:T(512)} reshape(s32[16,32]{1,0:T(8,128)} %fusion.5) | data formatting | bytes 4096 | tf_op jit(solution)/shard_map/convert_element_type | solution.py:187
  70.7 5.1 %convert.10.source_ref = f32[8,544,384]{2,1,0:T(8,128)} convert(bf16[8,544,384]{2,1,0:T(8,128)(2,1)} %bitcast.21) | non-fusion elementwise | flops 1671168 | bytes 10027008 | tf_op jit(solution)/shard_map/convert_element_type | solution.py:186
  75.9 0.0 copy-done.3
  75.9 0.0 copy-done.4
  75.9 45.5 %shard_map.64 = bf16[512,32,256]{2,1,0:T(8,128)(2,1)} custom-call(s32[512]{0:T(512)S(1)} %copy-done.4, s32[512]{0:T(512)S(1)} %copy-done.3, s32[512]{0:T(512)S(1)} %copy-done.2, s32[2]{0:T(128)S(1)} %copy-done.5, f32[8,544,384]{2,1,0:T(8,128)} %convert.10.source_ref, bf16[8,2,272,384]{3,2,1,0:T(8,128)(2,1)S(1)} %bitcast.22, f32[32,1]{1,0:T(8,128)S(1)} %copy.7.own_ref, ...), custom_call_target="tpu_custom_call" | custom-call | tf_op jit(solution)/shard_map/pallas_call | solution.py:143
  (14 shorter events, 0.1 us)
Async XLA Ops:
  6.5 13.0 %copy-start.6 = (s32[512]{0:T(512)S(1)}, s32[512]{0:T(512)}, u32[]{:S(2)}) copy-start(s32[512]{0:T(512)} %param.9) | copy-start | bytes 6148
  6.5 61.3 %all-gather.3.cloned.1.call-start = ((), (), s32[]{:S(2)}) async-start(), calls=%async_computation | async-start | bytes 3551232 | tf_op jit(solution)/shard_map/all_gather | solution.py:181
  7.6 4.3 %collective-permute-start = (bf16[512,60]{1,0:T(8,128)(2,1)S(1)}, bf16[512,60]{1,0:T(8,128)(2,1)S(1)}, u32[]{:S(2)}, u32[]{:S(2)}) collective-permute-start(bf16[512,60]{1,0:T(8,128)(2,1)S(1)} %slice.34), channel_id=1, source_target_pairs={{0,1},{1,2},{2,3},{3,4},{4,5},{5,6},{6,7},{7,8},{8,9},{9,10},{10,1... | collective-permute-start | bytes 184328 | tf_op jit(solution)/shard_map/ppermute | solution.py:23
  13.4 62.4 %copy-start.1 = (bf16[384,256]{1,0:T(8,128)(2,1)S(1)}, bf16[384,256]{1,0:T(8,128)(2,1)}, u32[]{:S(2)}) copy-start(bf16[384,256]{1,0:T(8,128)(2,1)} %constant.137.delays_ref) | copy-start | bytes 589828
  13.5 4.0 %collective-permute-start.1 = (f32[256,384]{1,0:T(8,128)S(1)}, f32[256,384]{1,0:T(8,128)S(1)}, u32[]{:S(2)}, u32[]{:S(2)}) collective-permute-start(f32[256,384]{1,0:T(8,128)S(1)} %dynamic-slice_bitcast_fusion), channel_id=1, source_target_pairs={{0,1},{1,0},{2,3},{3,2},{4,5},{5,4},{6,7},{7,6},{8,9},{9,8},{10,11... | collective-permute-start | bytes 1179656 | tf_op jit(solution)/shard_map/ppermute | solution.py:176
  67.8 8.0 %copy-start = (bf16[4352,384]{1,0:T(8,128)(2,1)S(1)}, bf16[4352,384]{1,0:T(8,128)(2,1)}, u32[]{:S(2)}) copy-start(bf16[4352,384]{1,0:T(8,128)(2,1)} %all-gather.3.cloned.1.call-done) | copy-start | bytes 10027012
  70.7 5.2 %copy-start.2 = (s32[512]{0:T(512)S(1)}, s32[512]{0:T(512)}, u32[]{:S(2)}) copy-start(s32[512]{0:T(512)} %get-tuple-element.19.rows_ref) | copy-start | bytes 6148
  70.7 5.2 %copy-start.3 = (s32[512]{0:T(512)S(1)}, s32[512]{0:T(512)}, u32[]{:S(2)}) copy-start(s32[512]{0:T(512)} %get-tuple-element.20.picked_ref) | copy-start | bytes 6148
  70.7 5.2 %copy-start.4 = (s32[512]{0:T(512)S(1)}, s32[512]{0:T(512)}, u32[]{:S(2)}) copy-start(s32[512]{0:T(512)} %reshape.47.flags_ref) | copy-start | bytes 6148
  70.7 5.2 %copy-start.5 = (s32[2]{0:T(128)S(1)}, s32[2]{0:T(128)}, u32[]{:S(2)}) copy-start(s32[2]{0:T(128)} %pad_add_fusion.place_ref) | copy-start | bytes 28
Sparse Core Ops, SparseCore 0:
  18.9 48.8 all-gather.2

commit v12 on v10

--- a/solution.py
+++ b/solution.py
@@ -101,14 +101,13 @@
         def one_source(s, carry):
             at = part * share + s
             source = source_ref[at].astype(jnp.float32)
-            direct = jnp.zeros((receivers, 2 * NF), jnp.float32)
-            crossed = jnp.zeros((receivers, 2 * NF), jnp.float32)
+            turned = pltpu.roll(source, NF, 1)
+            cross = jnp.zeros((receivers, 2 * NF), jnp.float32)
             for w in range(SEGS):
-                row = source[w : w + 1, :]
-                direct = direct + row * plain_ref[w]
-                crossed = crossed + row * swapped_ref[w]
+                cross = cross + source[w : w + 1, :] * plain_ref[w]
+                cross = cross + turned[w : w + 1, :] * swapped_ref[w]
             flag = flags_ref[picked_ref[pl.program_id(0) * block + at]].astype(jnp.float32)
-            cross = (direct - pltpu.roll(crossed, NF, 1)) * flag
+            cross = cross * flag
             start = pl.multiple_of(s * receivers, receivers)
             cross_ref[pl.ds(start, receivers), :] = cross.astype(jnp.bfloat16)
             return carry

time: 123 us -> 127 us (1.033)
  Pallas kernels: 38.1 us -> 41.8 us
    pallas_call x1, Pallas kernels: 38.1 us -> 41.8 us  [correlate(): pl.pallas_call(correlate_kernel, grid_spec=grid_spec, out_shape=jax.Shape...]
where the time goes in v12:
time: 127 us
  waiting for transfers between devices  48.5 us (38%)
  Pallas kernels  41.8 us (33%)
  between operations  13.5 us (11%)
  local copies, waits for them, and re-layouts  11.2 us (9%)
  starting transfers between devices  5.09 us (4%)
  matrix products  3.38 us (3%)
  other arithmetic  3.18 us (3%)
    all_gather x1, waiting for transfers between devices, body(): gathered = lax.all_gather(piece, 'chan', axis=0, tiled=False)  47.2 us
    pallas_call x1, Pallas kernels, correlate(): pl.pallas_call(correlate_kernel, grid_spec=grid_spec, out_shape=jax.Shape...  41.8 us
    gather x1, local copies, waits for them, and re-layouts, body(): chosen = blocks[:, picked // span, picked % span].transpose(1, 0, 2)  5.63 us
    reshape x1, local copies, waits for them, and re-layouts, body(): blocks = gathered.reshape(SEGS, sharing, height, 2 * NF)  3.14 us
    ppermute x1, starting transfers between devices, body(): spectrum = spectrum + lax.ppermute(outgoing, 'chan', route)  2.68 us
  transfers between devices with their start and end apart: 3, of which 2 were waited for; matrix products, arithmetic and copies ran while one was open for 3% of the time, Pallas kernels for 0%

profile of v12, /device:TPU:0, one launch (start us, length us, event | category | flops | bytes accessed | tf_op | source)
XLA Modules:
  0.0 126.7 jit_solution(3706323713936866550)
XLA Ops:
  6.5 0.0 all-gather.3.cloned.1.call-start
  6.5 1.0 slice.34
  7.6 2.4 %collective-permute-start = (bf16[512,60]{1,0:T(8,128)(2,1)S(1)}, bf16[512,60]{1,0:T(8,128)(2,1)S(1)}, u32[]{:S(2)}, u32[]{:S(2)}) collective-permute-start(bf16[512,60]{1,0:T(8,128)(2,1)S(1)} %slice.34), channel_id=1, source_target_pairs={{0,1},{1,2},{2,3},{3,4},{4,5},{5,6},{6,7},{7,8},{8,9},{9,10},{10,1... | collective-permute-start | bytes 184328 | tf_op jit(solution)/shard_map/ppermute | solution.py:23
  10.0 1.9 %fusion.15 = f32[256,512]{1,0:T(8,128)S(1)} fusion(bf16[1024,256]{1,0:T(8,128)(2,1)} %constant.137, bf16[512,1024]{1,0:T(8,128)(2,1)} %param.8), kind=kOutput, calls=%fused_computation.38 | convolution fusion | flops 268435456 | bytes 2097152 | tf_op jit(solution)/shard_map/dot_general | solution.py:48
  11.9 0.0 copy-start
  11.9 0.0 collective-permute-done
  11.9 1.5 %fusion.1 = f32[512,384]{1,0:T(8,128)S(1)} fusion(f32[256,512]{1,0:T(8,128)S(1)} %fusion.15, bf16[60,256]{1,0:T(8,128)(2,1)} %constant.136, bf16[512,60]{1,0:T(8,128)(2,1)S(1)} %collective-permute-done, bf16[512,384]{1,0:T(8,128)(2,1)} %constant.138, s32[]{:T(128)S(6)} %select_n.50), kind=kOutput, calls=%fused_computation.3 | convolution fusion | flops 116654080 | bytes 1601540 | tf_op jit(solution)/shard_map/dot_general | solution.py:163
  13.5 2.7 %collective-permute-start.1 = (f32[256,384]{1,0:T(8,128)S(1)}, f32[256,384]{1,0:T(8,128)S(1)}, u32[]{:S(2)}, u32[]{:S(2)}) collective-permute-start(f32[256,384]{1,0:T(8,128)S(1)} %dynamic-slice_bitcast_fusion), channel_id=1, source_target_pairs={{0,1},{1,0},{2,3},{3,2},{4,5},{5,4},{6,7},{7,6},{8,9},{9,8},{10,11... | collective-permute-start | bytes 1179656 | tf_op jit(solution)/shard_map/ppermute | solution.py:173
  16.1 0.0 copy-done.1
  16.1 1.3 %collective-permute-done.1 = f32[256,384]{1,0:T(8,128)S(1)} collective-permute-done((f32[256,384]{1,0:T(8,128)S(1)}, f32[256,384]{1,0:T(8,128)S(1)}, u32[]{:S(2)}, u32[]{:S(2)}) %collective-permute-start.1) | collective-permute-done | bytes 393248 | tf_op jit(solution)/shard_map/ppermute | solution.py:173
  17.5 0.2 fusion.14
  17.8 0.2 multiply_convert_fusion.1
  18.0 0.8 fusion.3
  18.7 0.0 all-gather.3.cloned.1.call-update
  18.8 0.7 copy.10.own_ref
  19.5 0.6 pad_add_fusion.place_ref
  20.1 0.0 copy-done
  20.1 0.5 fusion.8
  20.6 47.2 %all-gather.3.cloned.1.call-done = bf16[4352,384]{1,0:T(8,128)(2,1)} async-done(((bf16[272,384]{1,0:T(8,128)(2,1)}), bf16[4352,384]{1,0:T(8,128)(2,1)}) %all-gather.3.cloned.1.call-update) | async-done | bytes 3342352 | tf_op jit(solution)/shard_map/all_gather | solution.py:178
  67.8 0.8 fusion.5
  68.6 0.7 reshape.45.flags_ref
  69.3 3.1 %copy.9 = bf16[8,2,272,384]{3,0,2,1:T(8,128)(2,1)S(1)} copy(bf16[8,2,272,384]{3,2,1,0:T(8,128)(2,1)} %bitcast.18) | data formatting | bytes 6684672 | tf_op jit(solution)/shard_map/reshape | solution.py:180
  72.4 5.6 %gather_fusion = bf16[512,8,384]{2,1,0:T(8,128)(2,1)} fusion(bf16[8,2,272,384]{3,0,2,1:T(8,128)(2,1)S(1)} %copy.9, s32[512]{0:T(512)S(1)} %get-tuple-element.19), kind=kCustom, calls=%fused_computation | custom fusion | bytes 6295552 | tf_op jit(solution)/shard_map/gather | solution.py:182
  78.0 41.8 %shard_map.64 = bf16[512,32,256]{2,1,0:T(8,128)(2,1)} custom-call(s32[512]{0:T(512)} %reshape.45.flags_ref, s32[512]{0:T(512)} %get-tuple-element.20.picked_ref, s32[2]{0:T(128)} %pad_add_fusion.place_ref, bf16[512,8,384]{2,1,0:T(8,128)(2,1)} %gather_fusion, bf16[8,2,272,384]{3,2,1,0:T(8,128)(2,1)} %bitcast.19, f32[32,1]{1,0:T(8,128)} %copy.10.own_ref, ...), custom_call_target="tpu_custom_call" | custom-call | tf_op jit(solution)/shard_map/pallas_call | solution.py:142
  (5 shorter events, 0.1 us)
Async XLA Ops:
  6.5 9.6 %copy-start.1 = (s32[32]{0:T(128)S(1)}, s32[32]{0:T(128)}, u32[]{:S(2)}) copy-start(s32[32]{0:T(128)} %param.10) | copy-start | bytes 388
  6.5 61.3 %all-gather.3.cloned.1.call-start = ((), (), s32[]{:S(2)}) async-start(), calls=%async_computation | async-start | bytes 3551232 | tf_op jit(solution)/shard_map/all_gather | solution.py:178
  7.6 4.3 %collective-permute-start = (bf16[512,60]{1,0:T(8,128)(2,1)S(1)}, bf16[512,60]{1,0:T(8,128)(2,1)S(1)}, u32[]{:S(2)}, u32[]{:S(2)}) collective-permute-start(bf16[512,60]{1,0:T(8,128)(2,1)S(1)} %slice.34), channel_id=1, source_target_pairs={{0,1},{1,2},{2,3},{3,4},{4,5},{5,6},{6,7},{7,8},{8,9},{9,10},{10,1... | collective-permute-start | bytes 184328 | tf_op jit(solution)/shard_map/ppermute | solution.py:23
  11.9 8.2 %copy-start = (s32[512]{0:T(512)S(1)}, s32[512]{0:T(512)}, u32[]{:S(2)}) copy-start(s32[512]{0:T(512)} %param.9) | copy-start | bytes 6148
  13.5 4.0 %collective-permute-start.1 = (f32[256,384]{1,0:T(8,128)S(1)}, f32[256,384]{1,0:T(8,128)S(1)}, u32[]{:S(2)}, u32[]{:S(2)}) collective-permute-start(f32[256,384]{1,0:T(8,128)S(1)} %dynamic-slice_bitcast_fusion), channel_id=1, source_target_pairs={{0,1},{1,0},{2,3},{3,2},{4,5},{5,4},{6,7},{7,6},{8,9},{9,8},{10,11... | collective-permute-start | bytes 1179656 | tf_op jit(solution)/shard_map/ppermute | solution.py:173
Sparse Core Ops, SparseCore 0:
  18.9 48.8 all-gather.2

commit v13 on v10

--- a/solution.py
+++ b/solution.py
@@ -101,12 +101,14 @@
         def one_source(s, carry):
             at = part * share + s
             source = source_ref[at].astype(jnp.float32)
-            direct = jnp.zeros((receivers, 2 * NF), jnp.float32)
-            crossed = jnp.zeros((receivers, 2 * NF), jnp.float32)
+            direct = [jnp.zeros((receivers, 2 * NF), jnp.float32)] * 2
+            crossed = [jnp.zeros((receivers, 2 * NF), jnp.float32)] * 2
             for w in range(SEGS):
                 row = source[w : w + 1, :]
-                direct = direct + row * plain_ref[w]
-                crossed = crossed + row * swapped_ref[w]
+                direct[w % 2] = direct[w % 2] + row * plain_ref[w]
+                crossed[w % 2] = crossed[w % 2] + row * swapped_ref[w]
+            direct = direct[0] + direct[1]
+            crossed = crossed[0] + crossed[1]
             flag = flags_ref[picked_ref[pl.program_id(0) * block + at]].astype(jnp.float32)
             cross = (direct - pltpu.roll(crossed, NF, 1)) * flag
             start = pl.multiple_of(s * receivers, receivers)

time: 123 us -> 124 us (level)
  no operation moved by 1% of the time
where the time goes in v13:
time: 124 us; the launch traced here: 123 us
  waiting for transfers between devices  48.5 us (39%)
  Pallas kernels  38.5 us (31%)
  between operations  13.5 us (11%)
  local copies, waits for them, and re-layouts  11.2 us (9%)
  starting transfers between devices  5.09 us (4%)
  matrix products  3.38 us (3%)
  other arithmetic  3.18 us (3%)
    all_gather x1, waiting for transfers between devices, body(): gathered = lax.all_gather(piece, 'chan', axis=0, tiled=False)  47.2 us
    pallas_call x1, Pallas kernels, correlate(): pl.pallas_call(correlate_kernel, grid_spec=grid_spec, out_shape=jax.Shape...  38.5 us
    gather x1, local copies, waits for them, and re-layouts, body(): chosen = blocks[:, picked // span, picked % span].transpose(1, 0, 2)  5.63 us
    reshape x1, local copies, waits for them, and re-layouts, body(): blocks = gathered.reshape(SEGS, sharing, height, 2 * NF)  3.14 us
    ppermute x1, starting transfers between devices, body(): spectrum = spectrum + lax.ppermute(outgoing, 'chan', route)  2.68 us
  transfers between devices with their start and end apart: 3, of which 2 were waited for; matrix products, arithmetic and copies ran while one was open for 3% of the time, Pallas kernels for 0%

profile of v13, /device:TPU:0, one launch (start us, length us, event | category | flops | bytes accessed | tf_op | source)
XLA Modules:
  0.0 123.4 jit_solution(5287924693716120879)
XLA Ops:
  6.5 0.0 all-gather.3.cloned.1.call-start
  6.5 1.0 slice.34
  7.6 2.4 %collective-permute-start = (bf16[512,60]{1,0:T(8,128)(2,1)S(1)}, bf16[512,60]{1,0:T(8,128)(2,1)S(1)}, u32[]{:S(2)}, u32[]{:S(2)}) collective-permute-start(bf16[512,60]{1,0:T(8,128)(2,1)S(1)} %slice.34), channel_id=1, source_target_pairs={{0,1},{1,2},{2,3},{3,4},{4,5},{5,6},{6,7},{7,8},{8,9},{9,10},{10,1... | collective-permute-start | bytes 184328 | tf_op jit(solution)/shard_map/ppermute | solution.py:23
  10.0 1.9 %fusion.15 = f32[256,512]{1,0:T(8,128)S(1)} fusion(bf16[1024,256]{1,0:T(8,128)(2,1)} %constant.137, bf16[512,1024]{1,0:T(8,128)(2,1)} %param.8), kind=kOutput, calls=%fused_computation.38 | convolution fusion | flops 268435456 | bytes 2097152 | tf_op jit(solution)/shard_map/dot_general | solution.py:48
  11.9 0.0 copy-start
  11.9 0.0 collective-permute-done
  11.9 1.5 %fusion.1 = f32[512,384]{1,0:T(8,128)S(1)} fusion(f32[256,512]{1,0:T(8,128)S(1)} %fusion.15, bf16[60,256]{1,0:T(8,128)(2,1)} %constant.136, bf16[512,60]{1,0:T(8,128)(2,1)S(1)} %collective-permute-done, bf16[512,384]{1,0:T(8,128)(2,1)} %constant.138, s32[]{:T(128)S(6)} %select_n.50), kind=kOutput, calls=%fused_computation.3 | convolution fusion | flops 116654080 | bytes 1601540 | tf_op jit(solution)/shard_map/dot_general | solution.py:166
  13.5 2.7 %collective-permute-start.1 = (f32[256,384]{1,0:T(8,128)S(1)}, f32[256,384]{1,0:T(8,128)S(1)}, u32[]{:S(2)}, u32[]{:S(2)}) collective-permute-start(f32[256,384]{1,0:T(8,128)S(1)} %dynamic-slice_bitcast_fusion), channel_id=1, source_target_pairs={{0,1},{1,0},{2,3},{3,2},{4,5},{5,4},{6,7},{7,6},{8,9},{9,8},{10,11... | collective-permute-start | bytes 1179656 | tf_op jit(solution)/shard_map/ppermute | solution.py:176
  16.1 0.0 copy-done.1
  16.1 1.3 %collective-permute-done.1 = f32[256,384]{1,0:T(8,128)S(1)} collective-permute-done((f32[256,384]{1,0:T(8,128)S(1)}, f32[256,384]{1,0:T(8,128)S(1)}, u32[]{:S(2)}, u32[]{:S(2)}) %collective-permute-start.1) | collective-permute-done | bytes 393248 | tf_op jit(solution)/shard_map/ppermute | solution.py:176
  17.5 0.2 fusion.14
  17.8 0.2 multiply_convert_fusion.1
  18.0 0.8 fusion.3
  18.7 0.0 all-gather.3.cloned.1.call-update
  18.8 0.7 copy.10.own_ref
  19.5 0.6 pad_add_fusion.place_ref
  20.1 0.0 copy-done
  20.1 0.5 fusion.8
  20.6 47.2 %all-gather.3.cloned.1.call-done = bf16[4352,384]{1,0:T(8,128)(2,1)} async-done(((bf16[272,384]{1,0:T(8,128)(2,1)}), bf16[4352,384]{1,0:T(8,128)(2,1)}) %all-gather.3.cloned.1.call-update) | async-done | bytes 3342352 | tf_op jit(solution)/shard_map/all_gather | solution.py:181
  67.8 0.8 fusion.5
  68.6 0.7 reshape.45.flags_ref
  69.3 3.1 %copy.9 = bf16[8,2,272,384]{3,0,2,1:T(8,128)(2,1)S(1)} copy(bf16[8,2,272,384]{3,2,1,0:T(8,128)(2,1)} %bitcast.18) | data formatting | bytes 6684672 | tf_op jit(solution)/shard_map/reshape | solution.py:183
  72.4 5.6 %gather_fusion = bf16[512,8,384]{2,1,0:T(8,128)(2,1)} fusion(bf16[8,2,272,384]{3,0,2,1:T(8,128)(2,1)S(1)} %copy.9, s32[512]{0:T(512)S(1)} %get-tuple-element.19), kind=kCustom, calls=%fused_computation | custom fusion | bytes 6295552 | tf_op jit(solution)/shard_map/gather | solution.py:185
  78.0 38.5 %shard_map.64 = bf16[512,32,256]{2,1,0:T(8,128)(2,1)} custom-call(s32[512]{0:T(512)} %reshape.45.flags_ref, s32[512]{0:T(512)} %get-tuple-element.20.picked_ref, s32[2]{0:T(128)} %pad_add_fusion.place_ref, bf16[512,8,384]{2,1,0:T(8,128)(2,1)} %gather_fusion, bf16[8,2,272,384]{3,2,1,0:T(8,128)(2,1)} %bitcast.19, f32[32,1]{1,0:T(8,128)} %copy.10.own_ref, ...), custom_call_target="tpu_custom_call" | custom-call | tf_op jit(solution)/shard_map/pallas_call | solution.py:145
  (5 shorter events, 0.1 us)
Async XLA Ops:
  6.5 9.6 %copy-start.1 = (s32[32]{0:T(128)S(1)}, s32[32]{0:T(128)}, u32[]{:S(2)}) copy-start(s32[32]{0:T(128)} %param.10) | copy-start | bytes 388
  6.5 61.3 %all-gather.3.cloned.1.call-start = ((), (), s32[]{:S(2)}) async-start(), calls=%async_computation | async-start | bytes 3551232 | tf_op jit(solution)/shard_map/all_gather | solution.py:181
  7.6 4.3 %collective-permute-start = (bf16[512,60]{1,0:T(8,128)(2,1)S(1)}, bf16[512,60]{1,0:T(8,128)(2,1)S(1)}, u32[]{:S(2)}, u32[]{:S(2)}) collective-permute-start(bf16[512,60]{1,0:T(8,128)(2,1)S(1)} %slice.34), channel_id=1, source_target_pairs={{0,1},{1,2},{2,3},{3,4},{4,5},{5,6},{6,7},{7,8},{8,9},{9,10},{10,1... | collective-permute-start | bytes 184328 | tf_op jit(solution)/shard_map/ppermute | solution.py:23
  11.9 8.2 %copy-start = (s32[512]{0:T(512)S(1)}, s32[512]{0:T(512)}, u32[]{:S(2)}) copy-start(s32[512]{0:T(512)} %param.9) | copy-start | bytes 6148
  13.5 4.0 %collective-permute-start.1 = (f32[256,384]{1,0:T(8,128)S(1)}, f32[256,384]{1,0:T(8,128)S(1)}, u32[]{:S(2)}, u32[]{:S(2)}) collective-permute-start(f32[256,384]{1,0:T(8,128)S(1)} %dynamic-slice_bitcast_fusion), channel_id=1, source_target_pairs={{0,1},{1,0},{2,3},{3,2},{4,5},{5,4},{6,7},{7,6},{8,9},{9,8},{10,11... | collective-permute-start | bytes 1179656 | tf_op jit(solution)/shard_map/ppermute | solution.py:176
Sparse Core Ops, SparseCore 0:
  18.9 48.8 all-gather.2

commit v14 on v10

--- a/solution.py
+++ b/solution.py
@@ -82,7 +82,7 @@
     flags_ref, picked_ref, place_ref, source_ref, recv_ref, own_ref, delays_ref, out_ref,
     plain_ref, swapped_ref, *cross_refs,
 ):
-    block = source_ref.shape[0]
+    block = source_ref.shape[1]
     receivers = recv_ref.shape[2]
     share = block // len(cross_refs)
 
@@ -100,11 +100,10 @@
 
         def one_source(s, carry):
             at = part * share + s
-            source = source_ref[at].astype(jnp.float32)
             direct = jnp.zeros((receivers, 2 * NF), jnp.float32)
             crossed = jnp.zeros((receivers, 2 * NF), jnp.float32)
             for w in range(SEGS):
-                row = source[w : w + 1, :]
+                row = source_ref[w, pl.ds(at, 1), :].astype(jnp.float32)
                 direct = direct + row * plain_ref[w]
                 crossed = crossed + row * swapped_ref[w]
             flag = flags_ref[picked_ref[pl.program_id(0) * block + at]].astype(jnp.float32)
@@ -122,13 +121,13 @@
 
 
 def correlate(chosen, flags_all, picked, place, blocks, own_flags, delays, block=64, parts=2):
-    source_count = chosen.shape[0]
+    source_count = chosen.shape[1]
     recv_count = own_flags.shape[0]
     grid_spec = pltpu.PrefetchScalarGridSpec(
         num_scalar_prefetch=3,
         grid=(source_count // block,),
         in_specs=[
-            pl.BlockSpec((block, SEGS, 2 * NF), lambda i, f, p, q: (i, 0, 0)),
+            pl.BlockSpec((SEGS, block, 2 * NF), lambda i, f, p, q: (0, i, 0)),
             pl.BlockSpec((SEGS, 1, recv_count, 2 * NF), lambda i, f, p, q: (0, q[0], q[1], 0)),
             pl.BlockSpec((recv_count, 1), lambda i, f, p, q: (0, 0)),
             pl.BlockSpec((2 * NF, LAGS), lambda i, f, p, q: (0, 0)),
@@ -180,7 +179,11 @@
     height = piece.shape[0]
     blocks = gathered.reshape(SEGS, sharing, height, 2 * NF)
     picked = jnp.clip(source_index, 0, channels - 1)
-    chosen = blocks[:, picked // span, picked % span].transpose(1, 0, 2)
+    table = gathered.reshape(SEGS, sharing * height, 2 * NF)
+    line = picked // span * height + picked % span
+    pick = (line[:, None] == jnp.arange(sharing * height, dtype=jnp.int32)[None, :]).astype(jnp.bfloat16)
+    chosen = jnp.einsum("sc,wcj->wsj", pick, table, preferred_element_type=jnp.float32)
+    chosen = chosen.astype(jnp.bfloat16)
     flags_all = gathered[:, span, :per_device].reshape(channels).astype(jnp.int32)
     first = me * per_device
     place = jnp.stack([first // span, first % span // per_device]).astype(jnp.int32)

time: 123 us -> 122 us (level)
  local copies, waits for them, and re-layouts: 11.2 us -> 2.4 us
  matrix products: 3.38 us -> 9.38 us
  Pallas kernels: 38.1 us -> 39.7 us
    dot_general x0 -> x1, matrix products: none -> 6 us  [body(): jnp.einsum('sc,wcj->wsj', pick, table, preferred_element_type=jnp.float32)]
    gather x1 -> x0, local copies, waits for them, and re-layouts: 5.63 us -> none  [body(): chosen = blocks[:, picked // span, picked % span].transpose(1, 0, 2)]
    reshape x1 -> x0, local copies, waits for them, and re-layouts: 3.14 us -> none  [body(): blocks = gathered.reshape(SEGS, sharing, height, 2 * NF)]
    pallas_call x1, Pallas kernels: 38.1 us -> 39.7 us  [correlate(): pl.pallas_call(correlate_kernel, grid_spec=grid_spec, out_shape=jax.Shape...]
where the time goes in v14:
time: 122 us
  waiting for transfers between devices  48.5 us (40%)
  Pallas kernels  39.7 us (33%)
  between operations  13.5 us (11%)
  matrix products  9.38 us (8%)
  starting transfers between devices  5.09 us (4%)
  other arithmetic  3.18 us (3%)
  local copies, waits for them, and re-layouts  2.4 us (2%)
    all_gather x1, waiting for transfers between devices, body(): gathered = lax.all_gather(piece, 'chan', axis=0, tiled=False)  47.2 us
    pallas_call x1, Pallas kernels, correlate(): pl.pallas_call(correlate_kernel, grid_spec=grid_spec, out_shape=jax.Shape...  39.7 us
    dot_general x1, matrix products, body(): jnp.einsum('sc,wcj->wsj', pick, table, preferred_element_type=jnp.float32)  6 us
    ppermute x1, starting transfers between devices, body(): spectrum = spectrum + lax.ppermute(outgoing, 'chan', route)  2.68 us
  transfers between devices with their start and end apart: 3, of which 2 were waited for; matrix products, arithmetic and copies ran while one was open for 3% of the time, Pallas kernels for 0%

profile of v14, /device:TPU:0, one launch (start us, length us, event | category | flops | bytes accessed | tf_op | source)
XLA Modules:
  0.0 121.8 jit_solution(13562678051857360192)
XLA Ops:
  6.5 0.0 copy-start.1
  6.5 0.0 all-gather.3.cloned.1.call-start
  6.5 1.0 slice.34
  7.6 2.4 %collective-permute-start = (bf16[512,60]{1,0:T(8,128)(2,1)S(1)}, bf16[512,60]{1,0:T(8,128)(2,1)S(1)}, u32[]{:S(2)}, u32[]{:S(2)}) collective-permute-start(bf16[512,60]{1,0:T(8,128)(2,1)S(1)} %slice.34), channel_id=1, source_target_pairs={{0,1},{1,2},{2,3},{3,4},{4,5},{5,6},{6,7},{7,8},{8,9},{9,10},{10,1... | collective-permute-start | bytes 184328 | tf_op jit(solution)/shard_map/ppermute | solution.py:23
  10.0 1.9 %fusion.15 = f32[256,512]{1,0:T(8,128)S(1)} fusion(bf16[1024,256]{1,0:T(8,128)(2,1)} %constant.135, bf16[512,1024]{1,0:T(8,128)(2,1)} %param.8), kind=kOutput, calls=%fused_computation.36 | convolution fusion | flops 268435456 | bytes 2097152 | tf_op jit(solution)/shard_map/dot_general | solution.py:48
  11.9 0.0 copy-start
  11.9 0.0 collective-permute-done
  11.9 1.5 %fusion.1 = f32[512,384]{1,0:T(8,128)S(1)} fusion(f32[256,512]{1,0:T(8,128)S(1)} %fusion.15, bf16[60,256]{1,0:T(8,128)(2,1)} %constant.134, bf16[512,60]{1,0:T(8,128)(2,1)S(1)} %collective-permute-done, bf16[512,384]{1,0:T(8,128)(2,1)} %constant.136, s32[]{:T(128)S(6)} %select_n.44), kind=kOutput, calls=%fused_computation.3 | convolution fusion | flops 116654080 | bytes 1601540 | tf_op jit(solution)/shard_map/dot_general | solution.py:163
  13.5 2.7 %collective-permute-start.1 = (f32[256,384]{1,0:T(8,128)S(1)}, f32[256,384]{1,0:T(8,128)S(1)}, u32[]{:S(2)}, u32[]{:S(2)}) collective-permute-start(f32[256,384]{1,0:T(8,128)S(1)} %dynamic-slice_bitcast_fusion), channel_id=1, source_target_pairs={{0,1},{1,0},{2,3},{3,2},{4,5},{5,4},{6,7},{7,6},{8,9},{9,8},{10,11... | collective-permute-start | bytes 1179656 | tf_op jit(solution)/shard_map/ppermute | solution.py:173
  16.1 0.0 copy-done.1
  16.1 1.3 %collective-permute-done.1 = f32[256,384]{1,0:T(8,128)S(1)} collective-permute-done((f32[256,384]{1,0:T(8,128)S(1)}, f32[256,384]{1,0:T(8,128)S(1)}, u32[]{:S(2)}, u32[]{:S(2)}) %collective-permute-start.1) | collective-permute-done | bytes 393248 | tf_op jit(solution)/shard_map/ppermute | solution.py:173
  17.5 0.2 fusion.14
  17.8 0.2 multiply_convert_fusion.1
  18.0 0.8 fusion.6
  18.7 0.0 all-gather.3.cloned.1.call-update
  18.8 0.7 copy.8.own_ref
  19.5 0.6 pad_add_fusion.place_ref
  20.1 0.0 copy-done
  20.1 0.5 fusion.10
  20.6 47.2 %all-gather.3.cloned.1.call-done = bf16[4352,384]{1,0:T(8,128)(2,1)} async-done(((bf16[272,384]{1,0:T(8,128)(2,1)}), bf16[4352,384]{1,0:T(8,128)(2,1)}) %all-gather.3.cloned.1.call-update) | async-done | bytes 3342352 | tf_op jit(solution)/shard_map/all_gather | solution.py:178
  67.8 0.8 fusion.8
  68.6 0.7 reshape.50.flags_ref
  69.3 6.0 %convert_bitcast_fusion.source_ref = bf16[8,512,384]{2,1,0:T(8,128)(2,1)} fusion(bf16[8,544,384]{2,1,0:T(8,128)(2,1)} %bitcast.25, s32[512]{0:T(512)S(1)} %get-tuple-element.19), kind=kOutput, calls=%fused_computation | convolution fusion | flops 1713127424 | bytes 6490112 | tf_op jit(solution)/shard_map/sc,wcj->wsj/dot_general | solution.py:185
  75.3 39.7 %shard_map.64 = bf16[512,32,256]{2,1,0:T(8,128)(2,1)} custom-call(s32[512]{0:T(512)} %reshape.50.flags_ref, s32[512]{0:T(512)} %get-tuple-element.20.picked_ref, s32[2]{0:T(128)} %pad_add_fusion.place_ref, bf16[8,512,384]{2,1,0:T(8,128)(2,1)} %convert_bitcast_fusion.source_ref, bf16[8,2,272,384]{3,2,1,0:T(8,128)(2,1)} %bitcast.26, f32[32,1]{1,0:T(8,128)} %copy.8.own_ref, ...), custom_call_target="tpu_custom_call" | custom-call | tf_op jit(solution)/shard_map/pallas_call | solution.py:142
  (4 shorter events, 0.1 us)
Async XLA Ops:
  6.5 9.6 %copy-start.1 = (s32[32]{0:T(128)S(1)}, s32[32]{0:T(128)}, u32[]{:S(2)}) copy-start(s32[32]{0:T(128)} %param.10) | copy-start | bytes 388
  6.5 61.3 %all-gather.3.cloned.1.call-start = ((), (), s32[]{:S(2)}) async-start(), calls=%async_computation | async-start | bytes 3551232 | tf_op jit(solution)/shard_map/all_gather | solution.py:178
  7.6 4.3 %collective-permute-start = (bf16[512,60]{1,0:T(8,128)(2,1)S(1)}, bf16[512,60]{1,0:T(8,128)(2,1)S(1)}, u32[]{:S(2)}, u32[]{:S(2)}) collective-permute-start(bf16[512,60]{1,0:T(8,128)(2,1)S(1)} %slice.34), channel_id=1, source_target_pairs={{0,1},{1,2},{2,3},{3,4},{4,5},{5,6},{6,7},{7,8},{8,9},{9,10},{10,1... | collective-permute-start | bytes 184328 | tf_op jit(solution)/shard_map/ppermute | solution.py:23
  11.9 8.2 %copy-start = (s32[512]{0:T(512)S(1)}, s32[512]{0:T(512)}, u32[]{:S(2)}) copy-start(s32[512]{0:T(512)} %param.9) | copy-start | bytes 6148
  13.5 4.0 %collective-permute-start.1 = (f32[256,384]{1,0:T(8,128)S(1)}, f32[256,384]{1,0:T(8,128)S(1)}, u32[]{:S(2)}, u32[]{:S(2)}) collective-permute-start(f32[256,384]{1,0:T(8,128)S(1)} %dynamic-slice_bitcast_fusion), channel_id=1, source_target_pairs={{0,1},{1,0},{2,3},{3,2},{4,5},{5,4},{6,7},{7,6},{8,9},{9,8},{10,11... | collective-permute-start | bytes 1179656 | tf_op jit(solution)/shard_map/ppermute | solution.py:173
Sparse Core Ops, SparseCore 0:
  18.9 48.8 all-gather.2

commit v15 on v14

--- a/solution.py
+++ b/solution.py
@@ -79,10 +79,10 @@
 
 
 def correlate_kernel(
-    flags_ref, picked_ref, place_ref, source_ref, recv_ref, own_ref, delays_ref, out_ref,
-    plain_ref, swapped_ref, *cross_refs,
+    flags_ref, picked_ref, place_ref, lines_ref, table_ref, recv_ref, own_ref, delays_ref, out_ref,
+    plain_ref, swapped_ref, source_ref, *cross_refs,
 ):
-    block = source_ref.shape[1]
+    block = out_ref.shape[0]
     receivers = recv_ref.shape[2]
     share = block // len(cross_refs)
 
@@ -96,6 +96,12 @@
             plain_ref[w] = jnp.where(lower, spectra, turned)
             swapped_ref[w] = jnp.where(lower, turned, -spectra)
 
+    height = table_ref.shape[1]
+    wanted = lines_ref[...]
+    pick = (wanted == lax.broadcasted_iota(jnp.int32, (block, height), 1)).astype(jnp.bfloat16)
+    for w in range(SEGS):
+        source_ref[w] = jnp.dot(pick, table_ref[w], preferred_element_type=jnp.float32)
+
     for part, cross_ref in enumerate(cross_refs):
 
         def one_source(s, carry):
@@ -103,7 +109,7 @@
             direct = jnp.zeros((receivers, 2 * NF), jnp.float32)
             crossed = jnp.zeros((receivers, 2 * NF), jnp.float32)
             for w in range(SEGS):
-                row = source_ref[w, pl.ds(at, 1), :].astype(jnp.float32)
+                row = source_ref[w, pl.ds(at, 1), :]
                 direct = direct + row * plain_ref[w]
                 crossed = crossed + row * swapped_ref[w]
             flag = flags_ref[picked_ref[pl.program_id(0) * block + at]].astype(jnp.float32)
@@ -120,14 +126,15 @@
         )
 
 
-def correlate(chosen, flags_all, picked, place, blocks, own_flags, delays, block=64, parts=2):
-    source_count = chosen.shape[1]
+def correlate(table, lines, flags_all, picked, place, blocks, own_flags, delays, block=64, parts=2):
+    source_count = picked.shape[0]
     recv_count = own_flags.shape[0]
     grid_spec = pltpu.PrefetchScalarGridSpec(
         num_scalar_prefetch=3,
         grid=(source_count // block,),
         in_specs=[
-            pl.BlockSpec((SEGS, block, 2 * NF), lambda i, f, p, q: (0, i, 0)),
+            pl.BlockSpec((block, 1), lambda i, f, p, q: (i, 0)),
+            pl.BlockSpec(table.shape, lambda i, f, p, q: (0, 0, 0)),
             pl.BlockSpec((SEGS, 1, recv_count, 2 * NF), lambda i, f, p, q: (0, q[0], q[1], 0)),
             pl.BlockSpec((recv_count, 1), lambda i, f, p, q: (0, 0)),
             pl.BlockSpec((2 * NF, LAGS), lambda i, f, p, q: (0, 0)),
@@ -136,6 +143,7 @@
         scratch_shapes=[
             pltpu.VMEM((SEGS, recv_count, 2 * NF), jnp.float32),
             pltpu.VMEM((SEGS, recv_count, 2 * NF), jnp.float32),
+            pltpu.VMEM((SEGS, block, 2 * NF), jnp.float32),
         ]
         + [pltpu.VMEM((block // parts * recv_count, 2 * NF), jnp.bfloat16)] * parts,
     )
@@ -144,7 +152,7 @@
         grid_spec=grid_spec,
         out_shape=jax.ShapeDtypeStruct((source_count, recv_count, LAGS), jnp.bfloat16),
         compiler_params=pltpu.CompilerParams(dimension_semantics=("arbitrary",)),
-    )(flags_all, picked, place, chosen, blocks, own_flags, delays)
+    )(flags_all, picked, place, lines, table, blocks, own_flags, delays)
 
 
 def body(recording, source_index, channel_mask):
@@ -181,14 +189,11 @@
     picked = jnp.clip(source_index, 0, channels - 1)
     table = gathered.reshape(SEGS, sharing * height, 2 * NF)
     line = picked // span * height + picked % span
-    pick = (line[:, None] == jnp.arange(sharing * height, dtype=jnp.int32)[None, :]).astype(jnp.bfloat16)
-    chosen = jnp.einsum("sc,wcj->wsj", pick, table, preferred_element_type=jnp.float32)
-    chosen = chosen.astype(jnp.bfloat16)
     flags_all = gathered[:, span, :per_device].reshape(channels).astype(jnp.int32)
     first = me * per_device
     place = jnp.stack([first // span, first % span // per_device]).astype(jnp.int32)
     own_flags = channel_mask.astype(jnp.float32)[:, None]
-    result = correlate(chosen, flags_all, picked, place, blocks, own_flags, delay_table())
+    result = correlate(table, line[:, None], flags_all, picked, place, blocks, own_flags, delay_table())
     return result.reshape(SOURCES, per_device, LAGS)
 
 

time: 122 us -> 121 us (level)
  matrix products: 9.38 us -> 3.38 us
  Pallas kernels: 39.7 us -> 45.1 us
    dot_general x1 -> x0, matrix products: 6 us -> none  [body(): jnp.einsum('sc,wcj->wsj', pick, table, preferred_element_type=jnp.float32)]
    pallas_call x1, Pallas kernels: 39.7 us -> 45.1 us  [correlate(): pl.pallas_call(correlate_kernel, grid_spec=grid_spec, out_shape=jax.Shape...]
  transfers between devices with their start and end apart: 3 -> 3, of which waited for: 2 -> 2; matrix products, arithmetic and copies ran while one was open for 3% -> 4% of each run, Pallas kernels for 0% -> 0%
where the time goes in v15:
time: 121 us
  waiting for transfers between devices  47.6 us (39%)
  Pallas kernels  45.1 us (37%)
  between operations  13.5 us (11%)
  starting transfers between devices  5.09 us (4%)
  matrix products  3.38 us (3%)
  other arithmetic  3.26 us (3%)
  local copies, waits for them, and re-layouts  3.25 us (3%)
    all_gather x1, waiting for transfers between devices, body(): gathered = lax.all_gather(piece, 'chan', axis=0, tiled=False)  46.2 us
    pallas_call x1, Pallas kernels, correlate(): pl.pallas_call(correlate_kernel, grid_spec=grid_spec, out_shape=jax.Shape...  45.1 us
    ppermute x1, starting transfers between devices, body(): spectrum = spectrum + lax.ppermute(outgoing, 'chan', route)  2.68 us
  transfers between devices with their start and end apart: 3, of which 2 were waited for; matrix products, arithmetic and copies ran while one was open for 4% of the time, Pallas kernels for 0%

profile of v15, /device:TPU:0, one launch (start us, length us, event | category | flops | bytes accessed | tf_op | source)
XLA Modules:
  0.0 121.1 jit_solution(4028845926020184653)
XLA Ops:
  6.5 0.0 copy-start.1
  6.5 0.0 all-gather.3.cloned.1.call-start
  6.5 1.0 slice.34
  7.6 2.4 %collective-permute-start = (bf16[512,60]{1,0:T(8,128)(2,1)S(1)}, bf16[512,60]{1,0:T(8,128)(2,1)S(1)}, u32[]{:S(2)}, u32[]{:S(2)}) collective-permute-start(bf16[512,60]{1,0:T(8,128)(2,1)S(1)} %slice.34), channel_id=1, source_target_pairs={{0,1},{1,2},{2,3},{3,4},{4,5},{5,6},{6,7},{7,8},{8,9},{9,10},{10,1... | collective-permute-start | bytes 184328 | tf_op jit(solution)/shard_map/ppermute | solution.py:23
  10.0 1.9 %fusion.12 = f32[256,512]{1,0:T(8,128)S(1)} fusion(bf16[1024,256]{1,0:T(8,128)(2,1)} %constant.135, bf16[512,1024]{1,0:T(8,128)(2,1)} %param.8), kind=kOutput, calls=%fused_computation.32 | convolution fusion | flops 268435456 | bytes 2097152 | tf_op jit(solution)/shard_map/dot_general | solution.py:48
  11.9 0.0 copy-start
  11.9 0.0 collective-permute-done
  11.9 1.5 %fusion.1 = f32[512,384]{1,0:T(8,128)S(1)} fusion(f32[256,512]{1,0:T(8,128)S(1)} %fusion.12, bf16[60,256]{1,0:T(8,128)(2,1)} %constant.134, bf16[512,60]{1,0:T(8,128)(2,1)S(1)} %collective-permute-done, bf16[512,384]{1,0:T(8,128)(2,1)} %constant.136, s32[]{:T(128)S(6)} %select_n.44), kind=kOutput, calls=%fused_computation.2 | convolution fusion | flops 116654080 | bytes 1601540 | tf_op jit(solution)/shard_map/dot_general | solution.py:171
  13.5 2.7 %collective-permute-start.1 = (f32[256,384]{1,0:T(8,128)S(1)}, f32[256,384]{1,0:T(8,128)S(1)}, u32[]{:S(2)}, u32[]{:S(2)}) collective-permute-start(f32[256,384]{1,0:T(8,128)S(1)} %dynamic-slice_bitcast_fusion), channel_id=1, source_target_pairs={{0,1},{1,0},{2,3},{3,2},{4,5},{5,4},{6,7},{7,6},{8,9},{9,8},{10,11... | collective-permute-start | bytes 1179656 | tf_op jit(solution)/shard_map/ppermute | solution.py:181
  16.1 0.0 copy-done.1
  16.1 1.3 %collective-permute-done.1 = f32[256,384]{1,0:T(8,128)S(1)} collective-permute-done((f32[256,384]{1,0:T(8,128)S(1)}, f32[256,384]{1,0:T(8,128)S(1)}, u32[]{:S(2)}, u32[]{:S(2)}) %collective-permute-start.1) | collective-permute-done | bytes 393248 | tf_op jit(solution)/shard_map/ppermute | solution.py:181
  17.5 0.2 fusion.11
  17.8 0.2 multiply_convert_fusion.1
  18.0 0.8 fusion.3
  18.7 0.0 all-gather.3.cloned.1.call-update
  18.8 0.7 copy.9.own_ref
  19.5 0.0 copy-done
  19.5 0.6 fusion.7
  20.1 0.9 copy.8.lines_ref
  20.9 0.6 pad_add_fusion.place_ref
  21.6 46.2 %all-gather.3.cloned.1.call-done = bf16[4352,384]{1,0:T(8,128)(2,1)} async-done(((bf16[272,384]{1,0:T(8,128)(2,1)}), bf16[4352,384]{1,0:T(8,128)(2,1)}) %all-gather.3.cloned.1.call-update) | async-done | bytes 3342352 | tf_op jit(solution)/shard_map/all_gather | solution.py:186
  67.8 0.8 fusion.5
  68.6 0.6 reshape.49.flags_ref
  69.2 45.1 %shard_map.64 = bf16[512,32,256]{2,1,0:T(8,128)(2,1)} custom-call(s32[512]{0:T(512)} %reshape.49.flags_ref, s32[512]{0:T(512)} %get-tuple-element.20.picked_ref, s32[2]{0:T(128)} %pad_add_fusion.place_ref, s32[512,1]{1,0:T(8,128)} %copy.8.lines_ref, bf16[8,544,384]{2,1,0:T(8,128)(2,1)} %bitcast.20, bf16[8,2,272,384]{3,2,1,0:T(8,128)(2,1)} %bitcast.21, ...), custom_call_target="tpu_custom_call" | custom-call | tf_op jit(solution)/shard_map/pallas_call | solution.py:150
  (4 shorter events, 0.1 us)
Async XLA Ops:
  6.5 9.6 %copy-start.1 = (s32[32]{0:T(128)S(1)}, s32[32]{0:T(128)}, u32[]{:S(2)}) copy-start(s32[32]{0:T(128)} %param.10) | copy-start | bytes 388
  6.5 61.3 %all-gather.3.cloned.1.call-start = ((), (), s32[]{:S(2)}) async-start(), calls=%async_computation | async-start | bytes 3551232 | tf_op jit(solution)/shard_map/all_gather | solution.py:186
  7.6 4.3 %collective-permute-start = (bf16[512,60]{1,0:T(8,128)(2,1)S(1)}, bf16[512,60]{1,0:T(8,128)(2,1)S(1)}, u32[]{:S(2)}, u32[]{:S(2)}) collective-permute-start(bf16[512,60]{1,0:T(8,128)(2,1)S(1)} %slice.34), channel_id=1, source_target_pairs={{0,1},{1,2},{2,3},{3,4},{4,5},{5,6},{6,7},{7,8},{8,9},{9,10},{10,1... | collective-permute-start | bytes 184328 | tf_op jit(solution)/shard_map/ppermute | solution.py:23
  11.9 7.6 %copy-start = (s32[512]{0:T(512)S(1)}, s32[512]{0:T(512)}, u32[]{:S(2)}) copy-start(s32[512]{0:T(512)} %param.9) | copy-start | bytes 6148
  13.5 4.0 %collective-permute-start.1 = (f32[256,384]{1,0:T(8,128)S(1)}, f32[256,384]{1,0:T(8,128)S(1)}, u32[]{:S(2)}, u32[]{:S(2)}) collective-permute-start(f32[256,384]{1,0:T(8,128)S(1)} %dynamic-slice_bitcast_fusion), channel_id=1, source_target_pairs={{0,1},{1,0},{2,3},{3,2},{4,5},{5,4},{6,7},{7,6},{8,9},{9,8},{10,11... | collective-permute-start | bytes 1179656 | tf_op jit(solution)/shard_map/ppermute | solution.py:181
Sparse Core Ops, SparseCore 0:
  18.9 48.8 all-gather.2

commit v16 on v15

--- a/solution.py
+++ b/solution.py
@@ -99,10 +99,12 @@
     height = table_ref.shape[1]
     wanted = lines_ref[...]
     pick = (wanted == lax.broadcasted_iota(jnp.int32, (block, height), 1)).astype(jnp.bfloat16)
-    for w in range(SEGS):
-        source_ref[w] = jnp.dot(pick, table_ref[w], preferred_element_type=jnp.float32)
-
     for part, cross_ref in enumerate(cross_refs):
+        window = slice(part * share, (part + 1) * share)
+        for w in range(SEGS):
+            source_ref[w, window] = jnp.dot(
+                pick[window], table_ref[w], preferred_element_type=jnp.float32
+            )
 
         def one_source(s, carry):
             at = part * share + s

time: 121 us -> 126 us (1.041)
  Pallas kernels: 45.1 us -> 50.1 us
    pallas_call x1, Pallas kernels: 45.1 us -> 50.1 us  [correlate(): pl.pallas_call(correlate_kernel, grid_spec=grid_spec, out_shape=jax.Shape...]
where the time goes in v16:
time: 126 us
  Pallas kernels  50.1 us (40%)
  waiting for transfers between devices  47.6 us (38%)
  between operations  13.5 us (11%)
  starting transfers between devices  5.09 us (4%)
  matrix products  3.38 us (3%)
  other arithmetic  3.26 us (3%)
  local copies, waits for them, and re-layouts  3.25 us (3%)
    pallas_call x1, Pallas kernels, correlate(): pl.pallas_call(correlate_kernel, grid_spec=grid_spec, out_shape=jax.Shape...  50.1 us
    all_gather x1, waiting for transfers between devices, body(): gathered = lax.all_gather(piece, 'chan', axis=0, tiled=False)  46.2 us
    ppermute x1, starting transfers between devices, body(): spectrum = spectrum + lax.ppermute(outgoing, 'chan', route)  2.68 us
  transfers between devices with their start and end apart: 3, of which 2 were waited for; matrix products, arithmetic and copies ran while one was open for 4% of the time, Pallas kernels for 0%

profile of v16, /device:TPU:0, one launch (start us, length us, event | category | flops | bytes accessed | tf_op | source)
XLA Modules:
  0.0 126.2 jit_solution(8022795553605812163)
XLA Ops:
  6.5 0.0 copy-start.1
  6.5 0.0 all-gather.3.cloned.1.call-start
  6.5 1.0 slice.34
  7.6 2.4 %collective-permute-start = (bf16[512,60]{1,0:T(8,128)(2,1)S(1)}, bf16[512,60]{1,0:T(8,128)(2,1)S(1)}, u32[]{:S(2)}, u32[]{:S(2)}) collective-permute-start(bf16[512,60]{1,0:T(8,128)(2,1)S(1)} %slice.34), channel_id=1, source_target_pairs={{0,1},{1,2},{2,3},{3,4},{4,5},{5,6},{6,7},{7,8},{8,9},{9,10},{10,1... | collective-permute-start | bytes 184328 | tf_op jit(solution)/shard_map/ppermute | solution.py:23
  10.0 1.9 %fusion.12 = f32[256,512]{1,0:T(8,128)S(1)} fusion(bf16[1024,256]{1,0:T(8,128)(2,1)} %constant.135, bf16[512,1024]{1,0:T(8,128)(2,1)} %param.8), kind=kOutput, calls=%fused_computation.32 | convolution fusion | flops 268435456 | bytes 2097152 | tf_op jit(solution)/shard_map/dot_general | solution.py:48
  11.9 0.0 copy-start
  11.9 0.0 collective-permute-done
  11.9 1.5 %fusion.1 = f32[512,384]{1,0:T(8,128)S(1)} fusion(f32[256,512]{1,0:T(8,128)S(1)} %fusion.12, bf16[60,256]{1,0:T(8,128)(2,1)} %constant.134, bf16[512,60]{1,0:T(8,128)(2,1)S(1)} %collective-permute-done, bf16[512,384]{1,0:T(8,128)(2,1)} %constant.136, s32[]{:T(128)S(6)} %select_n.44), kind=kOutput, calls=%fused_computation.2 | convolution fusion | flops 116654080 | bytes 1601540 | tf_op jit(solution)/shard_map/dot_general | solution.py:173
  13.5 2.7 %collective-permute-start.1 = (f32[256,384]{1,0:T(8,128)S(1)}, f32[256,384]{1,0:T(8,128)S(1)}, u32[]{:S(2)}, u32[]{:S(2)}) collective-permute-start(f32[256,384]{1,0:T(8,128)S(1)} %dynamic-slice_bitcast_fusion), channel_id=1, source_target_pairs={{0,1},{1,0},{2,3},{3,2},{4,5},{5,4},{6,7},{7,6},{8,9},{9,8},{10,11... | collective-permute-start | bytes 1179656 | tf_op jit(solution)/shard_map/ppermute | solution.py:183
  16.1 0.0 copy-done.1
  16.1 1.3 %collective-permute-done.1 = f32[256,384]{1,0:T(8,128)S(1)} collective-permute-done((f32[256,384]{1,0:T(8,128)S(1)}, f32[256,384]{1,0:T(8,128)S(1)}, u32[]{:S(2)}, u32[]{:S(2)}) %collective-permute-start.1) | collective-permute-done | bytes 393248 | tf_op jit(solution)/shard_map/ppermute | solution.py:183
  17.5 0.2 fusion.11
  17.8 0.2 multiply_convert_fusion.1
  18.0 0.8 fusion.3
  18.7 0.0 all-gather.3.cloned.1.call-update
  18.8 0.7 copy.9.own_ref
  19.5 0.0 copy-done
  19.5 0.6 fusion.7
  20.1 0.9 copy.8.lines_ref
  20.9 0.6 pad_add_fusion.place_ref
  21.6 46.2 %all-gather.3.cloned.1.call-done = bf16[4352,384]{1,0:T(8,128)(2,1)} async-done(((bf16[272,384]{1,0:T(8,128)(2,1)}), bf16[4352,384]{1,0:T(8,128)(2,1)}) %all-gather.3.cloned.1.call-update) | async-done | bytes 3342352 | tf_op jit(solution)/shard_map/all_gather | solution.py:188
  67.8 0.8 fusion.5
  68.6 0.6 reshape.49.flags_ref
  69.2 50.1 %shard_map.64 = bf16[512,32,256]{2,1,0:T(8,128)(2,1)} custom-call(s32[512]{0:T(512)} %reshape.49.flags_ref, s32[512]{0:T(512)} %get-tuple-element.20.picked_ref, s32[2]{0:T(128)} %pad_add_fusion.place_ref, s32[512,1]{1,0:T(8,128)} %copy.8.lines_ref, bf16[8,544,384]{2,1,0:T(8,128)(2,1)} %bitcast.20, bf16[8,2,272,384]{3,2,1,0:T(8,128)(2,1)} %bitcast.21, ...), custom_call_target="tpu_custom_call" | custom-call | tf_op jit(solution)/shard_map/pallas_call | solution.py:152
  (4 shorter events, 0.1 us)
Async XLA Ops:
  6.5 9.6 %copy-start.1 = (s32[32]{0:T(128)S(1)}, s32[32]{0:T(128)}, u32[]{:S(2)}) copy-start(s32[32]{0:T(128)} %param.10) | copy-start | bytes 388
  6.5 61.3 %all-gather.3.cloned.1.call-start = ((), (), s32[]{:S(2)}) async-start(), calls=%async_computation | async-start | bytes 3551232 | tf_op jit(solution)/shard_map/all_gather | solution.py:188
  7.6 4.3 %collective-permute-start = (bf16[512,60]{1,0:T(8,128)(2,1)S(1)}, bf16[512,60]{1,0:T(8,128)(2,1)S(1)}, u32[]{:S(2)}, u32[]{:S(2)}) collective-permute-start(bf16[512,60]{1,0:T(8,128)(2,1)S(1)} %slice.34), channel_id=1, source_target_pairs={{0,1},{1,2},{2,3},{3,4},{4,5},{5,6},{6,7},{7,8},{8,9},{9,10},{10,1... | collective-permute-start | bytes 184328 | tf_op jit(solution)/shard_map/ppermute | solution.py:23
  11.9 7.6 %copy-start = (s32[512]{0:T(512)S(1)}, s32[512]{0:T(512)}, u32[]{:S(2)}) copy-start(s32[512]{0:T(512)} %param.9) | copy-start | bytes 6148
  13.5 4.0 %collective-permute-start.1 = (f32[256,384]{1,0:T(8,128)S(1)}, f32[256,384]{1,0:T(8,128)S(1)}, u32[]{:S(2)}, u32[]{:S(2)}) collective-permute-start(f32[256,384]{1,0:T(8,128)S(1)} %dynamic-slice_bitcast_fusion), channel_id=1, source_target_pairs={{0,1},{1,0},{2,3},{3,2},{4,5},{5,4},{6,7},{7,6},{8,9},{9,8},{10,11... | collective-permute-start | bytes 1179656 | tf_op jit(solution)/shard_map/ppermute | solution.py:183
Sparse Core Ops, SparseCore 0:
  18.9 48.8 all-gather.2

commit v17 on v15

--- a/solution.py
+++ b/solution.py
@@ -97,10 +97,21 @@
             swapped_ref[w] = jnp.where(lower, turned, -spectra)
 
     height = table_ref.shape[1]
-    wanted = lines_ref[...]
-    pick = (wanted == lax.broadcasted_iota(jnp.int32, (block, height), 1)).astype(jnp.bfloat16)
-    for w in range(SEGS):
-        source_ref[w] = jnp.dot(pick, table_ref[w], preferred_element_type=jnp.float32)
+    step = pl.program_id(0)
+
+    def select(at, slot):
+        start = pl.multiple_of(at * block, block)
+        wanted = lines_ref[pl.ds(start, block), :]
+        pick = (wanted == lax.broadcasted_iota(jnp.int32, (block, height), 1)).astype(jnp.bfloat16)
+        for w in range(SEGS):
+            source_ref[slot, w] = jnp.dot(pick, table_ref[w], preferred_element_type=jnp.float32)
+
+    @pl.when(step == 0)
+    def _():
+        select(0, 0)
+
+    slot = step % 2
+    select(jnp.minimum(step + 1, pl.num_programs(0) - 1), 1 - slot)
 
     for part, cross_ref in enumerate(cross_refs):
 
@@ -109,7 +120,7 @@
             direct = jnp.zeros((receivers, 2 * NF), jnp.float32)
             crossed = jnp.zeros((receivers, 2 * NF), jnp.float32)
             for w in range(SEGS):
-                row = source_ref[w, pl.ds(at, 1), :]
+                row = source_ref[slot, w, pl.ds(at, 1), :]
                 direct = direct + row * plain_ref[w]
                 crossed = crossed + row * swapped_ref[w]
             flag = flags_ref[picked_ref[pl.program_id(0) * block + at]].astype(jnp.float32)
@@ -133,7 +144,7 @@
         num_scalar_prefetch=3,
         grid=(source_count // block,),
         in_specs=[
-            pl.BlockSpec((block, 1), lambda i, f, p, q: (i, 0)),
+            pl.BlockSpec((source_count, 1), lambda i, f, p, q: (0, 0)),
             pl.BlockSpec(table.shape, lambda i, f, p, q: (0, 0, 0)),
             pl.BlockSpec((SEGS, 1, recv_count, 2 * NF), lambda i, f, p, q: (0, q[0], q[1], 0)),
             pl.BlockSpec((recv_count, 1), lambda i, f, p, q: (0, 0)),
@@ -143,7 +154,7 @@
         scratch_shapes=[
             pltpu.VMEM((SEGS, recv_count, 2 * NF), jnp.float32),
             pltpu.VMEM((SEGS, recv_count, 2 * NF), jnp.float32),
-            pltpu.VMEM((SEGS, block, 2 * NF), jnp.float32),
+            pltpu.VMEM((2, SEGS, block, 2 * NF), jnp.float32),
         ]
         + [pltpu.VMEM((block // parts * recv_count, 2 * NF), jnp.bfloat16)] * parts,
     )

time: 121 us -> 121 us (level)
  no operation moved by 1% of the time
where the time goes in v17:
time: 121 us
  waiting for transfers between devices  47.6 us (39%)
  Pallas kernels  44.8 us (37%)
  between operations  13.5 us (11%)
  starting transfers between devices  5.09 us (4%)
  matrix products  3.38 us (3%)
  other arithmetic  3.26 us (3%)
  local copies, waits for them, and re-layouts  3.25 us (3%)
    all_gather x1, waiting for transfers between devices, body(): gathered = lax.all_gather(piece, 'chan', axis=0, tiled=False)  46.2 us
    pallas_call x1, Pallas kernels, correlate(): pl.pallas_call(correlate_kernel, grid_spec=grid_spec, out_shape=jax.Shape...  44.8 us
    ppermute x1, starting transfers between devices, body(): spectrum = spectrum + lax.ppermute(outgoing, 'chan', route)  2.68 us
  transfers between devices with their start and end apart: 3, of which 2 were waited for; matrix products, arithmetic and copies ran while one was open for 4% of the time, Pallas kernels for 0%

profile of v17, /device:TPU:0, one launch (start us, length us, event | category | flops | bytes accessed | tf_op | source)
XLA Modules:
  0.0 120.9 jit_solution(1228200445741838646)
XLA Ops:
  6.5 0.0 copy-start.1
  6.5 0.0 all-gather.3.cloned.1.call-start
  6.5 1.0 slice.34
  7.6 2.4 %collective-permute-start = (bf16[512,60]{1,0:T(8,128)(2,1)S(1)}, bf16[512,60]{1,0:T(8,128)(2,1)S(1)}, u32[]{:S(2)}, u32[]{:S(2)}) collective-permute-start(bf16[512,60]{1,0:T(8,128)(2,1)S(1)} %slice.34), channel_id=1, source_target_pairs={{0,1},{1,2},{2,3},{3,4},{4,5},{5,6},{6,7},{7,8},{8,9},{9,10},{10,1... | collective-permute-start | bytes 184328 | tf_op jit(solution)/shard_map/ppermute | solution.py:23
  10.0 1.9 %fusion.12 = f32[256,512]{1,0:T(8,128)S(1)} fusion(bf16[1024,256]{1,0:T(8,128)(2,1)} %constant.135, bf16[512,1024]{1,0:T(8,128)(2,1)} %param.8), kind=kOutput, calls=%fused_computation.32 | convolution fusion | flops 268435456 | bytes 2097152 | tf_op jit(solution)/shard_map/dot_general | solution.py:48
  11.9 0.0 copy-start
  11.9 0.0 collective-permute-done
  11.9 1.5 %fusion.1 = f32[512,384]{1,0:T(8,128)S(1)} fusion(f32[256,512]{1,0:T(8,128)S(1)} %fusion.12, bf16[60,256]{1,0:T(8,128)(2,1)} %constant.134, bf16[512,60]{1,0:T(8,128)(2,1)S(1)} %collective-permute-done, bf16[512,384]{1,0:T(8,128)(2,1)} %constant.136, s32[]{:T(128)S(6)} %select_n.44), kind=kOutput, calls=%fused_computation.2 | convolution fusion | flops 116654080 | bytes 1601540 | tf_op jit(solution)/shard_map/dot_general | solution.py:182
  13.5 2.7 %collective-permute-start.1 = (f32[256,384]{1,0:T(8,128)S(1)}, f32[256,384]{1,0:T(8,128)S(1)}, u32[]{:S(2)}, u32[]{:S(2)}) collective-permute-start(f32[256,384]{1,0:T(8,128)S(1)} %dynamic-slice_bitcast_fusion), channel_id=1, source_target_pairs={{0,1},{1,0},{2,3},{3,2},{4,5},{5,4},{6,7},{7,6},{8,9},{9,8},{10,11... | collective-permute-start | bytes 1179656 | tf_op jit(solution)/shard_map/ppermute | solution.py:192
  16.1 0.0 copy-done.1
  16.1 1.3 %collective-permute-done.1 = f32[256,384]{1,0:T(8,128)S(1)} collective-permute-done((f32[256,384]{1,0:T(8,128)S(1)}, f32[256,384]{1,0:T(8,128)S(1)}, u32[]{:S(2)}, u32[]{:S(2)}) %collective-permute-start.1) | collective-permute-done | bytes 393248 | tf_op jit(solution)/shard_map/ppermute | solution.py:192
  17.5 0.2 fusion.11
  17.8 0.2 multiply_convert_fusion.1
  18.0 0.8 fusion.3
  18.7 0.0 all-gather.3.cloned.1.call-update
  18.8 0.7 copy.9.own_ref
  19.5 0.0 copy-done
  19.5 0.6 fusion.7
  20.1 0.9 copy.8.lines_ref
  20.9 0.6 pad_add_fusion.place_ref
  21.6 46.2 %all-gather.3.cloned.1.call-done = bf16[4352,384]{1,0:T(8,128)(2,1)} async-done(((bf16[272,384]{1,0:T(8,128)(2,1)}), bf16[4352,384]{1,0:T(8,128)(2,1)}) %all-gather.3.cloned.1.call-update) | async-done | bytes 3342352 | tf_op jit(solution)/shard_map/all_gather | solution.py:197
  67.8 0.8 fusion.5
  68.6 0.6 reshape.49.flags_ref
  69.2 44.8 %shard_map.64 = bf16[512,32,256]{2,1,0:T(8,128)(2,1)} custom-call(s32[512]{0:T(512)} %reshape.49.flags_ref, s32[512]{0:T(512)} %get-tuple-element.20.picked_ref, s32[2]{0:T(128)} %pad_add_fusion.place_ref, s32[512,1]{1,0:T(8,128)} %copy.8.lines_ref, bf16[8,544,384]{2,1,0:T(8,128)(2,1)} %bitcast.20, bf16[8,2,272,384]{3,2,1,0:T(8,128)(2,1)} %bitcast.21, ...), custom_call_target="tpu_custom_call" | custom-call | tf_op jit(solution)/shard_map/pallas_call | solution.py:161
  (4 shorter events, 0.1 us)
Async XLA Ops:
  6.5 9.6 %copy-start.1 = (s32[32]{0:T(128)S(1)}, s32[32]{0:T(128)}, u32[]{:S(2)}) copy-start(s32[32]{0:T(128)} %param.10) | copy-start | bytes 388
  6.5 61.3 %all-gather.3.cloned.1.call-start = ((), (), s32[]{:S(2)}) async-start(), calls=%async_computation | async-start | bytes 3551232 | tf_op jit(solution)/shard_map/all_gather | solution.py:197
  7.6 4.3 %collective-permute-start = (bf16[512,60]{1,0:T(8,128)(2,1)S(1)}, bf16[512,60]{1,0:T(8,128)(2,1)S(1)}, u32[]{:S(2)}, u32[]{:S(2)}) collective-permute-start(bf16[512,60]{1,0:T(8,128)(2,1)S(1)} %slice.34), channel_id=1, source_target_pairs={{0,1},{1,2},{2,3},{3,4},{4,5},{5,6},{6,7},{7,8},{8,9},{9,10},{10,1... | collective-permute-start | bytes 184328 | tf_op jit(solution)/shard_map/ppermute | solution.py:23
  11.9 7.6 %copy-start = (s32[512]{0:T(512)S(1)}, s32[512]{0:T(512)}, u32[]{:S(2)}) copy-start(s32[512]{0:T(512)} %param.9) | copy-start | bytes 6148
  13.5 4.0 %collective-permute-start.1 = (f32[256,384]{1,0:T(8,128)S(1)}, f32[256,384]{1,0:T(8,128)S(1)}, u32[]{:S(2)}, u32[]{:S(2)}) collective-permute-start(f32[256,384]{1,0:T(8,128)S(1)} %dynamic-slice_bitcast_fusion), channel_id=1, source_target_pairs={{0,1},{1,0},{2,3},{3,2},{4,5},{5,4},{6,7},{7,6},{8,9},{9,8},{10,11... | collective-permute-start | bytes 1179656 | tf_op jit(solution)/shard_map/ppermute | solution.py:192
Sparse Core Ops, SparseCore 0:
  18.9 48.8 all-gather.2

commit v18 on v17

--- a/solution.py
+++ b/solution.py
@@ -137,7 +137,7 @@
         )
 
 
-def correlate(table, lines, flags_all, picked, place, blocks, own_flags, delays, block=64, parts=2):
+def correlate(table, lines, flags_all, picked, place, blocks, own_flags, delays, block=128, parts=2):
     source_count = picked.shape[0]
     recv_count = own_flags.shape[0]
     grid_spec = pltpu.PrefetchScalarGridSpec(

time: 121 us -> 120 us (level)
  no operation moved by 1% of the time
where the time goes in v18:
time: 120 us
  waiting for transfers between devices  47.6 us (40%)
  Pallas kernels  44 us (37%)
  between operations  13.5 us (11%)
  starting transfers between devices  5.09 us (4%)
  matrix products  3.38 us (3%)
  other arithmetic  3.26 us (3%)
  local copies, waits for them, and re-layouts  3.25 us (3%)
    all_gather x1, waiting for transfers between devices, body(): gathered = lax.all_gather(piece, 'chan', axis=0, tiled=False)  46.2 us
    pallas_call x1, Pallas kernels, correlate(): pl.pallas_call(correlate_kernel, grid_spec=grid_spec, out_shape=jax.Shape...  44 us
    ppermute x1, starting transfers between devices, body(): spectrum = spectrum + lax.ppermute(outgoing, 'chan', route)  2.68 us
    ppermute x1, starting transfers between devices, from_behind(): return lax.ppermute(block, axis, route)  2.4 us
  transfers between devices with their start and end apart: 3, of which 2 were waited for; matrix products, arithmetic and copies ran while one was open for 4% of the time, Pallas kernels for 0%

profile of v18, /device:TPU:0, one launch (start us, length us, event | category | flops | bytes accessed | tf_op | source)
XLA Modules:
  0.0 120.1 jit_solution(3115816103007757889)
XLA Ops:
  6.5 0.0 copy-start.1
  6.5 0.0 all-gather.3.cloned.1.call-start
  6.5 1.0 slice.34
  7.6 2.4 %collective-permute-start = (bf16[512,60]{1,0:T(8,128)(2,1)S(1)}, bf16[512,60]{1,0:T(8,128)(2,1)S(1)}, u32[]{:S(2)}, u32[]{:S(2)}) collective-permute-start(bf16[512,60]{1,0:T(8,128)(2,1)S(1)} %slice.34), channel_id=1, source_target_pairs={{0,1},{1,2},{2,3},{3,4},{4,5},{5,6},{6,7},{7,8},{8,9},{9,10},{10,1... | collective-permute-start | bytes 184328 | tf_op jit(solution)/shard_map/ppermute | solution.py:23
  10.0 1.9 %fusion.12 = f32[256,512]{1,0:T(8,128)S(1)} fusion(bf16[1024,256]{1,0:T(8,128)(2,1)} %constant.135, bf16[512,1024]{1,0:T(8,128)(2,1)} %param.8), kind=kOutput, calls=%fused_computation.32 | convolution fusion | flops 268435456 | bytes 2097152 | tf_op jit(solution)/shard_map/dot_general | solution.py:48
  11.9 0.0 copy-start
  11.9 0.0 collective-permute-done
  11.9 1.5 %fusion.1 = f32[512,384]{1,0:T(8,128)S(1)} fusion(f32[256,512]{1,0:T(8,128)S(1)} %fusion.12, bf16[60,256]{1,0:T(8,128)(2,1)} %constant.134, bf16[512,60]{1,0:T(8,128)(2,1)S(1)} %collective-permute-done, bf16[512,384]{1,0:T(8,128)(2,1)} %constant.136, s32[]{:T(128)S(6)} %select_n.44), kind=kOutput, calls=%fused_computation.2 | convolution fusion | flops 116654080 | bytes 1601540 | tf_op jit(solution)/shard_map/dot_general | solution.py:182
  13.5 2.7 %collective-permute-start.1 = (f32[256,384]{1,0:T(8,128)S(1)}, f32[256,384]{1,0:T(8,128)S(1)}, u32[]{:S(2)}, u32[]{:S(2)}) collective-permute-start(f32[256,384]{1,0:T(8,128)S(1)} %dynamic-slice_bitcast_fusion), channel_id=1, source_target_pairs={{0,1},{1,0},{2,3},{3,2},{4,5},{5,4},{6,7},{7,6},{8,9},{9,8},{10,11... | collective-permute-start | bytes 1179656 | tf_op jit(solution)/shard_map/ppermute | solution.py:192
  16.1 0.0 copy-done.1
  16.1 1.3 %collective-permute-done.1 = f32[256,384]{1,0:T(8,128)S(1)} collective-permute-done((f32[256,384]{1,0:T(8,128)S(1)}, f32[256,384]{1,0:T(8,128)S(1)}, u32[]{:S(2)}, u32[]{:S(2)}) %collective-permute-start.1) | collective-permute-done | bytes 393248 | tf_op jit(solution)/shard_map/ppermute | solution.py:192
  17.5 0.2 fusion.11
  17.8 0.2 multiply_convert_fusion.1
  18.0 0.8 fusion.3
  18.7 0.0 all-gather.3.cloned.1.call-update
  18.8 0.7 copy.9.own_ref
  19.5 0.0 copy-done
  19.5 0.6 fusion.7
  20.1 0.9 copy.8.lines_ref
  20.9 0.6 pad_add_fusion.place_ref
  21.6 46.2 %all-gather.3.cloned.1.call-done = bf16[4352,384]{1,0:T(8,128)(2,1)} async-done(((bf16[272,384]{1,0:T(8,128)(2,1)}), bf16[4352,384]{1,0:T(8,128)(2,1)}) %all-gather.3.cloned.1.call-update) | async-done | bytes 3342352 | tf_op jit(solution)/shard_map/all_gather | solution.py:197
  67.8 0.8 fusion.5
  68.6 0.6 reshape.49.flags_ref
  69.2 44.0 %shard_map.64 = bf16[512,32,256]{2,1,0:T(8,128)(2,1)} custom-call(s32[512]{0:T(512)} %reshape.49.flags_ref, s32[512]{0:T(512)} %get-tuple-element.20.picked_ref, s32[2]{0:T(128)} %pad_add_fusion.place_ref, s32[512,1]{1,0:T(8,128)} %copy.8.lines_ref, bf16[8,544,384]{2,1,0:T(8,128)(2,1)} %bitcast.20, bf16[8,2,272,384]{3,2,1,0:T(8,128)(2,1)} %bitcast.21, ...), custom_call_target="tpu_custom_call" | custom-call | tf_op jit(solution)/shard_map/pallas_call | solution.py:161
  (4 shorter events, 0.1 us)
Async XLA Ops:
  6.5 9.6 %copy-start.1 = (s32[32]{0:T(128)S(1)}, s32[32]{0:T(128)}, u32[]{:S(2)}) copy-start(s32[32]{0:T(128)} %param.10) | copy-start | bytes 388
  6.5 61.3 %all-gather.3.cloned.1.call-start = ((), (), s32[]{:S(2)}) async-start(), calls=%async_computation | async-start | bytes 3551232 | tf_op jit(solution)/shard_map/all_gather | solution.py:197
  7.6 4.3 %collective-permute-start = (bf16[512,60]{1,0:T(8,128)(2,1)S(1)}, bf16[512,60]{1,0:T(8,128)(2,1)S(1)}, u32[]{:S(2)}, u32[]{:S(2)}) collective-permute-start(bf16[512,60]{1,0:T(8,128)(2,1)S(1)} %slice.34), channel_id=1, source_target_pairs={{0,1},{1,2},{2,3},{3,4},{4,5},{5,6},{6,7},{7,8},{8,9},{9,10},{10,1... | collective-permute-start | bytes 184328 | tf_op jit(solution)/shard_map/ppermute | solution.py:23
  11.9 7.6 %copy-start = (s32[512]{0:T(512)S(1)}, s32[512]{0:T(512)}, u32[]{:S(2)}) copy-start(s32[512]{0:T(512)} %param.9) | copy-start | bytes 6148
  13.5 4.0 %collective-permute-start.1 = (f32[256,384]{1,0:T(8,128)S(1)}, f32[256,384]{1,0:T(8,128)S(1)}, u32[]{:S(2)}, u32[]{:S(2)}) collective-permute-start(f32[256,384]{1,0:T(8,128)S(1)} %dynamic-slice_bitcast_fusion), channel_id=1, source_target_pairs={{0,1},{1,0},{2,3},{3,2},{4,5},{5,4},{6,7},{7,6},{8,9},{9,8},{10,11... | collective-permute-start | bytes 1179656 | tf_op jit(solution)/shard_map/ppermute | solution.py:192
Sparse Core Ops, SparseCore 0:
  18.9 48.8 all-gather.2

commit v19 on v18

--- a/solution.py
+++ b/solution.py
@@ -137,7 +137,7 @@
         )
 
 
-def correlate(table, lines, flags_all, picked, place, blocks, own_flags, delays, block=128, parts=2):
+def correlate(table, lines, flags_all, picked, place, blocks, own_flags, delays, block=128, parts=4):
     source_count = picked.shape[0]
     recv_count = own_flags.shape[0]
     grid_spec = pltpu.PrefetchScalarGridSpec(

time: 120 us -> 120 us (level)
  no operation moved by 1% of the time
where the time goes in v19:
time: 120 us; the launch traced here: 119 us
  waiting for transfers between devices  47.6 us (40%)
  Pallas kernels  43.2 us (36%)
  between operations  13.5 us (11%)
  starting transfers between devices  5.09 us (4%)
  matrix products  3.38 us (3%)
  other arithmetic  3.26 us (3%)
  local copies, waits for them, and re-layouts  3.25 us (3%)
    all_gather x1, waiting for transfers between devices, body(): gathered = lax.all_gather(piece, 'chan', axis=0, tiled=False)  46.2 us
    pallas_call x1, Pallas kernels, correlate(): pl.pallas_call(correlate_kernel, grid_spec=grid_spec, out_shape=jax.Shape...  43.2 us
    ppermute x1, starting transfers between devices, body(): spectrum = spectrum + lax.ppermute(outgoing, 'chan', route)  2.68 us
    ppermute x1, starting transfers between devices, from_behind(): return lax.ppermute(block, axis, route)  2.4 us
  transfers between devices with their start and end apart: 3, of which 2 were waited for; matrix products, arithmetic and copies ran while one was open for 4% of the time, Pallas kernels for 0%

profile of v19, /device:TPU:0, one launch (start us, length us, event | category | flops | bytes accessed | tf_op | source)
XLA Modules:
  0.0 119.3 jit_solution(6286972333496659617)
XLA Ops:
  6.5 0.0 copy-start.1
  6.5 0.0 all-gather.3.cloned.1.call-start
  6.5 1.0 slice.34
  7.6 2.4 %collective-permute-start = (bf16[512,60]{1,0:T(8,128)(2,1)S(1)}, bf16[512,60]{1,0:T(8,128)(2,1)S(1)}, u32[]{:S(2)}, u32[]{:S(2)}) collective-permute-start(bf16[512,60]{1,0:T(8,128)(2,1)S(1)} %slice.34), channel_id=1, source_target_pairs={{0,1},{1,2},{2,3},{3,4},{4,5},{5,6},{6,7},{7,8},{8,9},{9,10},{10,1... | collective-permute-start | bytes 184328 | tf_op jit(solution)/shard_map/ppermute | solution.py:23
  10.0 1.9 %fusion.12 = f32[256,512]{1,0:T(8,128)S(1)} fusion(bf16[1024,256]{1,0:T(8,128)(2,1)} %constant.135, bf16[512,1024]{1,0:T(8,128)(2,1)} %param.8), kind=kOutput, calls=%fused_computation.32 | convolution fusion | flops 268435456 | bytes 2097152 | tf_op jit(solution)/shard_map/dot_general | solution.py:48
  11.9 0.0 copy-start
  11.9 0.0 collective-permute-done
  11.9 1.5 %fusion.1 = f32[512,384]{1,0:T(8,128)S(1)} fusion(f32[256,512]{1,0:T(8,128)S(1)} %fusion.12, bf16[60,256]{1,0:T(8,128)(2,1)} %constant.134, bf16[512,60]{1,0:T(8,128)(2,1)S(1)} %collective-permute-done, bf16[512,384]{1,0:T(8,128)(2,1)} %constant.136, s32[]{:T(128)S(6)} %select_n.44), kind=kOutput, calls=%fused_computation.2 | convolution fusion | flops 116654080 | bytes 1601540 | tf_op jit(solution)/shard_map/dot_general | solution.py:182
  13.5 2.7 %collective-permute-start.1 = (f32[256,384]{1,0:T(8,128)S(1)}, f32[256,384]{1,0:T(8,128)S(1)}, u32[]{:S(2)}, u32[]{:S(2)}) collective-permute-start(f32[256,384]{1,0:T(8,128)S(1)} %dynamic-slice_bitcast_fusion), channel_id=1, source_target_pairs={{0,1},{1,0},{2,3},{3,2},{4,5},{5,4},{6,7},{7,6},{8,9},{9,8},{10,11... | collective-permute-start | bytes 1179656 | tf_op jit(solution)/shard_map/ppermute | solution.py:192
  16.1 0.0 copy-done.1
  16.1 1.3 %collective-permute-done.1 = f32[256,384]{1,0:T(8,128)S(1)} collective-permute-done((f32[256,384]{1,0:T(8,128)S(1)}, f32[256,384]{1,0:T(8,128)S(1)}, u32[]{:S(2)}, u32[]{:S(2)}) %collective-permute-start.1) | collective-permute-done | bytes 393248 | tf_op jit(solution)/shard_map/ppermute | solution.py:192
  17.5 0.2 fusion.11
  17.8 0.2 multiply_convert_fusion.1
  18.0 0.8 fusion.3
  18.7 0.0 all-gather.3.cloned.1.call-update
  18.8 0.7 copy.9.own_ref
  19.5 0.0 copy-done
  19.5 0.6 fusion.7
  20.1 0.9 copy.8.lines_ref
  20.9 0.6 pad_add_fusion.place_ref
  21.6 46.2 %all-gather.3.cloned.1.call-done = bf16[4352,384]{1,0:T(8,128)(2,1)} async-done(((bf16[272,384]{1,0:T(8,128)(2,1)}), bf16[4352,384]{1,0:T(8,128)(2,1)}) %all-gather.3.cloned.1.call-update) | async-done | bytes 3342352 | tf_op jit(solution)/shard_map/all_gather | solution.py:197
  67.8 0.8 fusion.5
  68.6 0.6 reshape.49.flags_ref
  69.2 43.2 %shard_map.64 = bf16[512,32,256]{2,1,0:T(8,128)(2,1)} custom-call(s32[512]{0:T(512)} %reshape.49.flags_ref, s32[512]{0:T(512)} %get-tuple-element.20.picked_ref, s32[2]{0:T(128)} %pad_add_fusion.place_ref, s32[512,1]{1,0:T(8,128)} %copy.8.lines_ref, bf16[8,544,384]{2,1,0:T(8,128)(2,1)} %bitcast.20, bf16[8,2,272,384]{3,2,1,0:T(8,128)(2,1)} %bitcast.21, ...), custom_call_target="tpu_custom_call" | custom-call | tf_op jit(solution)/shard_map/pallas_call | solution.py:161
  (4 shorter events, 0.1 us)
Async XLA Ops:
  6.5 9.6 %copy-start.1 = (s32[32]{0:T(128)S(1)}, s32[32]{0:T(128)}, u32[]{:S(2)}) copy-start(s32[32]{0:T(128)} %param.10) | copy-start | bytes 388
  6.5 61.3 %all-gather.3.cloned.1.call-start = ((), (), s32[]{:S(2)}) async-start(), calls=%async_computation | async-start | bytes 3551232 | tf_op jit(solution)/shard_map/all_gather | solution.py:197
  7.6 4.3 %collective-permute-start = (bf16[512,60]{1,0:T(8,128)(2,1)S(1)}, bf16[512,60]{1,0:T(8,128)(2,1)S(1)}, u32[]{:S(2)}, u32[]{:S(2)}) collective-permute-start(bf16[512,60]{1,0:T(8,128)(2,1)S(1)} %slice.34), channel_id=1, source_target_pairs={{0,1},{1,2},{2,3},{3,4},{4,5},{5,6},{6,7},{7,8},{8,9},{9,10},{10,1... | collective-permute-start | bytes 184328 | tf_op jit(solution)/shard_map/ppermute | solution.py:23
  11.9 7.6 %copy-start = (s32[512]{0:T(512)S(1)}, s32[512]{0:T(512)}, u32[]{:S(2)}) copy-start(s32[512]{0:T(512)} %param.9) | copy-start | bytes 6148
  13.5 4.0 %collective-permute-start.1 = (f32[256,384]{1,0:T(8,128)S(1)}, f32[256,384]{1,0:T(8,128)S(1)}, u32[]{:S(2)}, u32[]{:S(2)}) collective-permute-start(f32[256,384]{1,0:T(8,128)S(1)} %dynamic-slice_bitcast_fusion), channel_id=1, source_target_pairs={{0,1},{1,0},{2,3},{3,2},{4,5},{5,4},{6,7},{7,6},{8,9},{9,8},{10,11... | collective-permute-start | bytes 1179656 | tf_op jit(solution)/shard_map/ppermute | solution.py:192
Sparse Core Ops, SparseCore 0:
  18.9 48.8 all-gather.2

commit v20 on v19

--- a/solution.py
+++ b/solution.py
@@ -137,7 +137,7 @@
         )
 
 
-def correlate(table, lines, flags_all, picked, place, blocks, own_flags, delays, block=128, parts=4):
+def correlate(table, lines, flags_all, picked, place, blocks, own_flags, delays, block=128, parts=8):
     source_count = picked.shape[0]
     recv_count = own_flags.shape[0]
     grid_spec = pltpu.PrefetchScalarGridSpec(

time: 120 us -> 119 us (level)
  no operation moved by 1% of the time
where the time goes in v20:
time: 119 us
  waiting for transfers between devices  47.6 us (40%)
  Pallas kernels  42.6 us (36%)
  between operations  13.5 us (11%)
  starting transfers between devices  5.09 us (4%)
  matrix products  3.38 us (3%)
  other arithmetic  3.26 us (3%)
  local copies, waits for them, and re-layouts  3.25 us (3%)
    all_gather x1, waiting for transfers between devices, body(): gathered = lax.all_gather(piece, 'chan', axis=0, tiled=False)  46.2 us
    pallas_call x1, Pallas kernels, correlate(): pl.pallas_call(correlate_kernel, grid_spec=grid_spec, out_shape=jax.Shape...  42.6 us
    ppermute x1, starting transfers between devices, body(): spectrum = spectrum + lax.ppermute(outgoing, 'chan', route)  2.68 us
    ppermute x1, starting transfers between devices, from_behind(): return lax.ppermute(block, axis, route)  2.4 us
  transfers between devices with their start and end apart: 3, of which 2 were waited for; matrix products, arithmetic and copies ran while one was open for 4% of the time, Pallas kernels for 0%

profile of v20, /device:TPU:0, one launch (start us, length us, event | category | flops | bytes accessed | tf_op | source)
XLA Modules:
  0.0 118.7 jit_solution(17148451813820817337)
XLA Ops:
  6.5 0.0 copy-start.1
  6.5 0.0 all-gather.3.cloned.1.call-start
  6.5 1.0 slice.34
  7.6 2.4 %collective-permute-start = (bf16[512,60]{1,0:T(8,128)(2,1)S(1)}, bf16[512,60]{1,0:T(8,128)(2,1)S(1)}, u32[]{:S(2)}, u32[]{:S(2)}) collective-permute-start(bf16[512,60]{1,0:T(8,128)(2,1)S(1)} %slice.34), channel_id=1, source_target_pairs={{0,1},{1,2},{2,3},{3,4},{4,5},{5,6},{6,7},{7,8},{8,9},{9,10},{10,1... | collective-permute-start | bytes 184328 | tf_op jit(solution)/shard_map/ppermute | solution.py:23
  10.0 1.9 %fusion.12 = f32[256,512]{1,0:T(8,128)S(1)} fusion(bf16[1024,256]{1,0:T(8,128)(2,1)} %constant.135, bf16[512,1024]{1,0:T(8,128)(2,1)} %param.8), kind=kOutput, calls=%fused_computation.32 | convolution fusion | flops 268435456 | bytes 2097152 | tf_op jit(solution)/shard_map/dot_general | solution.py:48
  11.9 0.0 copy-start
  11.9 0.0 collective-permute-done
  11.9 1.5 %fusion.1 = f32[512,384]{1,0:T(8,128)S(1)} fusion(f32[256,512]{1,0:T(8,128)S(1)} %fusion.12, bf16[60,256]{1,0:T(8,128)(2,1)} %constant.134, bf16[512,60]{1,0:T(8,128)(2,1)S(1)} %collective-permute-done, bf16[512,384]{1,0:T(8,128)(2,1)} %constant.136, s32[]{:T(128)S(6)} %select_n.44), kind=kOutput, calls=%fused_computation.2 | convolution fusion | flops 116654080 | bytes 1601540 | tf_op jit(solution)/shard_map/dot_general | solution.py:182
  13.5 2.7 %collective-permute-start.1 = (f32[256,384]{1,0:T(8,128)S(1)}, f32[256,384]{1,0:T(8,128)S(1)}, u32[]{:S(2)}, u32[]{:S(2)}) collective-permute-start(f32[256,384]{1,0:T(8,128)S(1)} %dynamic-slice_bitcast_fusion), channel_id=1, source_target_pairs={{0,1},{1,0},{2,3},{3,2},{4,5},{5,4},{6,7},{7,6},{8,9},{9,8},{10,11... | collective-permute-start | bytes 1179656 | tf_op jit(solution)/shard_map/ppermute | solution.py:192
  16.1 0.0 copy-done.1
  16.1 1.3 %collective-permute-done.1 = f32[256,384]{1,0:T(8,128)S(1)} collective-permute-done((f32[256,384]{1,0:T(8,128)S(1)}, f32[256,384]{1,0:T(8,128)S(1)}, u32[]{:S(2)}, u32[]{:S(2)}) %collective-permute-start.1) | collective-permute-done | bytes 393248 | tf_op jit(solution)/shard_map/ppermute | solution.py:192
  17.5 0.2 fusion.11
  17.8 0.2 multiply_convert_fusion.1
  18.0 0.8 fusion.3
  18.7 0.0 all-gather.3.cloned.1.call-update
  18.8 0.7 copy.9.own_ref
  19.5 0.0 copy-done
  19.5 0.6 fusion.7
  20.1 0.9 copy.8.lines_ref
  20.9 0.6 pad_add_fusion.place_ref
  21.6 46.2 %all-gather.3.cloned.1.call-done = bf16[4352,384]{1,0:T(8,128)(2,1)} async-done(((bf16[272,384]{1,0:T(8,128)(2,1)}), bf16[4352,384]{1,0:T(8,128)(2,1)}) %all-gather.3.cloned.1.call-update) | async-done | bytes 3342352 | tf_op jit(solution)/shard_map/all_gather | solution.py:197
  67.8 0.8 fusion.5
  68.6 0.6 reshape.49.flags_ref
  69.2 42.6 %shard_map.64 = bf16[512,32,256]{2,1,0:T(8,128)(2,1)} custom-call(s32[512]{0:T(512)} %reshape.49.flags_ref, s32[512]{0:T(512)} %get-tuple-element.20.picked_ref, s32[2]{0:T(128)} %pad_add_fusion.place_ref, s32[512,1]{1,0:T(8,128)} %copy.8.lines_ref, bf16[8,544,384]{2,1,0:T(8,128)(2,1)} %bitcast.20, bf16[8,2,272,384]{3,2,1,0:T(8,128)(2,1)} %bitcast.21, ...), custom_call_target="tpu_custom_call" | custom-call | tf_op jit(solution)/shard_map/pallas_call | solution.py:161
  (4 shorter events, 0.1 us)
Async XLA Ops:
  6.5 9.6 %copy-start.1 = (s32[32]{0:T(128)S(1)}, s32[32]{0:T(128)}, u32[]{:S(2)}) copy-start(s32[32]{0:T(128)} %param.10) | copy-start | bytes 388
  6.5 61.3 %all-gather.3.cloned.1.call-start = ((), (), s32[]{:S(2)}) async-start(), calls=%async_computation | async-start | bytes 3551232 | tf_op jit(solution)/shard_map/all_gather | solution.py:197
  7.6 4.3 %collective-permute-start = (bf16[512,60]{1,0:T(8,128)(2,1)S(1)}, bf16[512,60]{1,0:T(8,128)(2,1)S(1)}, u32[]{:S(2)}, u32[]{:S(2)}) collective-permute-start(bf16[512,60]{1,0:T(8,128)(2,1)S(1)} %slice.34), channel_id=1, source_target_pairs={{0,1},{1,2},{2,3},{3,4},{4,5},{5,6},{6,7},{7,8},{8,9},{9,10},{10,1... | collective-permute-start | bytes 184328 | tf_op jit(solution)/shard_map/ppermute | solution.py:23
  11.9 7.6 %copy-start = (s32[512]{0:T(512)S(1)}, s32[512]{0:T(512)}, u32[]{:S(2)}) copy-start(s32[512]{0:T(512)} %param.9) | copy-start | bytes 6148
  13.5 4.0 %collective-permute-start.1 = (f32[256,384]{1,0:T(8,128)S(1)}, f32[256,384]{1,0:T(8,128)S(1)}, u32[]{:S(2)}, u32[]{:S(2)}) collective-permute-start(f32[256,384]{1,0:T(8,128)S(1)} %dynamic-slice_bitcast_fusion), channel_id=1, source_target_pairs={{0,1},{1,0},{2,3},{3,2},{4,5},{5,4},{6,7},{7,6},{8,9},{9,8},{10,11... | collective-permute-start | bytes 1179656 | tf_op jit(solution)/shard_map/ppermute | solution.py:192
Sparse Core Ops, SparseCore 0:
  18.9 48.8 all-gather.2

commit v21 on v20

--- a/solution.py
+++ b/solution.py
@@ -137,7 +137,7 @@
         )
 
 
-def correlate(table, lines, flags_all, picked, place, blocks, own_flags, delays, block=128, parts=8):
+def correlate(table, lines, flags_all, picked, place, blocks, own_flags, delays, block=128, parts=16):
     source_count = picked.shape[0]
     recv_count = own_flags.shape[0]
     grid_spec = pltpu.PrefetchScalarGridSpec(

time: 119 us -> 119 us (level)
  no operation moved by 1% of the time
where the time goes in v21:
time: 119 us; the launch traced here: 118 us
  waiting for transfers between devices  47.6 us (40%)
  Pallas kernels  42.3 us (36%)
  between operations  13.5 us (11%)
  starting transfers between devices  5.09 us (4%)
  matrix products  3.38 us (3%)
  other arithmetic  3.26 us (3%)
  local copies, waits for them, and re-layouts  3.25 us (3%)
    all_gather x1, waiting for transfers between devices, body(): gathered = lax.all_gather(piece, 'chan', axis=0, tiled=False)  46.2 us
    pallas_call x1, Pallas kernels, correlate(): pl.pallas_call(correlate_kernel, grid_spec=grid_spec, out_shape=jax.Shape...  42.3 us
    ppermute x1, starting transfers between devices, body(): spectrum = spectrum + lax.ppermute(outgoing, 'chan', route)  2.68 us
    ppermute x1, starting transfers between devices, from_behind(): return lax.ppermute(block, axis, route)  2.4 us
  transfers between devices with their start and end apart: 3, of which 2 were waited for; matrix products, arithmetic and copies ran while one was open for 4% of the time, Pallas kernels for 0%

profile of v21, /device:TPU:0, one launch (start us, length us, event | category | flops | bytes accessed | tf_op | source)
XLA Modules:
  0.0 118.4 jit_solution(2487970819276443073)
XLA Ops:
  6.5 0.0 copy-start.1
  6.5 0.0 all-gather.3.cloned.1.call-start
  6.5 1.0 slice.34
  7.6 2.4 %collective-permute-start = (bf16[512,60]{1,0:T(8,128)(2,1)S(1)}, bf16[512,60]{1,0:T(8,128)(2,1)S(1)}, u32[]{:S(2)}, u32[]{:S(2)}) collective-permute-start(bf16[512,60]{1,0:T(8,128)(2,1)S(1)} %slice.34), channel_id=1, source_target_pairs={{0,1},{1,2},{2,3},{3,4},{4,5},{5,6},{6,7},{7,8},{8,9},{9,10},{10,1... | collective-permute-start | bytes 184328 | tf_op jit(solution)/shard_map/ppermute | solution.py:23
  10.0 1.9 %fusion.12 = f32[256,512]{1,0:T(8,128)S(1)} fusion(bf16[1024,256]{1,0:T(8,128)(2,1)} %constant.135, bf16[512,1024]{1,0:T(8,128)(2,1)} %param.8), kind=kOutput, calls=%fused_computation.32 | convolution fusion | flops 268435456 | bytes 2097152 | tf_op jit(solution)/shard_map/dot_general | solution.py:48
  11.9 0.0 copy-start
  11.9 0.0 collective-permute-done
  11.9 1.5 %fusion.1 = f32[512,384]{1,0:T(8,128)S(1)} fusion(f32[256,512]{1,0:T(8,128)S(1)} %fusion.12, bf16[60,256]{1,0:T(8,128)(2,1)} %constant.134, bf16[512,60]{1,0:T(8,128)(2,1)S(1)} %collective-permute-done, bf16[512,384]{1,0:T(8,128)(2,1)} %constant.136, s32[]{:T(128)S(6)} %select_n.44), kind=kOutput, calls=%fused_computation.2 | convolution fusion | flops 116654080 | bytes 1601540 | tf_op jit(solution)/shard_map/dot_general | solution.py:182
  13.5 2.7 %collective-permute-start.1 = (f32[256,384]{1,0:T(8,128)S(1)}, f32[256,384]{1,0:T(8,128)S(1)}, u32[]{:S(2)}, u32[]{:S(2)}) collective-permute-start(f32[256,384]{1,0:T(8,128)S(1)} %dynamic-slice_bitcast_fusion), channel_id=1, source_target_pairs={{0,1},{1,0},{2,3},{3,2},{4,5},{5,4},{6,7},{7,6},{8,9},{9,8},{10,11... | collective-permute-start | bytes 1179656 | tf_op jit(solution)/shard_map/ppermute | solution.py:192
  16.1 0.0 copy-done.1
  16.1 1.3 %collective-permute-done.1 = f32[256,384]{1,0:T(8,128)S(1)} collective-permute-done((f32[256,384]{1,0:T(8,128)S(1)}, f32[256,384]{1,0:T(8,128)S(1)}, u32[]{:S(2)}, u32[]{:S(2)}) %collective-permute-start.1) | collective-permute-done | bytes 393248 | tf_op jit(solution)/shard_map/ppermute | solution.py:192
  17.5 0.2 fusion.11
  17.8 0.2 multiply_convert_fusion.1
  18.0 0.8 fusion.3
  18.7 0.0 all-gather.3.cloned.1.call-update
  18.8 0.7 copy.9.own_ref
  19.5 0.0 copy-done
  19.5 0.6 fusion.7
  20.1 0.9 copy.8.lines_ref
  20.9 0.6 pad_add_fusion.place_ref
  21.6 46.2 %all-gather.3.cloned.1.call-done = bf16[4352,384]{1,0:T(8,128)(2,1)} async-done(((bf16[272,384]{1,0:T(8,128)(2,1)}), bf16[4352,384]{1,0:T(8,128)(2,1)}) %all-gather.3.cloned.1.call-update) | async-done | bytes 3342352 | tf_op jit(solution)/shard_map/all_gather | solution.py:197
  67.8 0.8 fusion.5
  68.6 0.6 reshape.49.flags_ref
  69.2 42.3 %shard_map.64 = bf16[512,32,256]{2,1,0:T(8,128)(2,1)} custom-call(s32[512]{0:T(512)} %reshape.49.flags_ref, s32[512]{0:T(512)} %get-tuple-element.20.picked_ref, s32[2]{0:T(128)} %pad_add_fusion.place_ref, s32[512,1]{1,0:T(8,128)} %copy.8.lines_ref, bf16[8,544,384]{2,1,0:T(8,128)(2,1)} %bitcast.20, bf16[8,2,272,384]{3,2,1,0:T(8,128)(2,1)} %bitcast.21, ...), custom_call_target="tpu_custom_call" | custom-call | tf_op jit(solution)/shard_map/pallas_call | solution.py:161
  (4 shorter events, 0.1 us)
Async XLA Ops:
  6.5 9.6 %copy-start.1 = (s32[32]{0:T(128)S(1)}, s32[32]{0:T(128)}, u32[]{:S(2)}) copy-start(s32[32]{0:T(128)} %param.10) | copy-start | bytes 388
  6.5 61.3 %all-gather.3.cloned.1.call-start = ((), (), s32[]{:S(2)}) async-start(), calls=%async_computation | async-start | bytes 3551232 | tf_op jit(solution)/shard_map/all_gather | solution.py:197
  7.6 4.3 %collective-permute-start = (bf16[512,60]{1,0:T(8,128)(2,1)S(1)}, bf16[512,60]{1,0:T(8,128)(2,1)S(1)}, u32[]{:S(2)}, u32[]{:S(2)}) collective-permute-start(bf16[512,60]{1,0:T(8,128)(2,1)S(1)} %slice.34), channel_id=1, source_target_pairs={{0,1},{1,2},{2,3},{3,4},{4,5},{5,6},{6,7},{7,8},{8,9},{9,10},{10,1... | collective-permute-start | bytes 184328 | tf_op jit(solution)/shard_map/ppermute | solution.py:23
  11.9 7.6 %copy-start = (s32[512]{0:T(512)S(1)}, s32[512]{0:T(512)}, u32[]{:S(2)}) copy-start(s32[512]{0:T(512)} %param.9) | copy-start | bytes 6148
  13.5 4.0 %collective-permute-start.1 = (f32[256,384]{1,0:T(8,128)S(1)}, f32[256,384]{1,0:T(8,128)S(1)}, u32[]{:S(2)}, u32[]{:S(2)}) collective-permute-start(f32[256,384]{1,0:T(8,128)S(1)} %dynamic-slice_bitcast_fusion), channel_id=1, source_target_pairs={{0,1},{1,0},{2,3},{3,2},{4,5},{5,4},{6,7},{7,6},{8,9},{9,8},{10,11... | collective-permute-start | bytes 1179656 | tf_op jit(solution)/shard_map/ppermute | solution.py:192
Sparse Core Ops, SparseCore 0:
  18.9 48.8 all-gather.2

commit v22 on v21

--- a/solution.py
+++ b/solution.py
@@ -137,7 +137,7 @@
         )
 
 
-def correlate(table, lines, flags_all, picked, place, blocks, own_flags, delays, block=128, parts=16):
+def correlate(table, lines, flags_all, picked, place, blocks, own_flags, delays, block=128, parts=32):
     source_count = picked.shape[0]
     recv_count = own_flags.shape[0]
     grid_spec = pltpu.PrefetchScalarGridSpec(

time: 119 us -> 119 us (level)
  no operation moved by 1% of the time
where the time goes in v22:
time: 119 us
  waiting for transfers between devices  47.6 us (40%)
  Pallas kernels  42.4 us (36%)
  between operations  13.5 us (11%)
  starting transfers between devices  5.09 us (4%)
  matrix products  3.38 us (3%)
  other arithmetic  3.26 us (3%)
  local copies, waits for them, and re-layouts  3.25 us (3%)
    all_gather x1, waiting for transfers between devices, body(): gathered = lax.all_gather(piece, 'chan', axis=0, tiled=False)  46.2 us
    pallas_call x1, Pallas kernels, correlate(): pl.pallas_call(correlate_kernel, grid_spec=grid_spec, out_shape=jax.Shape...  42.4 us
    ppermute x1, starting transfers between devices, body(): spectrum = spectrum + lax.ppermute(outgoing, 'chan', route)  2.68 us
    ppermute x1, starting transfers between devices, from_behind(): return lax.ppermute(block, axis, route)  2.4 us
  transfers between devices with their start and end apart: 3, of which 2 were waited for; matrix products, arithmetic and copies ran while one was open for 4% of the time, Pallas kernels for 0%

profile of v22, /device:TPU:0, one launch (start us, length us, event | category | flops | bytes accessed | tf_op | source)
XLA Modules:
  0.0 118.5 jit_solution(1473727990361898185)
XLA Ops:
  6.5 0.0 copy-start.1
  6.5 0.0 all-gather.3.cloned.1.call-start
  6.5 1.0 slice.34
  7.6 2.4 %collective-permute-start = (bf16[512,60]{1,0:T(8,128)(2,1)S(1)}, bf16[512,60]{1,0:T(8,128)(2,1)S(1)}, u32[]{:S(2)}, u32[]{:S(2)}) collective-permute-start(bf16[512,60]{1,0:T(8,128)(2,1)S(1)} %slice.34), channel_id=1, source_target_pairs={{0,1},{1,2},{2,3},{3,4},{4,5},{5,6},{6,7},{7,8},{8,9},{9,10},{10,1... | collective-permute-start | bytes 184328 | tf_op jit(solution)/shard_map/ppermute | solution.py:23
  10.0 1.9 %fusion.12 = f32[256,512]{1,0:T(8,128)S(1)} fusion(bf16[1024,256]{1,0:T(8,128)(2,1)} %constant.135, bf16[512,1024]{1,0:T(8,128)(2,1)} %param.8), kind=kOutput, calls=%fused_computation.32 | convolution fusion | flops 268435456 | bytes 2097152 | tf_op jit(solution)/shard_map/dot_general | solution.py:48
  11.9 0.0 copy-start
  11.9 0.0 collective-permute-done
  11.9 1.5 %fusion.1 = f32[512,384]{1,0:T(8,128)S(1)} fusion(f32[256,512]{1,0:T(8,128)S(1)} %fusion.12, bf16[60,256]{1,0:T(8,128)(2,1)} %constant.134, bf16[512,60]{1,0:T(8,128)(2,1)S(1)} %collective-permute-done, bf16[512,384]{1,0:T(8,128)(2,1)} %constant.136, s32[]{:T(128)S(6)} %select_n.44), kind=kOutput, calls=%fused_computation.2 | convolution fusion | flops 116654080 | bytes 1601540 | tf_op jit(solution)/shard_map/dot_general | solution.py:182
  13.5 2.7 %collective-permute-start.1 = (f32[256,384]{1,0:T(8,128)S(1)}, f32[256,384]{1,0:T(8,128)S(1)}, u32[]{:S(2)}, u32[]{:S(2)}) collective-permute-start(f32[256,384]{1,0:T(8,128)S(1)} %dynamic-slice_bitcast_fusion), channel_id=1, source_target_pairs={{0,1},{1,0},{2,3},{3,2},{4,5},{5,4},{6,7},{7,6},{8,9},{9,8},{10,11... | collective-permute-start | bytes 1179656 | tf_op jit(solution)/shard_map/ppermute | solution.py:192
  16.1 0.0 copy-done.1
  16.1 1.3 %collective-permute-done.1 = f32[256,384]{1,0:T(8,128)S(1)} collective-permute-done((f32[256,384]{1,0:T(8,128)S(1)}, f32[256,384]{1,0:T(8,128)S(1)}, u32[]{:S(2)}, u32[]{:S(2)}) %collective-permute-start.1) | collective-permute-done | bytes 393248 | tf_op jit(solution)/shard_map/ppermute | solution.py:192
  17.5 0.2 fusion.11
  17.8 0.2 multiply_convert_fusion.1
  18.0 0.8 fusion.3
  18.7 0.0 all-gather.3.cloned.1.call-update
  18.8 0.7 copy.9.own_ref
  19.5 0.0 copy-done
  19.5 0.6 fusion.7
  20.1 0.9 copy.8.lines_ref
  20.9 0.6 pad_add_fusion.place_ref
  21.6 46.2 %all-gather.3.cloned.1.call-done = bf16[4352,384]{1,0:T(8,128)(2,1)} async-done(((bf16[272,384]{1,0:T(8,128)(2,1)}), bf16[4352,384]{1,0:T(8,128)(2,1)}) %all-gather.3.cloned.1.call-update) | async-done | bytes 3342352 | tf_op jit(solution)/shard_map/all_gather | solution.py:197
  67.8 0.8 fusion.5
  68.6 0.6 reshape.49.flags_ref
  69.2 42.4 %shard_map.64 = bf16[512,32,256]{2,1,0:T(8,128)(2,1)} custom-call(s32[512]{0:T(512)} %reshape.49.flags_ref, s32[512]{0:T(512)} %get-tuple-element.20.picked_ref, s32[2]{0:T(128)} %pad_add_fusion.place_ref, s32[512,1]{1,0:T(8,128)} %copy.8.lines_ref, bf16[8,544,384]{2,1,0:T(8,128)(2,1)} %bitcast.20, bf16[8,2,272,384]{3,2,1,0:T(8,128)(2,1)} %bitcast.21, ...), custom_call_target="tpu_custom_call" | custom-call | tf_op jit(solution)/shard_map/pallas_call | solution.py:161
  (4 shorter events, 0.1 us)
Async XLA Ops:
  6.5 9.6 %copy-start.1 = (s32[32]{0:T(128)S(1)}, s32[32]{0:T(128)}, u32[]{:S(2)}) copy-start(s32[32]{0:T(128)} %param.10) | copy-start | bytes 388
  6.5 61.3 %all-gather.3.cloned.1.call-start = ((), (), s32[]{:S(2)}) async-start(), calls=%async_computation | async-start | bytes 3551232 | tf_op jit(solution)/shard_map/all_gather | solution.py:197
  7.6 4.3 %collective-permute-start = (bf16[512,60]{1,0:T(8,128)(2,1)S(1)}, bf16[512,60]{1,0:T(8,128)(2,1)S(1)}, u32[]{:S(2)}, u32[]{:S(2)}) collective-permute-start(bf16[512,60]{1,0:T(8,128)(2,1)S(1)} %slice.34), channel_id=1, source_target_pairs={{0,1},{1,2},{2,3},{3,4},{4,5},{5,6},{6,7},{7,8},{8,9},{9,10},{10,1... | collective-permute-start | bytes 184328 | tf_op jit(solution)/shard_map/ppermute | solution.py:23
  11.9 7.6 %copy-start = (s32[512]{0:T(512)S(1)}, s32[512]{0:T(512)}, u32[]{:S(2)}) copy-start(s32[512]{0:T(512)} %param.9) | copy-start | bytes 6148
  13.5 4.0 %collective-permute-start.1 = (f32[256,384]{1,0:T(8,128)S(1)}, f32[256,384]{1,0:T(8,128)S(1)}, u32[]{:S(2)}, u32[]{:S(2)}) collective-permute-start(f32[256,384]{1,0:T(8,128)S(1)} %dynamic-slice_bitcast_fusion), channel_id=1, source_target_pairs={{0,1},{1,0},{2,3},{3,2},{4,5},{5,4},{6,7},{7,6},{8,9},{9,8},{10,11... | collective-permute-start | bytes 1179656 | tf_op jit(solution)/shard_map/ppermute | solution.py:192
Sparse Core Ops, SparseCore 0:
  18.9 48.8 all-gather.2
